TPU v7x, 256 devices: a whole 4x4x8 slice. The times are simulated.
256 devices in a mesh: dp: 16 (over x_lo, z), space: 16 (over x_hi, y, core).
Axes of the slice: x: 4 (x_hi: 2, x_lo: 2; x = x_hi * 2 + x_lo), y: 4, z: 8, core: 2. Of those that a mesh axis runs over, the one named last changes fastest.
Arguments:
- volume: bfloat16 [16, 4, 64, 8, 512], P('dp', None, 'space'), may hold values from -6 to 6
- cotangent: bfloat16 [16, 32, 16, 2, 128], P('dp', None, 'space'), may hold values from -1 to 1
- w_first: bfloat16 [16, 4, 3, 3, 3], replicated, may hold values from -0.625 to 0.625
- b_first: float32 [16], replicated, may hold values from -3 to 3
- w_second: bfloat16 [32, 16, 3, 3, 3], replicated, may hold values from -0.3125 to 0.3125
- b_second: float32 [32], replicated, may hold values from -3 to 3
Outputs:
- output: bfloat16 [16, 32, 16, 2, 128], P('dp', None, 'space')
- grad_w_first: float32 [16, 4, 3, 3, 3], replicated
- grad_b_first: float32 [16], replicated
- grad_w_second: float32 [32, 16, 3, 3, 3], replicated
- grad_b_second: float32 [32], replicated
All inputs are finite; a program needn't handle non-finite values.
Results may differ from a plain program's by a relative error of at most 0.0047.
Values may be sent and summed in bfloat16 or wider, within the bound.
No kernel may reach another device: no remote copies, remote signals or barrier semaphores. Data moves between devices by JAX's collectives and lax.ppermute only.
A program may use at most 128 MiB of HBM per device.

v0:
```python
import jax
import jax.numpy as jnp
from jax import lax
from jax.sharding import PartitionSpec as P


def with_halo(cells, axis, dim):
    count = lax.axis_size(axis)
    ends = count - 1
    head = lax.slice_in_dim(cells, 0, 1, axis=dim)
    tail = lax.slice_in_dim(cells, cells.shape[dim] - 1, cells.shape[dim], axis=dim)
    return jnp.concatenate(
        [
            lax.ppermute(tail, axis, [(i, (i + 1) % count) for i in range(ends)]),
            cells,
            lax.ppermute(head, axis, [((i + 1) % count, i) for i in range(ends)]),
        ],
        axis=dim,
    )


def lane_shift(field, dm):
    if dm == 0:
        return field
    zeros = jnp.zeros(field.shape[:-1] + (1,), field.dtype)
    if dm < 0:
        return jnp.concatenate([zeros, field[..., :-1]], axis=-1)
    return jnp.concatenate([field[..., 1:], zeros], axis=-1)


def phase_patches(field):
    phases, _, depth, height, width = field.shape
    depth -= 2
    field = jnp.pad(field, ((0, 0), (0, 0), (0, 0), (1, 1), (0, 0)))
    sources = {}
    for r in range(phases):
        for e in range(3):
            key = ((r + e - 1) % phases, (r + e - 1) // phases)
            if key not in sources:
                sources[key] = lane_shift(field[key[0]], key[1])
    keys = sorted(sources)
    rows = {}
    for key in keys:
        for b in range(3):
            rows[key + (b,)] = sources[key][:, :, b : b + height, :]
    names = sorted(rows)
    rows = dict(zip(names, lax.optimization_barrier(tuple(rows[n] for n in names))))
    out = []
    for r in range(phases):
        taps = []
        for a in range(3):
            for b in range(3):
                for e in range(3):
                    key = ((r + e - 1) % phases, (r + e - 1) // phases, b)
                    taps.append(rows[key][:, a : a + depth])
        out.append(jnp.stack(taps, axis=0))
    return jnp.stack(out, axis=0)


def conv_taps(kern, patches):
    return jnp.einsum("otc,rtcxym->orxym", kern, patches, preferred_element_type=jnp.float32)


def grad_taps(grads, patches):
    return jnp.einsum("orxym,rtcxym->otc", grads, patches, preferred_element_type=jnp.float32)


def pool(field):
    chan, phases, depth, height, width = field.shape
    blocks = field.reshape(chan, phases // 2, 2, depth // 2, 2, height // 2, 2, width)
    return blocks.sum(axis=(2, 4, 6)) * 0.125


def upsample(field, phases):
    return jnp.repeat(jnp.repeat(jnp.repeat(field, 2, axis=1), 2, axis=2), 2, axis=3)


def silu_slope(value):
    sig = jax.nn.sigmoid(value)
    return sig * (1.0 + value * (1.0 - sig))


def butterfly_sum(parts, axes):
    flat = jnp.concatenate([part.reshape(-1) for part in parts])
    for axis in axes:
        count = lax.axis_size(axis)
        step = 1
        while step < count:
            flat = flat + lax.ppermute(flat, axis, [(i, i ^ step) for i in range(count)])
            step *= 2
    sums, start = [], 0
    for part in parts:
        sums.append(flat[start : start + part.size].reshape(part.shape))
        start += part.size
    return tuple(sums)


def tap_major(kern):
    return jnp.transpose(kern, (0, 2, 3, 4, 1)).reshape(kern.shape[0], 27, kern.shape[1])


def tap_minor(grad, chan):
    return jnp.transpose(grad.reshape(grad.shape[0], 3, 3, 3, chan), (0, 4, 1, 2, 3))


def shards(volume, cotangent, w_first, b_first, w_second, b_second):
    sample = volume[0]
    cot = cotangent[0]
    chan0, _, height, width = sample.shape
    halo = with_halo(sample, "space", 1)
    split = jnp.moveaxis(halo.reshape(chan0, halo.shape[1], height, width // 4, 4), 4, 0)
    patches_first = phase_patches(split)
    pre_first = conv_taps(tap_major(w_first), patches_first) + b_first[:, None, None, None, None]
    pooled = pool(jax.nn.silu(pre_first)).astype(jnp.bfloat16)
    pooled_halo = jnp.moveaxis(with_halo(pooled, "space", 2), 1, 0)
    patches_second = phase_patches(pooled_halo)
    pre_second = conv_taps(tap_major(w_second), patches_second) + b_second[:, None, None, None, None]
    output = pool(jax.nn.silu(pre_second))[:, 0].astype(jnp.bfloat16)
    grad_second = (
        upsample(cot.astype(jnp.float32)[:, None], 2) * 0.125 * silu_slope(pre_second)
    ).astype(jnp.bfloat16)
    grad_w2 = grad_taps(grad_second, patches_second)
    grad_b2 = jnp.sum(grad_second.astype(jnp.float32), axis=(1, 2, 3, 4))
    grad_halo = jnp.moveaxis(with_halo(grad_second, "space", 2), 1, 0)
    flipped = tap_major(jnp.transpose(jnp.flip(w_second, (2, 3, 4)), (1, 0, 2, 3, 4)))
    back = conv_taps(flipped, phase_patches(grad_halo))
    grad_first = (upsample(back, 4) * 0.125 * silu_slope(pre_first)).astype(jnp.bfloat16)
    grad_w1 = grad_taps(grad_first, patches_first)
    grad_b1 = jnp.sum(grad_first.astype(jnp.float32), axis=(1, 2, 3, 4))
    totals = butterfly_sum(
        (tap_minor(grad_w1, chan0), grad_b1, tap_minor(grad_w2, w_second.shape[1]), grad_b2),
        ("space", "dp"),
    )
    return (output[None], totals[0], totals[1], totals[2], totals[3])


def solution(mesh):
    placed = (
        P("dp", None, "space", None, None),
        P("dp", None, "space", None, None),
        P(),
        P(),
        P(),
        P(),
    )
    return jax.shard_map(
        shards,
        mesh=mesh,
        in_specs=placed,
        out_specs=(P("dp", None, "space", None, None), P(), P(), P(), P()),
        check_vma=False,
    )
```

profile of v0, /device:TPU:6, one launch (start us, length us, event | category | flops | bytes accessed | tf_op | source)
XLA Modules:
  0.0 165.0 jit_solution(3044703418263215317)
XLA Ops:
  1.4 5.2 %collective-permute-start.1 = (bf16[4,1,8,512]{3,2,1,0:T(8,128)(2,1)S(1)}, bf16[4,1,8,512]{3,2,1,0:T(8,128)(2,1)S(1)}, u32[]{:S(2)}, u32[]{:S(2)}) collective-permute-start(bf16[4,1,8,512]{3,2,1,0:T(8,128)(2,1)S(1)} %get-tuple-element.254), channel_id=1, source_target_pairs={{1,0},{2,1},{3,2},{4,3},{5,4},{6,5},{7,6},{8,7},{9,8},{10,9},{11,1... | collective-permute-start | bytes 98312 | tf_op jit(solution)/shard_map/ppermute | solution.py:16
  6.6 1.9 %collective-permute-start = (bf16[4,1,8,512]{3,2,1,0:T(8,128)(2,1)S(1)}, bf16[4,1,8,512]{3,2,1,0:T(8,128)(2,1)S(1)}, u32[]{:S(2)}, u32[]{:S(2)}) collective-permute-start(bf16[4,1,8,512]{3,2,1,0:T(8,128)(2,1)S(1)} %get-tuple-element.253), channel_id=1, source_target_pairs={{0,1},{1,2},{2,3},{3,4},{4,5},{5,6},{6,7},{7,8},{8,9},{9,10},{10,1... | collective-permute-start | bytes 98312 | tf_op jit(solution)/shard_map/ppermute | solution.py:14
  8.6 1.8 %copy.4465 = bf16[1,4,4,8,512]{3,4,2,1,0:T(8,128)(2,1)S(1)} copy(bf16[1,4,4,8,512]{4,3,2,1,0:T(8,128)(2,1)} %param.6) | data formatting | bytes 262144 | tf_op args[0]
  11.8 3.7 %collective-permute-done = bf16[4,1,8,512]{3,2,1,0:T(8,128)(2,1)S(1)} collective-permute-done((bf16[4,1,8,512]{3,2,1,0:T(8,128)(2,1)S(1)}, bf16[4,1,8,512]{3,2,1,0:T(8,128)(2,1)S(1)}, u32[]{:S(2)}, u32[]{:S(2)}) %collective-permute-start) | collective-permute-done | bytes 32800 | tf_op jit(solution)/shard_map/ppermute | solution.py:14
  31.9 4.4 %stack.585 = bf16[27,4,4,8,128]{4,0,1,3,2:T(8,128)(2,1)S(1)} concatenate(bf16[1,4,4,8,128]{4,0,1,3,2:T(2,128)(2,1)S(1)} %copy.4539, bf16[1,4,4,8,128]{4,0,1,3,2:T(2,128)(2,1)S(1)} %copy.4575, bf16[1,4,4,8,128]{4,0,1,3,2:T(2,128)(2,1)S(1)} %copy.4611, bf16[1,4,4,8,128]{4,0,1,3,2:T(2,128)(2,1)S(1)} %copy.4542, bf16[1,4,4,8,128]{4,0,1,3,2:T(2,128)(2,1)S(1)} %copy.4578, ...), dimensions={0} | concatenate | bytes 1769472 | tf_op jit(solution)/shard_map/stack | solution.py:56
  36.3 6.0 %stack.574 = bf16[27,4,4,8,128]{4,0,1,3,2:T(8,128)(2,1)S(1)} concatenate(bf16[1,4,4,8,128]{4,0,1,3,2:T(2,128)(2,1)S(1)} %copy.4503, bf16[1,4,4,8,128]{4,0,1,3,2:T(2,128)(2,1)S(1)} %copy.4539, bf16[1,4,4,8,128]{4,0,1,3,2:T(2,128)(2,1)} %copy-done.10, bf16[1,4,4,8,128]{4,0,1,3,2:T(2,128)(2,1)S(1)} %copy.4506, bf16[1,4,4,8,128]{4,0,1,3,2:T(2,128)(2,1)S(1)} %copy.4542, ...), dimensions={0} | concatenate | bytes 1769472 | tf_op jit(solution)/shard_map/stack | solution.py:56
  42.4 8.4 %stack.563 = bf16[27,4,4,8,128]{4,0,1,3,2:T(8,128)(2,1)} concatenate(bf16[1,4,4,8,128]{4,0,1,3,2:T(2,128)(2,1)S(1)} %copy.4502, bf16[1,4,4,8,128]{4,0,1,3,2:T(2,128)(2,1)S(1)} %copy.4503, bf16[1,4,4,8,128]{4,0,1,3,2:T(2,128)(2,1)S(1)} %copy.4539, bf16[1,4,4,8,128]{4,0,1,3,2:T(2,128)(2,1)} %copy.4505, bf16[1,4,4,8,128]{4,0,1,3,2:T(2,128)(2,1)S(1)} %copy.4506, ...), dimensions={0} | concatenate | bytes 1769472 | tf_op jit(solution)/shard_map/stack | solution.py:56
  50.8 8.5 %stack.552 = bf16[27,4,4,8,128]{4,0,1,3,2:T(8,128)(2,1)} concatenate(bf16[1,4,4,8,128]{4,0,1,3,2:T(2,128)(2,1)} %copy.4501, bf16[1,4,4,8,128]{4,0,1,3,2:T(2,128)(2,1)S(1)} %copy.4502, bf16[1,4,4,8,128]{4,0,1,3,2:T(2,128)(2,1)S(1)} %copy.4503, bf16[1,4,4,8,128]{4,0,1,3,2:T(2,128)(2,1)} %copy.4504, bf16[1,4,4,8,128]{4,0,1,3,2:T(2,128)(2,1)} %copy.4505, ...), dimensions={0} | concatenate | bytes 1769472 | tf_op jit(solution)/shard_map/stack | solution.py:56
  59.4 3.5 %fusion.19 = (f32[16,4,4,8,128]{4,0,3,2,1:T(8,128)S(1)}, f32[16,4,4,8,128]{4,0,3,2,1:T(8,128)}) fusion(f32[16]{0:T(128)S(1)} %copy-done.22, bf16[16,27,4,1,1,1]{0,2,1,5,4,3:T(4,128)(2,1)S(1)} %bitcast.429, bf16[1,27,4,4,8,128]{5,1,2,4,3,0:T(8,128)(2,1)S(1)} %bitcast.444, bf16[1,27,4,4,8,128]{5,1,2,4,3,0:T(8,128)(2,1)S(1)} %bitcast.446, ...), kind=kOutput, calls=%fused_computation.21 | convolution fusion | flops 63242240 | bytes 5639616 | tf_op jit(solution)/shard_map/otc,rtcxym->orxym/dot_general | solution.py:61
  63.0 1.9 %collective-permute-start.2 = (bf16[16,2,1,4,128]{4,0,3,2,1:T(8,128)(2,1)S(1)}, bf16[16,2,1,4,128]{4,0,3,2,1:T(8,128)(2,1)S(1)}, u32[]{:S(2)}, u32[]{:S(2)}) collective-permute-start(bf16[16,2,1,4,128]{4,0,3,2,1:T(8,128)(2,1)S(1)} %get-tuple-element.303), channel_id=1, source_target_pairs={{0,1},{1,2},{2,3},{3,4},{4,5},{5,6},{6,7},{7,8},{8,9},{9,10},{10,1... | collective-permute-start | bytes 98312 | tf_op jit(solution)/shard_map/ppermute | solution.py:14
  64.9 7.3 %collective-permute-start.3 = (bf16[16,2,1,4,128]{4,0,3,2,1:T(8,128)(2,1)S(1)}, bf16[16,2,1,4,128]{4,0,3,2,1:T(8,128)(2,1)S(1)}, u32[]{:S(2)}, u32[]{:S(2)}) collective-permute-start(bf16[16,2,1,4,128]{4,0,3,2,1:T(8,128)(2,1)S(1)} %get-tuple-element.304), channel_id=1, source_target_pairs={{1,0},{2,1},{3,2},{4,3},{5,4},{6,5},{7,6},{8,7},{9,8},{10,9},{11,1... | collective-permute-start | bytes 98312 | tf_op jit(solution)/shard_map/ppermute | solution.py:16
  80.2 3.0 %stack.626 = bf16[27,16,2,4,128]{4,0,1,3,2:T(8,128)(2,1)S(1)} concatenate(bf16[1,16,2,4,128]{4,0,1,3,2:T(2,128)(2,1)S(1)} %copy.4638, bf16[1,16,2,4,128]{4,0,1,3,2:T(2,128)(2,1)S(1)} %copy.4639, bf16[1,16,2,4,128]{4,0,1,3,2:T(2,128)(2,1)S(1)} %copy.4666, bf16[1,16,2,4,128]{4,0,1,3,2:T(2,128)(2,1)S(1)} %copy.4641, bf16[1,16,2,4,128]{4,0,1,3,2:T(2,128)(2,1)S(1)} %copy.4642, ...), dimensions={0} | concatenate | bytes 1769472 | tf_op jit(solution)/shard_map/stack | solution.py:56
  83.2 5.9 %stack.615 = bf16[27,16,2,4,128]{4,0,1,3,2:T(8,128)(2,1)S(1)} concatenate(bf16[1,16,2,4,128]{4,0,1,3,2:T(2,128)(2,1)S(1)} %copy.4637, bf16[1,16,2,4,128]{4,0,1,3,2:T(2,128)(2,1)S(1)} %copy.4638, bf16[1,16,2,4,128]{4,0,1,3,2:T(2,128)(2,1)S(1)} %copy.4639, bf16[1,16,2,4,128]{4,0,1,3,2:T(2,128)(2,1)} %copy.4640, bf16[1,16,2,4,128]{4,0,1,3,2:T(2,128)(2,1)S(1)} %copy.4641, ...), dimensions={0} | concatenate | bytes 1769472 | tf_op jit(solution)/shard_map/stack | solution.py:56
  90.0 1.2 convert_reduce_fusion.1
  91.9 1.9 %collective-permute-start.4 = (bf16[32,2,1,4,128]{4,0,3,2,1:T(8,128)(2,1)}, bf16[32,2,1,4,128]{4,0,3,2,1:T(8,128)(2,1)}, u32[]{:S(2)}, u32[]{:S(2)}) collective-permute-start(bf16[32,2,1,4,128]{4,0,3,2,1:T(8,128)(2,1)} %get-tuple-element.249), channel_id=1, source_target_pairs={{0,1},{1,2},{2,3},{3,4},{4,5},{5,6},{6,7},{7,8},{8,9},{9,10},{10,1... | collective-permute-start | bytes 196616 | tf_op jit(solution)/shard_map/ppermute | solution.py:14
  93.8 7.3 %collective-permute-start.5 = (bf16[32,2,1,4,128]{4,0,3,2,1:T(8,128)(2,1)}, bf16[32,2,1,4,128]{4,0,3,2,1:T(8,128)(2,1)}, u32[]{:S(2)}, u32[]{:S(2)}) collective-permute-start(bf16[32,2,1,4,128]{4,0,3,2,1:T(8,128)(2,1)} %get-tuple-element.250), channel_id=1, source_target_pairs={{1,0},{2,1},{3,2},{4,3},{5,4},{6,5},{7,6},{8,7},{9,8},{10,9},{11,1... | collective-permute-start | bytes 196616 | tf_op jit(solution)/shard_map/ppermute | solution.py:16
  101.7 3.8 %copy.4699 = f32[32,16,3,3,3]{4,3,2,1,0:T(4,128)S(1)} copy(f32[32,16,3,3,3]{0,1,4,3,2:T(8,128)S(1)} %bitcast.453) | data formatting | bytes 110592 | tf_op jit(solution)/shard_map/transpose | solution.py:103
  105.5 2.0 %reshape.103 = f32[13824]{0:T(1024)S(1)} reshape(f32[32,16,3,3,3]{4,3,2,1,0:T(4,128)S(1)} %copy.4699) | data formatting | bytes 110592 | tf_op jit(solution)/shard_map/reshape | solution.py:84
  113.6 1.6 convolution_bitcast_fusion.2
  116.1 1.2 collective-permute-done.6
  117.5 4.3 %collective-permute-done.7 = f32[15600]{0:T(1024)S(1)} collective-permute-done((f32[15600]{0:T(1024)S(1)}, f32[15600]{0:T(1024)S(1)}, u32[]{:S(2)}, u32[]{:S(2)}) %collective-permute-start.7) | collective-permute-done | bytes 62432 | tf_op jit(solution)/shard_map/ppermute | solution.py:89
  121.8 5.8 %collective-permute-done.8 = f32[15600]{0:T(1024)S(1)} collective-permute-done((f32[15600]{0:T(1024)S(1)}, f32[15600]{0:T(1024)S(1)}, u32[]{:S(2)}, u32[]{:S(2)}) %collective-permute-start.8) | collective-permute-done | bytes 62432 | tf_op jit(solution)/shard_map/ppermute | solution.py:89
  127.7 5.8 %collective-permute-done.9 = f32[15600]{0:T(1024)S(1)} collective-permute-done((f32[15600]{0:T(1024)S(1)}, f32[15600]{0:T(1024)S(1)}, u32[]{:S(2)}, u32[]{:S(2)}) %collective-permute-start.9) | collective-permute-done | bytes 62432 | tf_op jit(solution)/shard_map/ppermute | solution.py:89
  133.5 2.0 %collective-permute-start.10 = (f32[15600]{0:T(1024)S(1)}, f32[15600]{0:T(1024)S(1)}, u32[]{:S(2)}, u32[]{:S(2)}) collective-permute-start(f32[15600]{0:T(1024)S(1)} %add.93), channel_id=1, source_target_pairs={{0,16},{16,0},{32,48},{48,32},{64,80},{80,64},{96,112},{112,96},{1... | collective-permute-start | bytes 187208 | tf_op jit(solution)/shard_map/ppermute | solution.py:89
  135.5 2.4 %collective-permute-done.10 = f32[15600]{0:T(1024)S(1)} collective-permute-done((f32[15600]{0:T(1024)S(1)}, f32[15600]{0:T(1024)S(1)}, u32[]{:S(2)}, u32[]{:S(2)}) %collective-permute-start.10) | collective-permute-done | bytes 62432 | tf_op jit(solution)/shard_map/ppermute | solution.py:89
  137.8 3.4 %collective-permute-start.11 = (f32[15600]{0:T(1024)S(1)}, f32[15600]{0:T(1024)S(1)}, u32[]{:S(2)}, u32[]{:S(2)}) collective-permute-start(f32[15600]{0:T(1024)S(1)} %add.94), channel_id=1, source_target_pairs={{0,32},{16,48},{32,0},{48,16},{64,96},{80,112},{96,64},{112,80},{1... | collective-permute-start | bytes 187208 | tf_op jit(solution)/shard_map/ppermute | solution.py:89
  141.2 2.2 %collective-permute-done.11 = f32[15600]{0:T(1024)S(1)} collective-permute-done((f32[15600]{0:T(1024)S(1)}, f32[15600]{0:T(1024)S(1)}, u32[]{:S(2)}, u32[]{:S(2)}) %collective-permute-start.11) | collective-permute-done | bytes 62432 | tf_op jit(solution)/shard_map/ppermute | solution.py:89
  143.5 8.3 %collective-permute-start.12 = (f32[15600]{0:T(1024)S(1)}, f32[15600]{0:T(1024)S(1)}, u32[]{:S(2)}, u32[]{:S(2)}) collective-permute-start(f32[15600]{0:T(1024)S(1)} %add.95), channel_id=1, source_target_pairs={{0,64},{16,80},{32,96},{48,112},{64,0},{80,16},{96,32},{112,48},{1... | collective-permute-start | bytes 187208 | tf_op jit(solution)/shard_map/ppermute | solution.py:89
  151.8 2.2 %collective-permute-done.12 = f32[15600]{0:T(1024)S(1)} collective-permute-done((f32[15600]{0:T(1024)S(1)}, f32[15600]{0:T(1024)S(1)}, u32[]{:S(2)}, u32[]{:S(2)}) %collective-permute-start.12) | collective-permute-done | bytes 62432 | tf_op jit(solution)/shard_map/ppermute | solution.py:89
  154.8 3.6 %collective-permute-done.13 = f32[15600]{0:T(1024)S(1)} collective-permute-done((f32[15600]{0:T(1024)S(1)}, f32[15600]{0:T(1024)S(1)}, u32[]{:S(2)}, u32[]{:S(2)}) %collective-permute-start.13) | collective-permute-done | bytes 62432 | tf_op jit(solution)/shard_map/ppermute | solution.py:89
  160.9 1.6 reshape.105
  162.4 2.5 %copy.4702 = f32[32,16,3,3,3]{0,1,4,3,2:T(8,128)} copy(f32[32,16,3,3,3]{4,3,2,1,0:T(4,128)S(1)} %reshape.105) | data formatting | bytes 110592
  (329 shorter events, 37.9 us)
Async XLA Ops:
  0.6 58.7 %copy-start = (bf16[16,4,3,3,3]{0,1,4,3,2:T(4,128)(2,1)S(1)}, bf16[16,4,3,3,3]{0,1,4,3,2:T(4,128)(2,1)}, u32[]{:S(2)}) copy-start(bf16[16,4,3,3,3]{0,1,4,3,2:T(4,128)(2,1)} %param.8) | copy-start | bytes 10372
  1.4 9.9 %collective-permute-start.1 = (bf16[4,1,8,512]{3,2,1,0:T(8,128)(2,1)S(1)}, bf16[4,1,8,512]{3,2,1,0:T(8,128)(2,1)S(1)}, u32[]{:S(2)}, u32[]{:S(2)}) collective-permute-start(bf16[4,1,8,512]{3,2,1,0:T(8,128)(2,1)S(1)} %get-tuple-element.254), channel_id=1, source_target_pairs={{1,0},{2,1},{3,2},{4,3},{5,4},{6,5},{7,6},{8,7},{9,8},{10,9},{11,1... | collective-permute-start | bytes 98312 | tf_op jit(solution)/shard_map/ppermute | solution.py:16
  6.6 8.8 %collective-permute-start = (bf16[4,1,8,512]{3,2,1,0:T(8,128)(2,1)S(1)}, bf16[4,1,8,512]{3,2,1,0:T(8,128)(2,1)S(1)}, u32[]{:S(2)}, u32[]{:S(2)}) collective-permute-start(bf16[4,1,8,512]{3,2,1,0:T(8,128)(2,1)S(1)} %get-tuple-element.253), channel_id=1, source_target_pairs={{0,1},{1,2},{2,3},{3,4},{4,5},{5,6},{6,7},{7,8},{8,9},{9,10},{10,1... | collective-permute-start | bytes 98312 | tf_op jit(solution)/shard_map/ppermute | solution.py:14
  29.2 2.7 %copy-start.8 = (bf16[1,4,4,8,128]{4,0,1,3,2:T(2,128)(2,1)}, bf16[1,4,4,8,128]{4,0,1,3,2:T(2,128)(2,1)S(1)}, u32[]{:S(2)}) copy-start(bf16[1,4,4,8,128]{4,0,1,3,2:T(2,128)(2,1)S(1)} %copy.4593) | copy-start | bytes 98308
  29.3 2.6 %copy-start.9 = (bf16[1,4,4,8,128]{4,0,1,3,2:T(2,128)(2,1)}, bf16[1,4,4,8,128]{4,0,1,3,2:T(2,128)(2,1)S(1)}, u32[]{:S(2)}) copy-start(bf16[1,4,4,8,128]{4,0,1,3,2:T(2,128)(2,1)S(1)} %copy.4584) | copy-start | bytes 98308
  29.4 2.5 %copy-start.10 = (bf16[1,4,4,8,128]{4,0,1,3,2:T(2,128)(2,1)}, bf16[1,4,4,8,128]{4,0,1,3,2:T(2,128)(2,1)S(1)}, u32[]{:S(2)}) copy-start(bf16[1,4,4,8,128]{4,0,1,3,2:T(2,128)(2,1)S(1)} %copy.4575) | copy-start | bytes 98308
  29.5 2.4 %copy-start.11 = (bf16[1,4,4,8,128]{4,0,1,3,2:T(2,128)(2,1)}, bf16[1,4,4,8,128]{4,0,1,3,2:T(2,128)(2,1)S(1)}, u32[]{:S(2)}) copy-start(bf16[1,4,4,8,128]{4,0,1,3,2:T(2,128)(2,1)S(1)} %copy.4596) | copy-start | bytes 98308
  29.6 2.3 %copy-start.12 = (bf16[1,4,4,8,128]{4,0,1,3,2:T(2,128)(2,1)}, bf16[1,4,4,8,128]{4,0,1,3,2:T(2,128)(2,1)S(1)}, u32[]{:S(2)}) copy-start(bf16[1,4,4,8,128]{4,0,1,3,2:T(2,128)(2,1)S(1)} %copy.4587) | copy-start | bytes 98308
  29.7 2.2 %copy-start.13 = (bf16[1,4,4,8,128]{4,0,1,3,2:T(2,128)(2,1)}, bf16[1,4,4,8,128]{4,0,1,3,2:T(2,128)(2,1)S(1)}, u32[]{:S(2)}) copy-start(bf16[1,4,4,8,128]{4,0,1,3,2:T(2,128)(2,1)S(1)} %copy.4578) | copy-start | bytes 98308
  29.8 2.1 %copy-start.14 = (bf16[1,4,4,8,128]{4,0,1,3,2:T(2,128)(2,1)}, bf16[1,4,4,8,128]{4,0,1,3,2:T(2,128)(2,1)S(1)}, u32[]{:S(2)}) copy-start(bf16[1,4,4,8,128]{4,0,1,3,2:T(2,128)(2,1)S(1)} %copy.4599) | copy-start | bytes 98308
  29.9 2.0 %copy-start.15 = (bf16[1,4,4,8,128]{4,0,1,3,2:T(2,128)(2,1)}, bf16[1,4,4,8,128]{4,0,1,3,2:T(2,128)(2,1)S(1)}, u32[]{:S(2)}) copy-start(bf16[1,4,4,8,128]{4,0,1,3,2:T(2,128)(2,1)S(1)} %copy.4590) | copy-start | bytes 98308
  30.0 2.0 %copy-start.16 = (bf16[1,4,4,8,128]{4,0,1,3,2:T(2,128)(2,1)}, bf16[1,4,4,8,128]{4,0,1,3,2:T(2,128)(2,1)S(1)}, u32[]{:S(2)}) copy-start(bf16[1,4,4,8,128]{4,0,1,3,2:T(2,128)(2,1)S(1)} %copy.4581) | copy-start | bytes 98308
  36.3 23.0 %copy-start.2 = (bf16[27,4,4,8,128]{4,0,1,3,2:T(8,128)(2,1)}, bf16[27,4,4,8,128]{4,0,1,3,2:T(8,128)(2,1)S(1)}, u32[]{:S(2)}) copy-start(bf16[27,4,4,8,128]{4,0,1,3,2:T(8,128)(2,1)S(1)} %stack.585) | copy-start | bytes 2654212
  42.4 17.0 %copy-start.4 = (bf16[27,4,4,8,128]{4,0,1,3,2:T(8,128)(2,1)}, bf16[27,4,4,8,128]{4,0,1,3,2:T(8,128)(2,1)S(1)}, u32[]{:S(2)}) copy-start(bf16[27,4,4,8,128]{4,0,1,3,2:T(8,128)(2,1)S(1)} %stack.574) | copy-start | bytes 2654212
  50.8 8.5 %copy-start.22 = (f32[16]{0:T(128)S(1)}, f32[16]{0:T(128)}, u32[]{:S(2)}) copy-start(f32[16]{0:T(128)} %param.9) | copy-start | bytes 196
  59.3 12.8 %copy-start.21 = (bf16[1,32,1,2,128]{4,3,2,1,0:T(2,128)(2,1)S(1)}, bf16[1,32,1,2,128]{4,3,2,1,0:T(2,128)(2,1)}, u32[]{:S(2)}) copy-start(bf16[1,32,1,2,128]{4,3,2,1,0:T(2,128)(2,1)} %param.7) | copy-start | bytes 49156
  59.3 12.9 %copy-start.17 = (bf16[32,16,3,3,3]{0,1,4,3,2:T(8,128)(2,1)S(1)}, bf16[32,16,3,3,3]{0,1,4,3,2:T(8,128)(2,1)}, u32[]{:S(2)}) copy-start(bf16[32,16,3,3,3]{0,1,4,3,2:T(8,128)(2,1)} %param.10) | copy-start | bytes 82948
  63.0 9.9 %collective-permute-start.2 = (bf16[16,2,1,4,128]{4,0,3,2,1:T(8,128)(2,1)S(1)}, bf16[16,2,1,4,128]{4,0,3,2,1:T(8,128)(2,1)S(1)}, u32[]{:S(2)}, u32[]{:S(2)}) collective-permute-start(bf16[16,2,1,4,128]{4,0,3,2,1:T(8,128)(2,1)S(1)} %get-tuple-element.303), channel_id=1, source_target_pairs={{0,1},{1,2},{2,3},{3,4},{4,5},{5,6},{6,7},{7,8},{8,9},{9,10},{10,1... | collective-permute-start | bytes 98312 | tf_op jit(solution)/shard_map/ppermute | solution.py:14
  64.9 8.8 %collective-permute-start.3 = (bf16[16,2,1,4,128]{4,0,3,2,1:T(8,128)(2,1)S(1)}, bf16[16,2,1,4,128]{4,0,3,2,1:T(8,128)(2,1)S(1)}, u32[]{:S(2)}, u32[]{:S(2)}) collective-permute-start(bf16[16,2,1,4,128]{4,0,3,2,1:T(8,128)(2,1)S(1)} %get-tuple-element.304), channel_id=1, source_target_pairs={{1,0},{2,1},{3,2},{4,3},{5,4},{6,5},{7,6},{8,7},{9,8},{10,9},{11,1... | collective-permute-start | bytes 98312 | tf_op jit(solution)/shard_map/ppermute | solution.py:16
  91.9 15.6 %collective-permute-start.4 = (bf16[32,2,1,4,128]{4,0,3,2,1:T(8,128)(2,1)}, bf16[32,2,1,4,128]{4,0,3,2,1:T(8,128)(2,1)}, u32[]{:S(2)}, u32[]{:S(2)}) collective-permute-start(bf16[32,2,1,4,128]{4,0,3,2,1:T(8,128)(2,1)} %get-tuple-element.249), channel_id=1, source_target_pairs={{0,1},{1,2},{2,3},{3,4},{4,5},{5,6},{6,7},{7,8},{8,9},{9,10},{10,1... | collective-permute-start | bytes 196616 | tf_op jit(solution)/shard_map/ppermute | solution.py:14
  93.8 13.7 %collective-permute-start.5 = (bf16[32,2,1,4,128]{4,0,3,2,1:T(8,128)(2,1)}, bf16[32,2,1,4,128]{4,0,3,2,1:T(8,128)(2,1)}, u32[]{:S(2)}, u32[]{:S(2)}) collective-permute-start(bf16[32,2,1,4,128]{4,0,3,2,1:T(8,128)(2,1)} %get-tuple-element.250), channel_id=1, source_target_pairs={{1,0},{2,1},{3,2},{4,3},{5,4},{6,5},{7,6},{8,7},{9,8},{10,9},{11,1... | collective-permute-start | bytes 196616 | tf_op jit(solution)/shard_map/ppermute | solution.py:16
  111.2 2.1 %copy-start.6 = (bf16[27,4,4,8,128]{4,0,1,3,2:T(8,128)(2,1)S(1)}, bf16[27,4,4,8,128]{4,0,1,3,2:T(8,128)(2,1)}, u32[]{:S(2)}) copy-start(bf16[27,4,4,8,128]{4,0,1,3,2:T(8,128)(2,1)} %stack.563) | copy-start | bytes 2654212
  111.2 2.4 %copy-start.7 = (bf16[27,4,4,8,128]{4,0,1,3,2:T(8,128)(2,1)S(1)}, bf16[27,4,4,8,128]{4,0,1,3,2:T(8,128)(2,1)}, u32[]{:S(2)}) copy-start(bf16[27,4,4,8,128]{4,0,1,3,2:T(8,128)(2,1)} %stack.552) | copy-start | bytes 2654212
  115.2 36.6 %copy-start.20 = (f32[32,4,128]{2,0,1:T(8,128)S(1)}, f32[32,4,128]{2,0,1:T(8,128)}, u32[]{:S(2)}) copy-start(f32[32,4,128]{2,0,1:T(8,128)} %get-tuple-element.220) | copy-start | bytes 196612
  116.0 1.3 collective-permute-start.6
  117.3 4.4 %collective-permute-start.7 = (f32[15600]{0:T(1024)S(1)}, f32[15600]{0:T(1024)S(1)}, u32[]{:S(2)}, u32[]{:S(2)}) collective-permute-start(f32[15600]{0:T(1024)S(1)} %add.90), channel_id=1, source_target_pairs={{0,2},{1,3},{2,0},{3,1},{4,6},{5,7},{6,4},{7,5},{8,10},{9,11},{10,... | collective-permute-start | bytes 187208 | tf_op jit(solution)/shard_map/ppermute | solution.py:89
  121.7 5.9 %collective-permute-start.8 = (f32[15600]{0:T(1024)S(1)}, f32[15600]{0:T(1024)S(1)}, u32[]{:S(2)}, u32[]{:S(2)}) collective-permute-start(f32[15600]{0:T(1024)S(1)} %add.91), channel_id=1, source_target_pairs={{0,4},{1,5},{2,6},{3,7},{4,0},{5,1},{6,2},{7,3},{8,12},{9,13},{10,... | collective-permute-start | bytes 187208 | tf_op jit(solution)/shard_map/ppermute | solution.py:89
  127.6 5.9 %collective-permute-start.9 = (f32[15600]{0:T(1024)S(1)}, f32[15600]{0:T(1024)S(1)}, u32[]{:S(2)}, u32[]{:S(2)}) collective-permute-start(f32[15600]{0:T(1024)S(1)} %add.92), channel_id=1, source_target_pairs={{0,8},{1,9},{2,10},{3,11},{4,12},{5,13},{6,14},{7,15},{8,0},{9,1},... | collective-permute-start | bytes 187208 | tf_op jit(solution)/shard_map/ppermute | solution.py:89
  133.5 4.4 %collective-permute-start.10 = (f32[15600]{0:T(1024)S(1)}, f32[15600]{0:T(1024)S(1)}, u32[]{:S(2)}, u32[]{:S(2)}) collective-permute-start(f32[15600]{0:T(1024)S(1)} %add.93), channel_id=1, source_target_pairs={{0,16},{16,0},{32,48},{48,32},{64,80},{80,64},{96,112},{112,96},{1... | collective-permute-start | bytes 187208 | tf_op jit(solution)/shard_map/ppermute | solution.py:89
  137.8 5.6 %collective-permute-start.11 = (f32[15600]{0:T(1024)S(1)}, f32[15600]{0:T(1024)S(1)}, u32[]{:S(2)}, u32[]{:S(2)}) collective-permute-start(f32[15600]{0:T(1024)S(1)} %add.94), channel_id=1, source_target_pairs={{0,32},{16,48},{32,0},{48,16},{64,96},{80,112},{96,64},{112,80},{1... | collective-permute-start | bytes 187208 | tf_op jit(solution)/shard_map/ppermute | solution.py:89
  143.5 10.6 %collective-permute-start.12 = (f32[15600]{0:T(1024)S(1)}, f32[15600]{0:T(1024)S(1)}, u32[]{:S(2)}, u32[]{:S(2)}) collective-permute-start(f32[15600]{0:T(1024)S(1)} %add.95), channel_id=1, source_target_pairs={{0,64},{16,80},{32,96},{48,112},{64,0},{80,16},{96,32},{112,48},{1... | collective-permute-start | bytes 187208 | tf_op jit(solution)/shard_map/ppermute | solution.py:89
  154.0 4.4 %collective-permute-start.13 = (f32[15600]{0:T(1024)S(1)}, f32[15600]{0:T(1024)S(1)}, u32[]{:S(2)}, u32[]{:S(2)}) collective-permute-start(f32[15600]{0:T(1024)S(1)} %add.96), channel_id=1, source_target_pairs={{0,128},{16,144},{32,160},{48,176},{64,192},{80,208},{96,224},{112... | collective-permute-start | bytes 187208 | tf_op jit(solution)/shard_map/ppermute | solution.py:89
  (6 other events, 7.4 us)
where the time goes:
time: 167 us; the launch traced here: 165 us
  local copies, waits for them, and re-layouts  81.2 us (49%)
  starting transfers between devices  39.6 us (24%)
  waiting for transfers between devices  32 us (19%)
  matrix products  7.56 us (5%)
  between operations  2.65 us (2%)
  other arithmetic  1.97 us (1%)
    another operation x116, local copies, waits for them, and re-layouts, phase_patches(): out.append(jnp.stack(taps, axis=0))  55.7 us
    ppermute x8, waiting for transfers between devices, butterfly_sum(): lax.ppermute(flat, axis, [(i, i ^ step) for i in range(count)])  27.5 us
    ppermute x3, starting transfers between devices, with_halo(): lax.ppermute(head, axis, [((i + 1) % count, i) for i in range(ends)])  19.7 us
    ppermute x8, starting transfers between devices, butterfly_sum(): lax.ppermute(flat, axis, [(i, i ^ step) for i in range(count)])  14.1 us
    unnamed x98, local copies, waits for them, and re-layouts  9.46 us
    ppermute x3, starting transfers between devices, with_halo(): lax.ppermute(tail, axis, [(i, (i + 1) % count) for i in range(ends)])  5.75 us
    dot_general x3, matrix products, conv_taps(): jnp.einsum('otc,rtcxym->orxym', kern, patches, preferred_element_type=jnp...  5.34 us
    transpose x2, local copies, waits for them, and re-layouts, tap_minor(): jnp.transpose(grad.reshape(grad.shape[0], 3, 3, 3, chan), (0, 4, 1, 2, 3))  4.14 us
  transfers between devices with their start and end apart: 14, of which 10 were waited for; matrix products, arithmetic and copies ran while one was open for 7% of the time, Pallas kernels for 0%

commit v1 on v0

--- a/solution.py
+++ b/solution.py
@@ -29,40 +29,30 @@
 
 
 def phase_patches(field):
-    phases, _, depth, height, width = field.shape
+    phases, depth, height, _, width = field.shape
     depth -= 2
-    field = jnp.pad(field, ((0, 0), (0, 0), (0, 0), (1, 1), (0, 0)))
+    field = jnp.pad(field, ((0, 0), (0, 0), (1, 1), (0, 0), (0, 0)))
     sources = {}
-    for r in range(phases):
-        for e in range(3):
-            key = ((r + e - 1) % phases, (r + e - 1) // phases)
-            if key not in sources:
-                sources[key] = lane_shift(field[key[0]], key[1])
-    keys = sorted(sources)
-    rows = {}
-    for key in keys:
-        for b in range(3):
-            rows[key + (b,)] = sources[key][:, :, b : b + height, :]
-    names = sorted(rows)
-    rows = dict(zip(names, lax.optimization_barrier(tuple(rows[n] for n in names))))
     out = []
     for r in range(phases):
         taps = []
         for a in range(3):
             for b in range(3):
                 for e in range(3):
-                    key = ((r + e - 1) % phases, (r + e - 1) // phases, b)
-                    taps.append(rows[key][:, a : a + depth])
-        out.append(jnp.stack(taps, axis=0))
+                    key = ((r + e - 1) % phases, (r + e - 1) // phases)
+                    if key not in sources:
+                        sources[key] = lane_shift(field[key[0]], key[1])
+                    taps.append(sources[key][a : a + depth, b : b + height])
+        out.append(jnp.concatenate(taps, axis=2))
     return jnp.stack(out, axis=0)
 
 
 def conv_taps(kern, patches):
-    return jnp.einsum("otc,rtcxym->orxym", kern, patches, preferred_element_type=jnp.float32)
+    return jnp.einsum("ok,rxykm->orxym", kern.reshape(kern.shape[0], -1), patches, preferred_element_type=jnp.float32)
 
 
 def grad_taps(grads, patches):
-    return jnp.einsum("orxym,rtcxym->otc", grads, patches, preferred_element_type=jnp.float32)
+    return jnp.einsum("orxym,rxykm->ok", grads, patches, preferred_element_type=jnp.float32)
 
 
 def pool(field):
@@ -108,11 +98,11 @@
     cot = cotangent[0]
     chan0, _, height, width = sample.shape
     halo = with_halo(sample, "space", 1)
-    split = jnp.moveaxis(halo.reshape(chan0, halo.shape[1], height, width // 4, 4), 4, 0)
+    split = jnp.transpose(halo.reshape(chan0, halo.shape[1], height, width // 4, 4), (4, 1, 2, 0, 3))
     patches_first = phase_patches(split)
     pre_first = conv_taps(tap_major(w_first), patches_first) + b_first[:, None, None, None, None]
     pooled = pool(jax.nn.silu(pre_first)).astype(jnp.bfloat16)
-    pooled_halo = jnp.moveaxis(with_halo(pooled, "space", 2), 1, 0)
+    pooled_halo = jnp.transpose(with_halo(pooled, "space", 2), (1, 2, 3, 0, 4))
     patches_second = phase_patches(pooled_halo)
     pre_second = conv_taps(tap_major(w_second), patches_second) + b_second[:, None, None, None, None]
     output = pool(jax.nn.silu(pre_second))[:, 0].astype(jnp.bfloat16)
@@ -121,7 +111,7 @@
     ).astype(jnp.bfloat16)
     grad_w2 = grad_taps(grad_second, patches_second)
     grad_b2 = jnp.sum(grad_second.astype(jnp.float32), axis=(1, 2, 3, 4))
-    grad_halo = jnp.moveaxis(with_halo(grad_second, "space", 2), 1, 0)
+    grad_halo = jnp.transpose(with_halo(grad_second, "space", 2), (1, 2, 3, 0, 4))
     flipped = tap_major(jnp.transpose(jnp.flip(w_second, (2, 3, 4)), (1, 0, 2, 3, 4)))
     back = conv_taps(flipped, phase_patches(grad_halo))
     grad_first = (upsample(back, 4) * 0.125 * silu_slope(pre_first)).astype(jnp.bfloat16)

time: 167 us -> 128 us (0.77)
  the two profiles are of different devices: /device:TPU:6 before, /device:TPU:24 now
where the time goes in v1:
time: 128 us; the launch traced here: 126 us
  local copies, waits for them, and re-layouts  46 us (36%)
  starting transfers between devices  40.4 us (32%)
  waiting for transfers between devices  29 us (23%)
  matrix products  6.66 us (5%)
  other arithmetic  2.54 us (2%)
  between operations  1.64 us (1%)
    ppermute x8, waiting for transfers between devices, butterfly_sum(): lax.ppermute(flat, axis, [(i, i ^ step) for i in range(count)])  25.7 us
    concatenate x8, local copies, waits for them, and re-layouts, phase_patches(): out.append(jnp.concatenate(taps, axis=2))  20.9 us
    ppermute x8, starting transfers between devices, butterfly_sum(): lax.ppermute(flat, axis, [(i, i ^ step) for i in range(count)])  17.2 us
    ppermute x3, starting transfers between devices, with_halo(): lax.ppermute(tail, axis, [(i, (i + 1) % count) for i in range(ends)])  15.5 us
    unnamed x128, local copies, waits for them, and re-layouts  10.5 us
    ppermute x3, starting transfers between devices, with_halo(): lax.ppermute(head, axis, [((i + 1) % count, i) for i in range(ends)])  7.66 us
    dot_general x3, matrix products, conv_taps(): jnp.einsum('ok,rxykm->orxym', kern.reshape(kern.shape[0], -1), patches, p...  4.99 us
    transpose x2, local copies, waits for them, and re-layouts, tap_minor(): jnp.transpose(grad.reshape(grad.shape[0], 3, 3, 3, chan), (0, 4, 1, 2, 3))  3.91 us
  transfers between devices with their start and end apart: 14, of which 9 were waited for; matrix products, arithmetic and copies ran while one was open for 9% of the time, Pallas kernels for 0%

profile of v1, /device:TPU:24, one launch (start us, length us, event | category | flops | bytes accessed | tf_op | source)
XLA Modules:
  0.0 126.3 jit_solution(10860024470358729688)
XLA Ops:
  1.4 1.9 %collective-permute-start = (bf16[4,1,8,512]{3,2,1,0:T(8,128)(2,1)S(1)}, bf16[4,1,8,512]{3,2,1,0:T(8,128)(2,1)S(1)}, u32[]{:S(2)}, u32[]{:S(2)}) collective-permute-start(bf16[4,1,8,512]{3,2,1,0:T(8,128)(2,1)S(1)} %get-tuple-element.39), channel_id=1, source_target_pairs={{0,1},{1,2},{2,3},{3,4},{4,5},{5,6},{6,7},{7,8},{8,9},{9,10},{10,1... | collective-permute-start | bytes 98312 | tf_op jit(solution)/shard_map/ppermute | solution.py:14
  3.3 3.6 %collective-permute-start.1 = (bf16[4,1,8,512]{3,2,1,0:T(8,128)(2,1)S(1)}, bf16[4,1,8,512]{3,2,1,0:T(8,128)(2,1)S(1)}, u32[]{:S(2)}, u32[]{:S(2)}) collective-permute-start(bf16[4,1,8,512]{3,2,1,0:T(8,128)(2,1)S(1)} %get-tuple-element.40), channel_id=1, source_target_pairs={{1,0},{2,1},{3,2},{4,3},{5,4},{6,5},{7,6},{8,7},{9,8},{10,9},{11,1... | collective-permute-start | bytes 98312 | tf_op jit(solution)/shard_map/ppermute | solution.py:16
  7.7 1.8 %copy.47 = bf16[1,4,4,8,512]{3,4,2,1,0:T(8,128)(2,1)S(1)} copy(bf16[1,4,4,8,512]{4,3,2,1,0:T(8,128)(2,1)} %param.6) | data formatting | bytes 262144 | tf_op args[0]
  9.6 1.2 copy.50
  14.7 9.6 %concatenate.68 = bf16[4,8,108,128]{3,2,1,0:T(8,128)(2,1)} concatenate(bf16[4,8,4,128]{3,2,1,0:T(4,128)(2,1)S(1)} %get-tuple-element.103, bf16[4,8,4,128]{3,2,1,0:T(4,128)(2,1)S(1)} %get-tuple-element.112, bf16[4,8,4,128]{3,2,1,0:T(4,128)(2,1)S(1)} %get-tuple-element.91, bf16[4,8,4,128]{3,2,1,0:T(4,128)(2,1)S(1)} %get-tuple-element.104, ...), dimensions={2} | concatenate | bytes 1769472 | tf_op jit(solution)/shard_map/concatenate | solution.py:46
  24.3 9.6 %concatenate.70 = bf16[4,8,108,128]{3,2,1,0:T(8,128)(2,1)} concatenate(bf16[4,8,4,128]{3,2,1,0:T(4,128)(2,1)S(1)} %get-tuple-element.112, bf16[4,8,4,128]{3,2,1,0:T(4,128)(2,1)S(1)} %get-tuple-element.91, bf16[4,8,4,128]{3,2,1,0:T(4,128)(2,1)S(1)} %get-tuple-element.82, bf16[4,8,4,128]{3,2,1,0:T(4,128)(2,1)S(1)} %get-tuple-element.113, ...), dimensions={2} | concatenate | bytes 1769472 | tf_op jit(solution)/shard_map/concatenate | solution.py:46
  33.9 3.3 %fusion.13 = (f32[16,4,4,8,128]{4,0,3,2,1:T(8,128)S(1)}, f32[16,4,4,8,128]{4,0,3,2,1:T(8,128)}) fusion(f32[16]{0:T(128)S(1)} %copy-done.10, bf16[16,108]{0,1:T(8,128)(2,1)S(1)} %reshape_reshape.9, bf16[1,4,8,108,128]{4,3,2,1,0:T(8,128)(2,1)} %bitcast.117, bf16[1,4,8,108,128]{4,3,2,1,0:T(8,128)(2,1)} %bitcast.115, ...), kind=kOutput, calls=%fused_computation.17 | convolution fusion | flops 63242240 | bytes 5639616 | tf_op jit(solution)/shard_map/ok,rxykm->orxym/dot_general | solution.py:51
  37.3 5.4 %collective-permute-start.2 = (bf16[16,2,1,4,128]{4,0,3,2,1:T(8,128)(2,1)S(1)}, bf16[16,2,1,4,128]{4,0,3,2,1:T(8,128)(2,1)S(1)}, u32[]{:S(2)}, u32[]{:S(2)}) collective-permute-start(bf16[16,2,1,4,128]{4,0,3,2,1:T(8,128)(2,1)S(1)} %get-tuple-element.45), channel_id=1, source_target_pairs={{0,1},{1,2},{2,3},{3,4},{4,5},{5,6},{6,7},{7,8},{8,9},{9,10},{10,1... | collective-permute-start | bytes 98312 | tf_op jit(solution)/shard_map/ppermute | solution.py:14
  42.8 1.9 %collective-permute-start.3 = (bf16[16,2,1,4,128]{4,0,3,2,1:T(8,128)(2,1)S(1)}, bf16[16,2,1,4,128]{4,0,3,2,1:T(8,128)(2,1)S(1)}, u32[]{:S(2)}, u32[]{:S(2)}) collective-permute-start(bf16[16,2,1,4,128]{4,0,3,2,1:T(8,128)(2,1)S(1)} %get-tuple-element.46), channel_id=1, source_target_pairs={{1,0},{2,1},{3,2},{4,3},{5,4},{6,5},{7,6},{8,7},{9,8},{10,9},{11,1... | collective-permute-start | bytes 98312 | tf_op jit(solution)/shard_map/ppermute | solution.py:16
  45.0 3.3 %collective-permute-done.3 = bf16[16,2,1,4,128]{4,0,3,2,1:T(8,128)(2,1)S(1)} collective-permute-done((bf16[16,2,1,4,128]{4,0,3,2,1:T(8,128)(2,1)S(1)}, bf16[16,2,1,4,128]{4,0,3,2,1:T(8,128)(2,1)S(1)}, u32[]{:S(2)}, u32[]{:S(2)}) %collective-permute-start.3) | collective-permute-done | bytes 32800 | tf_op jit(solution)/shard_map/ppermute | solution.py:16
  50.0 1.1 convert_reduce_fusion.1
  51.9 8.1 %collective-permute-start.4 = (bf16[32,2,1,4,128]{4,0,3,2,1:T(8,128)(2,1)}, bf16[32,2,1,4,128]{4,0,3,2,1:T(8,128)(2,1)}, u32[]{:S(2)}, u32[]{:S(2)}) collective-permute-start(bf16[32,2,1,4,128]{4,0,3,2,1:T(8,128)(2,1)} %get-tuple-element.35), channel_id=1, source_target_pairs={{0,1},{1,2},{2,3},{3,4},{4,5},{5,6},{6,7},{7,8},{8,9},{9,10},{10,1... | collective-permute-start | bytes 196616 | tf_op jit(solution)/shard_map/ppermute | solution.py:14
  60.0 2.1 %collective-permute-start.5 = (bf16[32,2,1,4,128]{4,0,3,2,1:T(8,128)(2,1)}, bf16[32,2,1,4,128]{4,0,3,2,1:T(8,128)(2,1)}, u32[]{:S(2)}, u32[]{:S(2)}) collective-permute-start(bf16[32,2,1,4,128]{4,0,3,2,1:T(8,128)(2,1)} %get-tuple-element.36), channel_id=1, source_target_pairs={{1,0},{2,1},{3,2},{4,3},{5,4},{6,5},{7,6},{8,7},{9,8},{10,9},{11,1... | collective-permute-start | bytes 196616 | tf_op jit(solution)/shard_map/ppermute | solution.py:16
  62.7 3.6 %copy.59 = f32[32,16,3,3,3]{4,3,2,1,0:T(4,128)S(1)} copy(f32[32,16,3,3,3]{0,1,4,3,2:T(8,128)S(1)} %bitcast.120) | data formatting | bytes 110592 | tf_op jit(solution)/shard_map/transpose | solution.py:93
  66.3 2.0 %reshape.91 = f32[13824]{0:T(1024)S(1)} reshape(f32[32,16,3,3,3]{4,3,2,1,0:T(4,128)S(1)} %copy.59) | data formatting | bytes 110592 | tf_op jit(solution)/shard_map/reshape | solution.py:74
  72.0 1.0 copy-done
  74.2 1.1 convolution_bitcast_fusion
  76.0 1.3 %collective-permute-start.6 = (f32[15600]{0:T(1024)S(1)}, f32[15600]{0:T(1024)S(1)}, u32[]{:S(2)}, u32[]{:S(2)}) collective-permute-start(f32[15600]{0:T(1024)S(1)} %concatenate.81), channel_id=1, source_target_pairs={{0,1},{1,0},{2,3},{3,2},{4,5},{5,4},{6,7},{7,6},{8,9},{9,8},{10,11... | collective-permute-start | bytes 187208 | tf_op jit(solution)/shard_map/ppermute | solution.py:79
  78.4 4.3 %collective-permute-done.7 = f32[15600]{0:T(1024)S(1)} collective-permute-done((f32[15600]{0:T(1024)S(1)}, f32[15600]{0:T(1024)S(1)}, u32[]{:S(2)}, u32[]{:S(2)}) %collective-permute-start.7) | collective-permute-done | bytes 62432 | tf_op jit(solution)/shard_map/ppermute | solution.py:79
  82.8 5.8 %collective-permute-done.8 = f32[15600]{0:T(1024)S(1)} collective-permute-done((f32[15600]{0:T(1024)S(1)}, f32[15600]{0:T(1024)S(1)}, u32[]{:S(2)}, u32[]{:S(2)}) %collective-permute-start.8) | collective-permute-done | bytes 62432 | tf_op jit(solution)/shard_map/ppermute | solution.py:79
  88.6 1.0 collective-permute-start.9
  89.6 4.9 %collective-permute-done.9 = f32[15600]{0:T(1024)S(1)} collective-permute-done((f32[15600]{0:T(1024)S(1)}, f32[15600]{0:T(1024)S(1)}, u32[]{:S(2)}, u32[]{:S(2)}) %collective-permute-start.9) | collective-permute-done | bytes 62432 | tf_op jit(solution)/shard_map/ppermute | solution.py:79
  94.5 2.0 %collective-permute-start.10 = (f32[15600]{0:T(1024)S(1)}, f32[15600]{0:T(1024)S(1)}, u32[]{:S(2)}, u32[]{:S(2)}) collective-permute-start(f32[15600]{0:T(1024)S(1)} %add.93), channel_id=1, source_target_pairs={{0,16},{16,0},{32,48},{48,32},{64,80},{80,64},{96,112},{112,96},{1... | collective-permute-start | bytes 187208 | tf_op jit(solution)/shard_map/ppermute | solution.py:79
  96.5 2.3 %collective-permute-done.10 = f32[15600]{0:T(1024)S(1)} collective-permute-done((f32[15600]{0:T(1024)S(1)}, f32[15600]{0:T(1024)S(1)}, u32[]{:S(2)}, u32[]{:S(2)}) %collective-permute-start.10) | collective-permute-done | bytes 62432 | tf_op jit(solution)/shard_map/ppermute | solution.py:79
  98.8 3.7 %collective-permute-start.11 = (f32[15600]{0:T(1024)S(1)}, f32[15600]{0:T(1024)S(1)}, u32[]{:S(2)}, u32[]{:S(2)}) collective-permute-start(f32[15600]{0:T(1024)S(1)} %add.94), channel_id=1, source_target_pairs={{0,32},{16,48},{32,0},{48,16},{64,96},{80,112},{96,64},{112,80},{1... | collective-permute-start | bytes 187208 | tf_op jit(solution)/shard_map/ppermute | solution.py:79
  102.6 2.2 %collective-permute-done.11 = f32[15600]{0:T(1024)S(1)} collective-permute-done((f32[15600]{0:T(1024)S(1)}, f32[15600]{0:T(1024)S(1)}, u32[]{:S(2)}, u32[]{:S(2)}) %collective-permute-start.11) | collective-permute-done | bytes 62432 | tf_op jit(solution)/shard_map/ppermute | solution.py:79
  104.8 8.1 %collective-permute-start.12 = (f32[15600]{0:T(1024)S(1)}, f32[15600]{0:T(1024)S(1)}, u32[]{:S(2)}, u32[]{:S(2)}) collective-permute-start(f32[15600]{0:T(1024)S(1)} %add.95), channel_id=1, source_target_pairs={{0,64},{16,80},{32,96},{48,112},{64,0},{80,16},{96,32},{112,48},{1... | collective-permute-start | bytes 187208 | tf_op jit(solution)/shard_map/ppermute | solution.py:79
  112.9 2.2 %collective-permute-done.12 = f32[15600]{0:T(1024)S(1)} collective-permute-done((f32[15600]{0:T(1024)S(1)}, f32[15600]{0:T(1024)S(1)}, u32[]{:S(2)}, u32[]{:S(2)}) %collective-permute-start.12) | collective-permute-done | bytes 62432 | tf_op jit(solution)/shard_map/ppermute | solution.py:79
  116.7 3.0 %collective-permute-done.13 = f32[15600]{0:T(1024)S(1)} collective-permute-done((f32[15600]{0:T(1024)S(1)}, f32[15600]{0:T(1024)S(1)}, u32[]{:S(2)}, u32[]{:S(2)}) %collective-permute-start.13) | collective-permute-done | bytes 62432 | tf_op jit(solution)/shard_map/ppermute | solution.py:79
  121.0 1.6 %reshape.93 = f32[32,16,3,3,3]{4,3,2,1,0:T(4,128)S(1)} reshape(f32[13824]{0:T(1024)S(1)} %slice.782) | data formatting | bytes 110592 | tf_op jit(solution)/shard_map/reshape | solution.py:83
  122.6 2.5 %copy.62 = f32[32,16,3,3,3]{0,1,4,3,2:T(8,128)} copy(f32[32,16,3,3,3]{4,3,2,1,0:T(4,128)S(1)} %reshape.93) | data formatting | bytes 110592
  125.4 0.9 copy.61
  (193 shorter events, 18.0 us)
Async XLA Ops:
  1.4 9.4 %collective-permute-start = (bf16[4,1,8,512]{3,2,1,0:T(8,128)(2,1)S(1)}, bf16[4,1,8,512]{3,2,1,0:T(8,128)(2,1)S(1)}, u32[]{:S(2)}, u32[]{:S(2)}) collective-permute-start(bf16[4,1,8,512]{3,2,1,0:T(8,128)(2,1)S(1)} %get-tuple-element.39), channel_id=1, source_target_pairs={{0,1},{1,2},{2,3},{3,4},{4,5},{5,6},{6,7},{7,8},{8,9},{9,10},{10,1... | collective-permute-start | bytes 98312 | tf_op jit(solution)/shard_map/ppermute | solution.py:14
  3.3 8.1 %collective-permute-start.1 = (bf16[4,1,8,512]{3,2,1,0:T(8,128)(2,1)S(1)}, bf16[4,1,8,512]{3,2,1,0:T(8,128)(2,1)S(1)}, u32[]{:S(2)}, u32[]{:S(2)}) collective-permute-start(bf16[4,1,8,512]{3,2,1,0:T(8,128)(2,1)S(1)} %get-tuple-element.40), channel_id=1, source_target_pairs={{1,0},{2,1},{3,2},{4,3},{5,4},{6,5},{7,6},{8,7},{9,8},{10,9},{11,1... | collective-permute-start | bytes 98312 | tf_op jit(solution)/shard_map/ppermute | solution.py:16
  7.7 3.1 %copy-start.9 = (bf16[16,4,3,3,3]{0,1,4,3,2:T(4,128)(2,1)S(1)}, bf16[16,4,3,3,3]{0,1,4,3,2:T(4,128)(2,1)}, u32[]{:S(2)}) copy-start(bf16[16,4,3,3,3]{0,1,4,3,2:T(4,128)(2,1)} %param.8) | copy-start | bytes 10372
  13.9 20.1 %copy-start.1 = (bf16[4,8,108,128]{3,2,1,0:T(8,128)(2,1)}, bf16[4,8,108,128]{3,2,1,0:T(8,128)(2,1)S(1)}, u32[]{:S(2)}) copy-start(bf16[4,8,108,128]{3,2,1,0:T(8,128)(2,1)S(1)} %concatenate.66) | copy-start | bytes 2654212
  14.7 19.3 %copy-start.3 = (bf16[4,8,108,128]{3,2,1,0:T(8,128)(2,1)}, bf16[4,8,108,128]{3,2,1,0:T(8,128)(2,1)S(1)}, u32[]{:S(2)}) copy-start(bf16[4,8,108,128]{3,2,1,0:T(8,128)(2,1)S(1)} %concatenate.67) | copy-start | bytes 2654212
  14.7 19.2 %copy-start.10 = (f32[16]{0:T(128)S(1)}, f32[16]{0:T(128)}, u32[]{:S(2)}) copy-start(f32[16]{0:T(128)} %param.9) | copy-start | bytes 196
  33.9 10.8 %copy-start.7 = (bf16[32,16,3,3,3]{0,1,4,3,2:T(8,128)(2,1)S(1)}, bf16[32,16,3,3,3]{0,1,4,3,2:T(8,128)(2,1)}, u32[]{:S(2)}) copy-start(bf16[32,16,3,3,3]{0,1,4,3,2:T(8,128)(2,1)} %param.10) | copy-start | bytes 82948
  37.3 7.6 %collective-permute-start.2 = (bf16[16,2,1,4,128]{4,0,3,2,1:T(8,128)(2,1)S(1)}, bf16[16,2,1,4,128]{4,0,3,2,1:T(8,128)(2,1)S(1)}, u32[]{:S(2)}, u32[]{:S(2)}) collective-permute-start(bf16[16,2,1,4,128]{4,0,3,2,1:T(8,128)(2,1)S(1)} %get-tuple-element.45), channel_id=1, source_target_pairs={{0,1},{1,2},{2,3},{3,4},{4,5},{5,6},{6,7},{7,8},{8,9},{9,10},{10,1... | collective-permute-start | bytes 98312 | tf_op jit(solution)/shard_map/ppermute | solution.py:14
  42.8 5.5 %collective-permute-start.3 = (bf16[16,2,1,4,128]{4,0,3,2,1:T(8,128)(2,1)S(1)}, bf16[16,2,1,4,128]{4,0,3,2,1:T(8,128)(2,1)S(1)}, u32[]{:S(2)}, u32[]{:S(2)}) collective-permute-start(bf16[16,2,1,4,128]{4,0,3,2,1:T(8,128)(2,1)S(1)} %get-tuple-element.46), channel_id=1, source_target_pairs={{1,0},{2,1},{3,2},{4,3},{5,4},{6,5},{7,6},{8,7},{9,8},{10,9},{11,1... | collective-permute-start | bytes 98312 | tf_op jit(solution)/shard_map/ppermute | solution.py:16
  49.0 1.0 copy-start.11
  51.9 16.4 %collective-permute-start.4 = (bf16[32,2,1,4,128]{4,0,3,2,1:T(8,128)(2,1)}, bf16[32,2,1,4,128]{4,0,3,2,1:T(8,128)(2,1)}, u32[]{:S(2)}, u32[]{:S(2)}) collective-permute-start(bf16[32,2,1,4,128]{4,0,3,2,1:T(8,128)(2,1)} %get-tuple-element.35), channel_id=1, source_target_pairs={{0,1},{1,2},{2,3},{3,4},{4,5},{5,6},{6,7},{7,8},{8,9},{9,10},{10,1... | collective-permute-start | bytes 196616 | tf_op jit(solution)/shard_map/ppermute | solution.py:14
  60.0 8.3 %collective-permute-start.5 = (bf16[32,2,1,4,128]{4,0,3,2,1:T(8,128)(2,1)}, bf16[32,2,1,4,128]{4,0,3,2,1:T(8,128)(2,1)}, u32[]{:S(2)}, u32[]{:S(2)}) collective-permute-start(bf16[32,2,1,4,128]{4,0,3,2,1:T(8,128)(2,1)} %get-tuple-element.36), channel_id=1, source_target_pairs={{1,0},{2,1},{3,2},{4,3},{5,4},{6,5},{7,6},{8,7},{9,8},{10,9},{11,1... | collective-permute-start | bytes 196616 | tf_op jit(solution)/shard_map/ppermute | solution.py:16
  71.8 1.2 copy-start
  71.9 1.7 %copy-start.2 = (bf16[4,8,108,128]{3,2,1,0:T(8,128)(2,1)S(1)}, bf16[4,8,108,128]{3,2,1,0:T(8,128)(2,1)}, u32[]{:S(2)}) copy-start(bf16[4,8,108,128]{3,2,1,0:T(8,128)(2,1)} %copy-done.1) | copy-start | bytes 2654212
  71.9 1.7 %copy-start.4 = (bf16[4,8,108,128]{3,2,1,0:T(8,128)(2,1)S(1)}, bf16[4,8,108,128]{3,2,1,0:T(8,128)(2,1)}, u32[]{:S(2)}) copy-start(bf16[4,8,108,128]{3,2,1,0:T(8,128)(2,1)} %copy-done.3) | copy-start | bytes 2654212
  71.9 2.0 %copy-start.5 = (bf16[4,8,108,128]{3,2,1,0:T(8,128)(2,1)S(1)}, bf16[4,8,108,128]{3,2,1,0:T(8,128)(2,1)}, u32[]{:S(2)}) copy-start(bf16[4,8,108,128]{3,2,1,0:T(8,128)(2,1)} %concatenate.68) | copy-start | bytes 2654212
  71.9 2.2 %copy-start.6 = (bf16[4,8,108,128]{3,2,1,0:T(8,128)(2,1)S(1)}, bf16[4,8,108,128]{3,2,1,0:T(8,128)(2,1)}, u32[]{:S(2)}) copy-start(bf16[4,8,108,128]{3,2,1,0:T(8,128)(2,1)} %concatenate.70) | copy-start | bytes 2654212
  75.3 37.6 %copy-start.8 = (f32[32,4,128]{2,0,1:T(8,128)S(1)}, f32[32,4,128]{2,0,1:T(8,128)}, u32[]{:S(2)}) copy-start(f32[32,4,128]{2,0,1:T(8,128)} %get-tuple-element.26) | copy-start | bytes 196612
  76.0 2.2 %collective-permute-start.6 = (f32[15600]{0:T(1024)S(1)}, f32[15600]{0:T(1024)S(1)}, u32[]{:S(2)}, u32[]{:S(2)}) collective-permute-start(f32[15600]{0:T(1024)S(1)} %concatenate.81), channel_id=1, source_target_pairs={{0,1},{1,0},{2,3},{3,2},{4,5},{5,4},{6,7},{7,6},{8,9},{9,8},{10,11... | collective-permute-start | bytes 187208 | tf_op jit(solution)/shard_map/ppermute | solution.py:79
  78.3 4.4 %collective-permute-start.7 = (f32[15600]{0:T(1024)S(1)}, f32[15600]{0:T(1024)S(1)}, u32[]{:S(2)}, u32[]{:S(2)}) collective-permute-start(f32[15600]{0:T(1024)S(1)} %add.90), channel_id=1, source_target_pairs={{0,2},{1,3},{2,0},{3,1},{4,6},{5,7},{6,4},{7,5},{8,10},{9,11},{10,... | collective-permute-start | bytes 187208 | tf_op jit(solution)/shard_map/ppermute | solution.py:79
  82.7 5.9 %collective-permute-start.8 = (f32[15600]{0:T(1024)S(1)}, f32[15600]{0:T(1024)S(1)}, u32[]{:S(2)}, u32[]{:S(2)}) collective-permute-start(f32[15600]{0:T(1024)S(1)} %add.91), channel_id=1, source_target_pairs={{0,4},{1,5},{2,6},{3,7},{4,0},{5,1},{6,2},{7,3},{8,12},{9,13},{10,... | collective-permute-start | bytes 187208 | tf_op jit(solution)/shard_map/ppermute | solution.py:79
  88.6 5.9 %collective-permute-start.9 = (f32[15600]{0:T(1024)S(1)}, f32[15600]{0:T(1024)S(1)}, u32[]{:S(2)}, u32[]{:S(2)}) collective-permute-start(f32[15600]{0:T(1024)S(1)} %add.92), channel_id=1, source_target_pairs={{0,8},{1,9},{2,10},{3,11},{4,12},{5,13},{6,14},{7,15},{8,0},{9,1},... | collective-permute-start | bytes 187208 | tf_op jit(solution)/shard_map/ppermute | solution.py:79
  94.5 4.4 %collective-permute-start.10 = (f32[15600]{0:T(1024)S(1)}, f32[15600]{0:T(1024)S(1)}, u32[]{:S(2)}, u32[]{:S(2)}) collective-permute-start(f32[15600]{0:T(1024)S(1)} %add.93), channel_id=1, source_target_pairs={{0,16},{16,0},{32,48},{48,32},{64,80},{80,64},{96,112},{112,96},{1... | collective-permute-start | bytes 187208 | tf_op jit(solution)/shard_map/ppermute | solution.py:79
  98.8 6.0 %collective-permute-start.11 = (f32[15600]{0:T(1024)S(1)}, f32[15600]{0:T(1024)S(1)}, u32[]{:S(2)}, u32[]{:S(2)}) collective-permute-start(f32[15600]{0:T(1024)S(1)} %add.94), channel_id=1, source_target_pairs={{0,32},{16,48},{32,0},{48,16},{64,96},{80,112},{96,64},{112,80},{1... | collective-permute-start | bytes 187208 | tf_op jit(solution)/shard_map/ppermute | solution.py:79
  104.8 10.3 %collective-permute-start.12 = (f32[15600]{0:T(1024)S(1)}, f32[15600]{0:T(1024)S(1)}, u32[]{:S(2)}, u32[]{:S(2)}) collective-permute-start(f32[15600]{0:T(1024)S(1)} %add.95), channel_id=1, source_target_pairs={{0,64},{16,80},{32,96},{48,112},{64,0},{80,16},{96,32},{112,48},{1... | collective-permute-start | bytes 187208 | tf_op jit(solution)/shard_map/ppermute | solution.py:79
  115.2 4.6 %collective-permute-start.13 = (f32[15600]{0:T(1024)S(1)}, f32[15600]{0:T(1024)S(1)}, u32[]{:S(2)}, u32[]{:S(2)}) collective-permute-start(f32[15600]{0:T(1024)S(1)} %add.96), channel_id=1, source_target_pairs={{0,128},{16,144},{32,160},{48,176},{64,192},{80,208},{96,224},{112... | collective-permute-start | bytes 187208 | tf_op jit(solution)/shard_map/ppermute | solution.py:79

commit v2 on v1

--- a/solution.py
+++ b/solution.py
@@ -32,7 +32,11 @@
     phases, depth, height, _, width = field.shape
     depth -= 2
     field = jnp.pad(field, ((0, 0), (0, 0), (1, 1), (0, 0), (0, 0)))
-    sources = {}
+    keys = sorted({((r + e - 1) % phases, (r + e - 1) // phases) for r in range(phases) for e in range(3)})
+    moved = [key for key in keys if key[1] != 0]
+    shifted = lax.optimization_barrier(tuple(lane_shift(field[key[0]], key[1]) for key in moved))
+    sources = {key: field[key[0]] for key in keys if key[1] == 0}
+    sources.update(zip(moved, shifted))
     out = []
     for r in range(phases):
         taps = []
@@ -40,8 +44,6 @@
             for b in range(3):
                 for e in range(3):
                     key = ((r + e - 1) % phases, (r + e - 1) // phases)
-                    if key not in sources:
-                        sources[key] = lane_shift(field[key[0]], key[1])
                     taps.append(sources[key][a : a + depth, b : b + height])
         out.append(jnp.concatenate(taps, axis=2))
     return jnp.stack(out, axis=0)
@@ -70,19 +72,14 @@
     return sig * (1.0 + value * (1.0 - sig))
 
 
-def butterfly_sum(parts, axes):
-    flat = jnp.concatenate([part.reshape(-1) for part in parts])
+def butterfly_sum(rows, axes):
     for axis in axes:
         count = lax.axis_size(axis)
         step = 1
         while step < count:
-            flat = flat + lax.ppermute(flat, axis, [(i, i ^ step) for i in range(count)])
+            rows = rows + lax.ppermute(rows, axis, [(i, i ^ step) for i in range(count)])
             step *= 2
-    sums, start = [], 0
-    for part in parts:
-        sums.append(flat[start : start + part.size].reshape(part.shape))
-        start += part.size
-    return tuple(sums)
+    return rows
 
 
 def tap_major(kern):
@@ -117,11 +114,22 @@
     grad_first = (upsample(back, 4) * 0.125 * silu_slope(pre_first)).astype(jnp.bfloat16)
     grad_w1 = grad_taps(grad_first, patches_first)
     grad_b1 = jnp.sum(grad_first.astype(jnp.float32), axis=(1, 2, 3, 4))
-    totals = butterfly_sum(
-        (tap_minor(grad_w1, chan0), grad_b1, tap_minor(grad_w2, w_second.shape[1]), grad_b2),
-        ("space", "dp"),
+    chan1 = w_second.shape[1]
+    lanes = grad_w2.shape[1]
+    biases = jnp.concatenate([grad_b1, grad_b2])
+    rows = jnp.concatenate(
+        [
+            grad_w2,
+            jnp.pad(grad_w1, ((0, 0), (0, lanes - grad_w1.shape[1]))),
+            jnp.pad(biases, (0, lanes - biases.shape[0]))[None],
+        ]
     )
-    return (output[None], totals[0], totals[1], totals[2], totals[3])
+    totals = butterfly_sum(rows, ("space", "dp"))
+    out_w2 = tap_minor(totals[: grad_w2.shape[0]], chan1)
+    out_w1 = tap_minor(totals[grad_w2.shape[0] : -1, : grad_w1.shape[1]], chan0)
+    out_b1 = totals[-1, : grad_b1.shape[0]]
+    out_b2 = totals[-1, grad_b1.shape[0] : biases.shape[0]]
+    return (output[None], out_w1, out_b1, out_w2, out_b2)
 
 
 def solution(mesh):

time: 128 us -> 133 us (1.039)
  waiting for transfers between devices: 29 us -> 36.1 us
  starting transfers between devices: 40.4 us -> 45.6 us
  local copies, waits for them, and re-layouts: 46 us -> 42 us
  matrix products: 6.66 us -> 5.15 us
    concatenate x8, local copies, waits for them, and re-layouts: 20.9 us -> 29.6 us  [phase_patches(): out.append(jnp.concatenate(taps, axis=2))]
    ppermute x8, waiting for transfers between devices: 25.7 us -> 32.1 us  [butterfly_sum(): lax.ppermute(rows, axis, [(i, i ^ step) for i in range(count)])]
    unnamed x128 -> x116, local copies, waits for them, and re-layouts: 10.5 us -> 4.82 us
    ppermute x8, starting transfers between devices: 17.2 us -> 22 us  [butterfly_sum(): lax.ppermute(rows, axis, [(i, i ^ step) for i in range(count)])]
    reshape x4 -> x0, local copies, waits for them, and re-layouts: 4.05 us -> none  [the longest x2 2.21 us: butterfly_sum(): flat = jnp.concatenate([part.reshape(-1) for part in parts])]
    transpose x2 -> x0, local copies, waits for them, and re-layouts: 3.91 us -> none  [tap_minor(): jnp.transpose(grad.reshape(grad.shape[0], 3, 3, 3, chan), (0, 4, 1, 2, 3))]
    dot_general x3, matrix products: 4.99 us -> 3.51 us  [conv_taps(): jnp.einsum('ok,rxykm->orxym', kern.reshape(kern.shape[0], -1), patches, p...]
  transfers between devices with their start and end apart: 14 -> 14, of which waited for: 9 -> 10; matrix products, arithmetic and copies ran while one was open for 9% -> 4% of each run, Pallas kernels for 0% -> 0%
where the time goes in v2:
time: 133 us; the launch traced here: 132 us
  starting transfers between devices  45.6 us (34%)
  local copies, waits for them, and re-layouts  42 us (32%)
  waiting for transfers between devices  36.1 us (27%)
  matrix products  5.15 us (4%)
  other arithmetic  1.83 us (1%)
  between operations  1.62 us (1%)
    ppermute x8, waiting for transfers between devices, butterfly_sum(): lax.ppermute(rows, axis, [(i, i ^ step) for i in range(count)])  32.1 us
    concatenate x8, local copies, waits for them, and re-layouts, phase_patches(): out.append(jnp.concatenate(taps, axis=2))  29.6 us
    ppermute x8, starting transfers between devices, butterfly_sum(): lax.ppermute(rows, axis, [(i, i ^ step) for i in range(count)])  22 us
    ppermute x3, starting transfers between devices, with_halo(): lax.ppermute(tail, axis, [(i, (i + 1) % count) for i in range(ends)])  16.1 us
    ppermute x3, starting transfers between devices, with_halo(): lax.ppermute(head, axis, [((i + 1) % count, i) for i in range(ends)])  7.48 us
    unnamed x116, local copies, waits for them, and re-layouts  4.82 us
    ppermute x3, waiting for transfers between devices, with_halo(): lax.ppermute(head, axis, [((i + 1) % count, i) for i in range(ends)])  3.96 us
    dot_general x3, matrix products, conv_taps(): jnp.einsum('ok,rxykm->orxym', kern.reshape(kern.shape[0], -1), patches, p...  3.51 us
  transfers between devices with their start and end apart: 14, of which 10 were waited for; matrix products, arithmetic and copies ran while one was open for 4% of the time, Pallas kernels for 0%

profile of v2, /device:TPU:24, one launch (start us, length us, event | category | flops | bytes accessed | tf_op | source)
XLA Modules:
  0.0 132.4 jit_solution(1951188217188287617)
XLA Ops:
  0.6 0.8 fusion.35
  1.4 1.9 %collective-permute-start = (bf16[4,1,8,512]{3,2,1,0:T(8,128)(2,1)S(1)}, bf16[4,1,8,512]{3,2,1,0:T(8,128)(2,1)S(1)}, u32[]{:S(2)}, u32[]{:S(2)}) collective-permute-start(bf16[4,1,8,512]{3,2,1,0:T(8,128)(2,1)S(1)} %get-tuple-element.41), channel_id=1, source_target_pairs={{0,1},{1,2},{2,3},{3,4},{4,5},{5,6},{6,7},{7,8},{8,9},{9,10},{10,1... | collective-permute-start | bytes 98312 | tf_op jit(solution)/shard_map/ppermute | solution.py:14
  3.3 3.6 %collective-permute-start.1 = (bf16[4,1,8,512]{3,2,1,0:T(8,128)(2,1)S(1)}, bf16[4,1,8,512]{3,2,1,0:T(8,128)(2,1)S(1)}, u32[]{:S(2)}, u32[]{:S(2)}) collective-permute-start(bf16[4,1,8,512]{3,2,1,0:T(8,128)(2,1)S(1)} %get-tuple-element.42), channel_id=1, source_target_pairs={{1,0},{2,1},{3,2},{4,3},{5,4},{6,5},{7,6},{8,7},{9,8},{10,9},{11,1... | collective-permute-start | bytes 98312 | tf_op jit(solution)/shard_map/ppermute | solution.py:16
  7.0 0.7 multiply_bitcast_fusion
  7.7 1.8 %copy.41 = bf16[1,4,4,8,512]{3,4,2,1,0:T(8,128)(2,1)S(1)} copy(bf16[1,4,4,8,512]{4,3,2,1,0:T(8,128)(2,1)} %param.6) | data formatting | bytes 262144 | tf_op args[0]
  9.6 1.2 copy.44
  13.0 0.8 concatenate.73
  13.9 9.6 %concatenate.72 = bf16[4,8,108,128]{3,2,1,0:T(8,128)(2,1)} concatenate(bf16[4,8,4,128]{3,2,1,0:T(4,128)(2,1)S(1)} %get-tuple-element.105, bf16[4,8,4,128]{3,2,1,0:T(4,128)(2,1)S(1)} %get-tuple-element.114, bf16[4,8,4,128]{3,2,1,0:T(4,128)(2,1)S(1)} %get-tuple-element.93, bf16[4,8,4,128]{3,2,1,0:T(4,128)(2,1)S(1)} %get-tuple-element.106, ...), dimensions={2} | concatenate | bytes 1769472 | tf_op jit(solution)/shard_map/concatenate | solution.py:48
  23.4 9.5 %concatenate.71 = bf16[4,8,108,128]{3,2,1,0:T(8,128)(2,1)} concatenate(bf16[4,8,4,128]{3,2,1,0:T(4,128)(2,1)S(1)} %get-tuple-element.66, bf16[4,8,4,128]{3,2,1,0:T(4,128)(2,1)S(1)} %get-tuple-element.105, bf16[4,8,4,128]{3,2,1,0:T(4,128)(2,1)S(1)} %get-tuple-element.114, bf16[4,8,4,128]{3,2,1,0:T(4,128)(2,1)S(1)} %get-tuple-element.65, ...), dimensions={2} | concatenate | bytes 1769472 | tf_op jit(solution)/shard_map/concatenate | solution.py:48
  32.9 9.7 %concatenate.70 = bf16[4,8,108,128]{3,2,1,0:T(8,128)(2,1)} concatenate(bf16[4,8,4,128]{3,2,1,0:T(4,128)(2,1)S(1)} %get-tuple-element.57, bf16[4,8,4,128]{3,2,1,0:T(4,128)(2,1)S(1)} %get-tuple-element.66, bf16[4,8,4,128]{3,2,1,0:T(4,128)(2,1)S(1)} %get-tuple-element.105, bf16[4,8,4,128]{3,2,1,0:T(4,128)(2,1)S(1)} %get-tuple-element.56, ...), dimensions={2} | concatenate | bytes 1769472 | tf_op jit(solution)/shard_map/concatenate | solution.py:48
  42.6 2.3 %fusion.14 = (f32[16,4,4,8,128]{4,0,3,2,1:T(8,128)S(1)}, f32[16,4,4,8,128]{4,0,3,2,1:T(8,128)S(1)}) fusion(f32[16]{0:T(128)S(1)} %copy-done.5, bf16[16,108]{0,1:T(8,128)(2,1)S(1)} %reshape_reshape.9, bf16[1,4,8,108,128]{4,3,2,1,0:T(8,128)(2,1)S(1)} %bitcast.104, bf16[1,4,8,108,128]{4,3,2,1,0:T(8,128)(2,1)} %bitcast.106, ...), kind=kOutput, calls=%fused_computation.18 | convolution fusion | flops 63242240 | bytes 5639616 | tf_op jit(solution)/shard_map/ok,rxykm->orxym/dot_general | solution.py:53
  45.1 6.1 %collective-permute-start.2 = (bf16[16,2,1,4,128]{4,0,3,2,1:T(8,128)(2,1)S(1)}, bf16[16,2,1,4,128]{4,0,3,2,1:T(8,128)(2,1)S(1)}, u32[]{:S(2)}, u32[]{:S(2)}) collective-permute-start(bf16[16,2,1,4,128]{4,0,3,2,1:T(8,128)(2,1)S(1)} %get-tuple-element.47), channel_id=1, source_target_pairs={{0,1},{1,2},{2,3},{3,4},{4,5},{5,6},{6,7},{7,8},{8,9},{9,10},{10,1... | collective-permute-start | bytes 98312 | tf_op jit(solution)/shard_map/ppermute | solution.py:14
  51.1 1.9 %collective-permute-start.3 = (bf16[16,2,1,4,128]{4,0,3,2,1:T(8,128)(2,1)S(1)}, bf16[16,2,1,4,128]{4,0,3,2,1:T(8,128)(2,1)S(1)}, u32[]{:S(2)}, u32[]{:S(2)}) collective-permute-start(bf16[16,2,1,4,128]{4,0,3,2,1:T(8,128)(2,1)S(1)} %get-tuple-element.48), channel_id=1, source_target_pairs={{1,0},{2,1},{3,2},{4,3},{5,4},{6,5},{7,6},{8,7},{9,8},{10,9},{11,1... | collective-permute-start | bytes 98312 | tf_op jit(solution)/shard_map/ppermute | solution.py:16
  53.3 2.7 %collective-permute-done.3 = bf16[16,2,1,4,128]{4,0,3,2,1:T(8,128)(2,1)S(1)} collective-permute-done((bf16[16,2,1,4,128]{4,0,3,2,1:T(8,128)(2,1)S(1)}, bf16[16,2,1,4,128]{4,0,3,2,1:T(8,128)(2,1)S(1)}, u32[]{:S(2)}, u32[]{:S(2)}) %collective-permute-start.3) | collective-permute-done | bytes 32800 | tf_op jit(solution)/shard_map/ppermute | solution.py:16
  57.8 8.2 %collective-permute-start.4 = (bf16[32,2,1,4,128]{4,0,3,2,1:T(8,128)(2,1)S(1)}, bf16[32,2,1,4,128]{4,0,3,2,1:T(8,128)(2,1)S(1)}, u32[]{:S(2)}, u32[]{:S(2)}) collective-permute-start(bf16[32,2,1,4,128]{4,0,3,2,1:T(8,128)(2,1)S(1)} %get-tuple-element.37), channel_id=1, source_target_pairs={{0,1},{1,2},{2,3},{3,4},{4,5},{5,6},{6,7},{7,8},{8,9},{9,10},{10,1... | collective-permute-start | bytes 196616 | tf_op jit(solution)/shard_map/ppermute | solution.py:14
  65.9 1.9 %collective-permute-start.5 = (bf16[32,2,1,4,128]{4,0,3,2,1:T(8,128)(2,1)S(1)}, bf16[32,2,1,4,128]{4,0,3,2,1:T(8,128)(2,1)S(1)}, u32[]{:S(2)}, u32[]{:S(2)}) collective-permute-start(bf16[32,2,1,4,128]{4,0,3,2,1:T(8,128)(2,1)S(1)} %get-tuple-element.38), channel_id=1, source_target_pairs={{1,0},{2,1},{3,2},{4,3},{5,4},{6,5},{7,6},{8,7},{9,8},{10,9},{11,1... | collective-permute-start | bytes 196616 | tf_op jit(solution)/shard_map/ppermute | solution.py:16
  68.5 1.3 collective-permute-done.5
  73.6 1.1 convolution_bitcast_fusion
  74.7 5.5 %collective-permute-start.6 = (f32[49,432]{1,0:T(8,128)S(1)}, f32[49,432]{1,0:T(8,128)S(1)}, u32[]{:S(2)}, u32[]{:S(2)}) collective-permute-start(f32[49,432]{1,0:T(8,128)S(1)} %fusion.17), channel_id=1, source_target_pairs={{0,1},{1,0},{2,3},{3,2},{4,5},{5,4},{6,7},{7,6},{8,9},{9,8},{10,11... | collective-permute-start | bytes 254024 | tf_op jit(solution)/shard_map/ppermute | solution.py:80
  80.2 1.0 collective-permute-done.6
  81.3 5.4 %collective-permute-done.7 = f32[49,432]{1,0:T(8,128)S(1)} collective-permute-done((f32[49,432]{1,0:T(8,128)S(1)}, f32[49,432]{1,0:T(8,128)S(1)}, u32[]{:S(2)}, u32[]{:S(2)}) %collective-permute-start.7) | collective-permute-done | bytes 84704 | tf_op jit(solution)/shard_map/ppermute | solution.py:80
  87.0 6.3 %collective-permute-done.8 = f32[49,432]{1,0:T(8,128)S(1)} collective-permute-done((f32[49,432]{1,0:T(8,128)S(1)}, f32[49,432]{1,0:T(8,128)S(1)}, u32[]{:S(2)}, u32[]{:S(2)}) %collective-permute-start.8) | collective-permute-done | bytes 84704 | tf_op jit(solution)/shard_map/ppermute | solution.py:80
  93.4 6.3 %collective-permute-done.9 = f32[49,432]{1,0:T(8,128)S(1)} collective-permute-done((f32[49,432]{1,0:T(8,128)S(1)}, f32[49,432]{1,0:T(8,128)S(1)}, u32[]{:S(2)}, u32[]{:S(2)}) %collective-permute-start.9) | collective-permute-done | bytes 84704 | tf_op jit(solution)/shard_map/ppermute | solution.py:80
  99.7 2.0 %collective-permute-start.10 = (f32[49,432]{1,0:T(8,128)S(1)}, f32[49,432]{1,0:T(8,128)S(1)}, u32[]{:S(2)}, u32[]{:S(2)}) collective-permute-start(f32[49,432]{1,0:T(8,128)S(1)} %add.97), channel_id=1, source_target_pairs={{0,16},{16,0},{32,48},{48,32},{64,80},{80,64},{96,112},{112,96},{1... | collective-permute-start | bytes 254024 | tf_op jit(solution)/shard_map/ppermute | solution.py:80
  101.7 2.9 %collective-permute-done.10 = f32[49,432]{1,0:T(8,128)S(1)} collective-permute-done((f32[49,432]{1,0:T(8,128)S(1)}, f32[49,432]{1,0:T(8,128)S(1)}, u32[]{:S(2)}, u32[]{:S(2)}) %collective-permute-start.10) | collective-permute-done | bytes 84704 | tf_op jit(solution)/shard_map/ppermute | solution.py:80
  104.6 4.4 %collective-permute-start.11 = (f32[49,432]{1,0:T(8,128)S(1)}, f32[49,432]{1,0:T(8,128)S(1)}, u32[]{:S(2)}, u32[]{:S(2)}) collective-permute-start(f32[49,432]{1,0:T(8,128)S(1)} %add.98), channel_id=1, source_target_pairs={{0,32},{16,48},{32,0},{48,16},{64,96},{80,112},{96,64},{112,80},{1... | collective-permute-start | bytes 254024 | tf_op jit(solution)/shard_map/ppermute | solution.py:80
  109.0 4.0 %collective-permute-done.11 = f32[49,432]{1,0:T(8,128)S(1)} collective-permute-done((f32[49,432]{1,0:T(8,128)S(1)}, f32[49,432]{1,0:T(8,128)S(1)}, u32[]{:S(2)}, u32[]{:S(2)}) %collective-permute-start.11) | collective-permute-done | bytes 84704 | tf_op jit(solution)/shard_map/ppermute | solution.py:80
  113.0 9.0 %collective-permute-start.12 = (f32[49,432]{1,0:T(8,128)S(1)}, f32[49,432]{1,0:T(8,128)S(1)}, u32[]{:S(2)}, u32[]{:S(2)}) collective-permute-start(f32[49,432]{1,0:T(8,128)S(1)} %add.99), channel_id=1, source_target_pairs={{0,64},{16,80},{32,96},{48,112},{64,0},{80,16},{96,32},{112,48},{1... | collective-permute-start | bytes 254024 | tf_op jit(solution)/shard_map/ppermute | solution.py:80
  122.0 2.8 %collective-permute-done.12 = f32[49,432]{1,0:T(8,128)S(1)} collective-permute-done((f32[49,432]{1,0:T(8,128)S(1)}, f32[49,432]{1,0:T(8,128)S(1)}, u32[]{:S(2)}, u32[]{:S(2)}) %collective-permute-start.12) | collective-permute-done | bytes 84704 | tf_op jit(solution)/shard_map/ppermute | solution.py:80
  124.8 0.7 collective-permute-start.13
  126.1 3.6 %collective-permute-done.13 = f32[49,432]{1,0:T(8,128)S(1)} collective-permute-done((f32[49,432]{1,0:T(8,128)S(1)}, f32[49,432]{1,0:T(8,128)S(1)}, u32[]{:S(2)}, u32[]{:S(2)}) %collective-permute-start.13) | collective-permute-done | bytes 84704 | tf_op jit(solution)/shard_map/ppermute | solution.py:80
  131.6 0.8 copy.51
  (183 shorter events, 11.2 us)
Async XLA Ops:
  0.6 8.9 %copy-start.4 = (bf16[16,4,3,3,3]{0,1,4,3,2:T(4,128)(2,1)S(1)}, bf16[16,4,3,3,3]{0,1,4,3,2:T(4,128)(2,1)}, u32[]{:S(2)}) copy-start(bf16[16,4,3,3,3]{0,1,4,3,2:T(4,128)(2,1)} %param.8) | copy-start | bytes 10372
  1.4 10.0 %collective-permute-start = (bf16[4,1,8,512]{3,2,1,0:T(8,128)(2,1)S(1)}, bf16[4,1,8,512]{3,2,1,0:T(8,128)(2,1)S(1)}, u32[]{:S(2)}, u32[]{:S(2)}) collective-permute-start(bf16[4,1,8,512]{3,2,1,0:T(8,128)(2,1)S(1)} %get-tuple-element.41), channel_id=1, source_target_pairs={{0,1},{1,2},{2,3},{3,4},{4,5},{5,6},{6,7},{7,8},{8,9},{9,10},{10,1... | collective-permute-start | bytes 98312 | tf_op jit(solution)/shard_map/ppermute | solution.py:14
  3.3 7.5 %collective-permute-start.1 = (bf16[4,1,8,512]{3,2,1,0:T(8,128)(2,1)S(1)}, bf16[4,1,8,512]{3,2,1,0:T(8,128)(2,1)S(1)}, u32[]{:S(2)}, u32[]{:S(2)}) collective-permute-start(bf16[4,1,8,512]{3,2,1,0:T(8,128)(2,1)S(1)} %get-tuple-element.42), channel_id=1, source_target_pairs={{1,0},{2,1},{3,2},{4,3},{5,4},{6,5},{7,6},{8,7},{9,8},{10,9},{11,1... | collective-permute-start | bytes 98312 | tf_op jit(solution)/shard_map/ppermute | solution.py:16
  23.4 19.2 %copy-start.5 = (f32[16]{0:T(128)S(1)}, f32[16]{0:T(128)}, u32[]{:S(2)}) copy-start(f32[16]{0:T(128)} %param.9) | copy-start | bytes 196
  42.6 10.5 %copy-start.3 = (bf16[32,16,3,3,3]{0,1,4,3,2:T(8,128)(2,1)S(1)}, bf16[32,16,3,3,3]{0,1,4,3,2:T(8,128)(2,1)}, u32[]{:S(2)}) copy-start(bf16[32,16,3,3,3]{0,1,4,3,2:T(8,128)(2,1)} %param.10) | copy-start | bytes 82948
  45.1 8.2 %collective-permute-start.2 = (bf16[16,2,1,4,128]{4,0,3,2,1:T(8,128)(2,1)S(1)}, bf16[16,2,1,4,128]{4,0,3,2,1:T(8,128)(2,1)S(1)}, u32[]{:S(2)}, u32[]{:S(2)}) collective-permute-start(bf16[16,2,1,4,128]{4,0,3,2,1:T(8,128)(2,1)S(1)} %get-tuple-element.47), channel_id=1, source_target_pairs={{0,1},{1,2},{2,3},{3,4},{4,5},{5,6},{6,7},{7,8},{8,9},{9,10},{10,1... | collective-permute-start | bytes 98312 | tf_op jit(solution)/shard_map/ppermute | solution.py:14
  51.1 4.9 %collective-permute-start.3 = (bf16[16,2,1,4,128]{4,0,3,2,1:T(8,128)(2,1)S(1)}, bf16[16,2,1,4,128]{4,0,3,2,1:T(8,128)(2,1)S(1)}, u32[]{:S(2)}, u32[]{:S(2)}) collective-permute-start(bf16[16,2,1,4,128]{4,0,3,2,1:T(8,128)(2,1)S(1)} %get-tuple-element.48), channel_id=1, source_target_pairs={{1,0},{2,1},{3,2},{4,3},{5,4},{6,5},{7,6},{8,7},{9,8},{10,9},{11,1... | collective-permute-start | bytes 98312 | tf_op jit(solution)/shard_map/ppermute | solution.py:16
  56.3 0.8 copy-start.6
  57.8 10.7 %collective-permute-start.4 = (bf16[32,2,1,4,128]{4,0,3,2,1:T(8,128)(2,1)S(1)}, bf16[32,2,1,4,128]{4,0,3,2,1:T(8,128)(2,1)S(1)}, u32[]{:S(2)}, u32[]{:S(2)}) collective-permute-start(bf16[32,2,1,4,128]{4,0,3,2,1:T(8,128)(2,1)S(1)} %get-tuple-element.37), channel_id=1, source_target_pairs={{0,1},{1,2},{2,3},{3,4},{4,5},{5,6},{6,7},{7,8},{8,9},{9,10},{10,1... | collective-permute-start | bytes 196616 | tf_op jit(solution)/shard_map/ppermute | solution.py:14
  65.9 3.8 %collective-permute-start.5 = (bf16[32,2,1,4,128]{4,0,3,2,1:T(8,128)(2,1)S(1)}, bf16[32,2,1,4,128]{4,0,3,2,1:T(8,128)(2,1)S(1)}, u32[]{:S(2)}, u32[]{:S(2)}) collective-permute-start(bf16[32,2,1,4,128]{4,0,3,2,1:T(8,128)(2,1)S(1)} %get-tuple-element.38), channel_id=1, source_target_pairs={{1,0},{2,1},{3,2},{4,3},{5,4},{6,5},{7,6},{8,7},{9,8},{10,9},{11,1... | collective-permute-start | bytes 196616 | tf_op jit(solution)/shard_map/ppermute | solution.py:16
  71.8 1.2 copy-start
  71.8 1.4 %copy-start.1 = (bf16[4,8,108,128]{3,2,1,0:T(8,128)(2,1)S(1)}, bf16[4,8,108,128]{3,2,1,0:T(8,128)(2,1)}, u32[]{:S(2)}) copy-start(bf16[4,8,108,128]{3,2,1,0:T(8,128)(2,1)} %concatenate.71) | copy-start | bytes 2654212
  71.8 1.7 %copy-start.2 = (bf16[4,8,108,128]{3,2,1,0:T(8,128)(2,1)S(1)}, bf16[4,8,108,128]{3,2,1,0:T(8,128)(2,1)}, u32[]{:S(2)}) copy-start(bf16[4,8,108,128]{3,2,1,0:T(8,128)(2,1)} %concatenate.70) | copy-start | bytes 2654212
  74.7 6.5 %collective-permute-start.6 = (f32[49,432]{1,0:T(8,128)S(1)}, f32[49,432]{1,0:T(8,128)S(1)}, u32[]{:S(2)}, u32[]{:S(2)}) collective-permute-start(f32[49,432]{1,0:T(8,128)S(1)} %fusion.17), channel_id=1, source_target_pairs={{0,1},{1,0},{2,3},{3,2},{4,5},{5,4},{6,7},{7,6},{8,9},{9,8},{10,11... | collective-permute-start | bytes 254024 | tf_op jit(solution)/shard_map/ppermute | solution.py:80
  81.2 5.5 %collective-permute-start.7 = (f32[49,432]{1,0:T(8,128)S(1)}, f32[49,432]{1,0:T(8,128)S(1)}, u32[]{:S(2)}, u32[]{:S(2)}) collective-permute-start(f32[49,432]{1,0:T(8,128)S(1)} %fusion.33), channel_id=1, source_target_pairs={{0,2},{1,3},{2,0},{3,1},{4,6},{5,7},{6,4},{7,5},{8,10},{9,11},{10,... | collective-permute-start | bytes 254024 | tf_op jit(solution)/shard_map/ppermute | solution.py:80
  86.7 6.6 %collective-permute-start.8 = (f32[49,432]{1,0:T(8,128)S(1)}, f32[49,432]{1,0:T(8,128)S(1)}, u32[]{:S(2)}, u32[]{:S(2)}) collective-permute-start(f32[49,432]{1,0:T(8,128)S(1)} %add.95), channel_id=1, source_target_pairs={{0,4},{1,5},{2,6},{3,7},{4,0},{5,1},{6,2},{7,3},{8,12},{9,13},{10,... | collective-permute-start | bytes 254024 | tf_op jit(solution)/shard_map/ppermute | solution.py:80
  93.3 6.4 %collective-permute-start.9 = (f32[49,432]{1,0:T(8,128)S(1)}, f32[49,432]{1,0:T(8,128)S(1)}, u32[]{:S(2)}, u32[]{:S(2)}) collective-permute-start(f32[49,432]{1,0:T(8,128)S(1)} %add.96), channel_id=1, source_target_pairs={{0,8},{1,9},{2,10},{3,11},{4,12},{5,13},{6,14},{7,15},{8,0},{9,1},... | collective-permute-start | bytes 254024 | tf_op jit(solution)/shard_map/ppermute | solution.py:80
  99.7 4.9 %collective-permute-start.10 = (f32[49,432]{1,0:T(8,128)S(1)}, f32[49,432]{1,0:T(8,128)S(1)}, u32[]{:S(2)}, u32[]{:S(2)}) collective-permute-start(f32[49,432]{1,0:T(8,128)S(1)} %add.97), channel_id=1, source_target_pairs={{0,16},{16,0},{32,48},{48,32},{64,80},{80,64},{96,112},{112,96},{1... | collective-permute-start | bytes 254024 | tf_op jit(solution)/shard_map/ppermute | solution.py:80
  104.6 8.4 %collective-permute-start.11 = (f32[49,432]{1,0:T(8,128)S(1)}, f32[49,432]{1,0:T(8,128)S(1)}, u32[]{:S(2)}, u32[]{:S(2)}) collective-permute-start(f32[49,432]{1,0:T(8,128)S(1)} %add.98), channel_id=1, source_target_pairs={{0,32},{16,48},{32,0},{48,16},{64,96},{80,112},{96,64},{112,80},{1... | collective-permute-start | bytes 254024 | tf_op jit(solution)/shard_map/ppermute | solution.py:80
  113.0 11.8 %collective-permute-start.12 = (f32[49,432]{1,0:T(8,128)S(1)}, f32[49,432]{1,0:T(8,128)S(1)}, u32[]{:S(2)}, u32[]{:S(2)}) collective-permute-start(f32[49,432]{1,0:T(8,128)S(1)} %add.99), channel_id=1, source_target_pairs={{0,64},{16,80},{32,96},{48,112},{64,0},{80,16},{96,32},{112,48},{1... | collective-permute-start | bytes 254024 | tf_op jit(solution)/shard_map/ppermute | solution.py:80
  124.8 4.9 %collective-permute-start.13 = (f32[49,432]{1,0:T(8,128)S(1)}, f32[49,432]{1,0:T(8,128)S(1)}, u32[]{:S(2)}, u32[]{:S(2)}) collective-permute-start(f32[49,432]{1,0:T(8,128)S(1)} %add.100), channel_id=1, source_target_pairs={{0,128},{16,144},{32,160},{48,176},{64,192},{80,208},{96,224},{112... | collective-permute-start | bytes 254024 | tf_op jit(solution)/shard_map/ppermute | solution.py:80

commit v3 on v2

--- a/solution.py
+++ b/solution.py
@@ -1,4 +1,5 @@
 import jax
+import numpy as np
 import jax.numpy as jnp
 from jax import lax
 from jax.sharding import PartitionSpec as P
@@ -32,11 +33,7 @@
     phases, depth, height, _, width = field.shape
     depth -= 2
     field = jnp.pad(field, ((0, 0), (0, 0), (1, 1), (0, 0), (0, 0)))
-    keys = sorted({((r + e - 1) % phases, (r + e - 1) // phases) for r in range(phases) for e in range(3)})
-    moved = [key for key in keys if key[1] != 0]
-    shifted = lax.optimization_barrier(tuple(lane_shift(field[key[0]], key[1]) for key in moved))
-    sources = {key: field[key[0]] for key in keys if key[1] == 0}
-    sources.update(zip(moved, shifted))
+    sources = {}
     out = []
     for r in range(phases):
         taps = []
@@ -44,6 +41,8 @@
             for b in range(3):
                 for e in range(3):
                     key = ((r + e - 1) % phases, (r + e - 1) // phases)
+                    if key not in sources:
+                        sources[key] = lane_shift(field[key[0]], key[1])
                     taps.append(sources[key][a : a + depth, b : b + height])
         out.append(jnp.concatenate(taps, axis=2))
     return jnp.stack(out, axis=0)
@@ -90,14 +89,53 @@
     return jnp.transpose(grad.reshape(grad.shape[0], 3, 3, 3, chan), (0, 4, 1, 2, 3))
 
 
+def phase_select(phases):
+    sel = np.zeros((phases, 3, phases, 3), np.float32)
+    for r in range(phases):
+        for e in range(3):
+            sel[r, (r + e - 1) // phases + 1, (r + e - 1) % phases, e] = 1.0
+    return sel
+
+
+def merged_patches(field):
+    depth, height = field.shape[0] - 2, field.shape[1]
+    field = jnp.pad(field, ((0, 0), (1, 1), (0, 0), (0, 0)))
+    shifted = [lane_shift(field, dm) for dm in (-1, 0, 1)]
+    taps = []
+    for a in range(3):
+        for b in range(3):
+            for dm in range(3):
+                taps.append(shifted[dm][a : a + depth, b : b + height])
+    return jnp.concatenate(taps, axis=2)
+
+
+def merged_kernel(kern, phases):
+    sel = phase_select(phases)
+    taps = jnp.transpose(kern.astype(jnp.float32), (0, 2, 3, 1, 4))
+    full = taps[:, None, :, :, None, None, :, :] * sel[None, :, None, None, :, :, None, :]
+    return full.sum(axis=-1).reshape(kern.shape[0], phases, -1).astype(kern.dtype)
+
+
+def merged_grad(grads, chan, phases):
+    sel = phase_select(phases)
+    full = grads.reshape(grads.shape[0], phases, 3, 3, 3, phases, chan)
+    summed = (full[..., None] * sel[None, :, None, None, :, :, None, :]).sum(axis=(1, 4, 5))
+    return jnp.transpose(summed, (0, 1, 2, 4, 3)).reshape(grads.shape[0], -1)
+
+
 def shards(volume, cotangent, w_first, b_first, w_second, b_second):
     sample = volume[0]
     cot = cotangent[0]
     chan0, _, height, width = sample.shape
     halo = with_halo(sample, "space", 1)
-    split = jnp.transpose(halo.reshape(chan0, halo.shape[1], height, width // 4, 4), (4, 1, 2, 0, 3))
-    patches_first = phase_patches(split)
-    pre_first = conv_taps(tap_major(w_first), patches_first) + b_first[:, None, None, None, None]
+    merged = jnp.transpose(halo.reshape(chan0, halo.shape[1], height, width // 4, 4), (1, 2, 4, 0, 3))
+    patches_first = merged_patches(merged.reshape(halo.shape[1], height, 4 * chan0, width // 4))
+    pre_first = (
+        jnp.einsum(
+            "ork,xykm->orxym", merged_kernel(w_first, 4), patches_first, preferred_element_type=jnp.float32
+        )
+        + b_first[:, None, None, None, None]
+    )
     pooled = pool(jax.nn.silu(pre_first)).astype(jnp.bfloat16)
     pooled_halo = jnp.transpose(with_halo(pooled, "space", 2), (1, 2, 3, 0, 4))
     patches_second = phase_patches(pooled_halo)
@@ -112,7 +150,11 @@
     flipped = tap_major(jnp.transpose(jnp.flip(w_second, (2, 3, 4)), (1, 0, 2, 3, 4)))
     back = conv_taps(flipped, phase_patches(grad_halo))
     grad_first = (upsample(back, 4) * 0.125 * silu_slope(pre_first)).astype(jnp.bfloat16)
-    grad_w1 = grad_taps(grad_first, patches_first)
+    grad_w1 = merged_grad(
+        jnp.einsum("orxym,xykm->ork", grad_first, patches_first, preferred_element_type=jnp.float32),
+        chan0,
+        4,
+    )
     grad_b1 = jnp.sum(grad_first.astype(jnp.float32), axis=(1, 2, 3, 4))
     chan1 = w_second.shape[1]
     lanes = grad_w2.shape[1]

time: 133 us -> 110 us (0.83)
  local copies, waits for them, and re-layouts: 42 us -> 16.1 us
  other arithmetic: 1.83 us -> 5.14 us
  starting transfers between devices: 45.6 us -> 43.2 us
  waiting for transfers between devices: 36.1 us -> 38.5 us
    concatenate x8 -> x4, local copies, waits for them, and re-layouts: 29.6 us -> 0.08 us  [phase_patches(): out.append(jnp.concatenate(taps, axis=2))]
    unnamed x116 -> x140, local copies, waits for them, and re-layouts: 4.82 us -> 9.24 us
    dot_general x0 -> x2, matrix products: none -> 2.88 us  [the longest x1 1.98 us: shards(): jnp.einsum('orxym,xykm->ork', grad_first, patches_first, preferred_elemen...]
    ppermute x3, starting transfers between devices: 16.1 us -> 13.3 us  [with_halo(): lax.ppermute(tail, axis, [(i, (i + 1) % count) for i in range(ends)])]
    reduce_sum x0 -> x2, other arithmetic: none -> 2.68 us  [the longest x1 1.92 us: merged_kernel(): full.sum(axis=-1).reshape(kern.shape[0], phases, -1).astype(kern.dtype)]
    ppermute x3, waiting for transfers between devices: 3.96 us -> 6.38 us  [with_halo(): lax.ppermute(head, axis, [((i + 1) % count, i) for i in range(ends)])]
    dot_general x3 -> x2, matrix products: 3.51 us -> 1.2 us  [conv_taps(): jnp.einsum('ok,rxykm->orxym', kern.reshape(kern.shape[0], -1), patches, p...]
  transfers between devices with their start and end apart: 14 -> 14, of which waited for: 10 -> 10; matrix products, arithmetic and copies ran while one was open for 4% -> 7% of each run, Pallas kernels for 0% -> 0%
where the time goes in v3:
time: 110 us; the launch traced here: 109 us
  starting transfers between devices  43.2 us (39%)
  waiting for transfers between devices  38.5 us (35%)
  local copies, waits for them, and re-layouts  16.1 us (15%)
  other arithmetic  5.14 us (5%)
  matrix products  4.65 us (4%)
  between operations  1.69 us (2%)
    ppermute x8, waiting for transfers between devices, butterfly_sum(): lax.ppermute(rows, axis, [(i, i ^ step) for i in range(count)])  32.1 us
    ppermute x8, starting transfers between devices, butterfly_sum(): lax.ppermute(rows, axis, [(i, i ^ step) for i in range(count)])  22 us
    ppermute x3, starting transfers between devices, with_halo(): lax.ppermute(tail, axis, [(i, (i + 1) % count) for i in range(ends)])  13.3 us
    unnamed x140, local copies, waits for them, and re-layouts  9.24 us
    ppermute x3, starting transfers between devices, with_halo(): lax.ppermute(head, axis, [((i + 1) % count, i) for i in range(ends)])  7.93 us
    ppermute x3, waiting for transfers between devices, with_halo(): lax.ppermute(head, axis, [((i + 1) % count, i) for i in range(ends)])  6.38 us
  transfers between devices with their start and end apart: 14, of which 10 were waited for; matrix products, arithmetic and copies ran while one was open for 7% of the time, Pallas kernels for 0%

profile of v3, /device:TPU:24, one launch (start us, length us, event | category | flops | bytes accessed | tf_op | source)
XLA Modules:
  0.0 109.4 jit_solution(17883250754315623419)
XLA Ops:
  0.6 0.8 fusion.35
  1.4 1.9 %collective-permute-start = (bf16[4,1,8,512]{3,2,1,0:T(8,128)(2,1)S(1)}, bf16[4,1,8,512]{3,2,1,0:T(8,128)(2,1)S(1)}, u32[]{:S(2)}, u32[]{:S(2)}) collective-permute-start(bf16[4,1,8,512]{3,2,1,0:T(8,128)(2,1)S(1)} %get-tuple-element.35), channel_id=1, source_target_pairs={{0,1},{1,2},{2,3},{3,4},{4,5},{5,6},{6,7},{7,8},{8,9},{9,10},{10,1... | collective-permute-start | bytes 98312 | tf_op jit(solution)/shard_map/ppermute | solution.py:15
  3.3 3.6 %collective-permute-start.1 = (bf16[4,1,8,512]{3,2,1,0:T(8,128)(2,1)S(1)}, bf16[4,1,8,512]{3,2,1,0:T(8,128)(2,1)S(1)}, u32[]{:S(2)}, u32[]{:S(2)}) collective-permute-start(bf16[4,1,8,512]{3,2,1,0:T(8,128)(2,1)S(1)} %get-tuple-element.36), channel_id=1, source_target_pairs={{1,0},{2,1},{3,2},{4,3},{5,4},{6,5},{7,6},{8,7},{9,8},{10,9},{11,1... | collective-permute-start | bytes 98312 | tf_op jit(solution)/shard_map/ppermute | solution.py:17
  7.0 0.8 convert_bitcast_fusion
  7.7 0.7 multiply_bitcast_fusion
  8.5 1.9 %multiply_reduce_fusion.1 = bf16[16,4,3,3,3,4,4]{0,6,5,4,3,2,1:T(4,128)(2,1)S(1)} fusion(f32[4,3,4,3]{3,2,1,0:T(4,128)} %constant.48, f32[16,3,3,4,3]{0,3,4,2,1:T(4,128)S(1)} %convert_bitcast_fusion), kind=kLoop, calls=%fused_computation.9 | loop fusion | flops 138240 | bytes 62784 | tf_op jit(solution)/shard_map/reduce_sum | solution.py:116
  10.4 1.8 %copy.85 = bf16[1,4,4,8,512]{3,4,2,1,0:T(8,128)(2,1)S(1)} copy(bf16[1,4,4,8,512]{4,3,2,1,0:T(8,128)(2,1)} %param.8) | data formatting | bytes 262144 | tf_op args[0]
  12.2 0.9 copy.88
  16.8 0.9 fusion.20
  17.7 0.8 copy-done.2
  18.7 3.2 %collective-permute-start.2 = (bf16[16,2,1,4,128]{4,0,3,2,1:T(8,128)(2,1)S(1)}, bf16[16,2,1,4,128]{4,0,3,2,1:T(8,128)(2,1)S(1)}, u32[]{:S(2)}, u32[]{:S(2)}) collective-permute-start(bf16[16,2,1,4,128]{4,0,3,2,1:T(8,128)(2,1)S(1)} %get-tuple-element.41), channel_id=1, source_target_pairs={{0,1},{1,2},{2,3},{3,4},{4,5},{5,6},{6,7},{7,8},{8,9},{9,10},{10,1... | collective-permute-start | bytes 98312 | tf_op jit(solution)/shard_map/ppermute | solution.py:15
  21.9 2.4 %collective-permute-start.3 = (bf16[16,2,1,4,128]{4,0,3,2,1:T(8,128)(2,1)S(1)}, bf16[16,2,1,4,128]{4,0,3,2,1:T(8,128)(2,1)S(1)}, u32[]{:S(2)}, u32[]{:S(2)}) collective-permute-start(bf16[16,2,1,4,128]{4,0,3,2,1:T(8,128)(2,1)S(1)} %get-tuple-element.42), channel_id=1, source_target_pairs={{1,0},{2,1},{3,2},{4,3},{5,4},{6,5},{7,6},{8,7},{9,8},{10,9},{11,1... | collective-permute-start | bytes 98312 | tf_op jit(solution)/shard_map/ppermute | solution.py:17
  24.5 5.1 %collective-permute-done.3 = bf16[16,2,1,4,128]{4,0,3,2,1:T(8,128)(2,1)S(1)} collective-permute-done((bf16[16,2,1,4,128]{4,0,3,2,1:T(8,128)(2,1)S(1)}, bf16[16,2,1,4,128]{4,0,3,2,1:T(8,128)(2,1)S(1)}, u32[]{:S(2)}, u32[]{:S(2)}) %collective-permute-start.3) | collective-permute-done | bytes 32800 | tf_op jit(solution)/shard_map/ppermute | solution.py:17
  32.0 8.2 %collective-permute-start.4 = (bf16[32,2,1,4,128]{4,0,3,2,1:T(8,128)(2,1)S(1)}, bf16[32,2,1,4,128]{4,0,3,2,1:T(8,128)(2,1)S(1)}, u32[]{:S(2)}, u32[]{:S(2)}) collective-permute-start(bf16[32,2,1,4,128]{4,0,3,2,1:T(8,128)(2,1)S(1)} %get-tuple-element.31), channel_id=1, source_target_pairs={{0,1},{1,2},{2,3},{3,4},{4,5},{5,6},{6,7},{7,8},{8,9},{9,10},{10,1... | collective-permute-start | bytes 196616 | tf_op jit(solution)/shard_map/ppermute | solution.py:15
  40.1 1.9 %collective-permute-start.5 = (bf16[32,2,1,4,128]{4,0,3,2,1:T(8,128)(2,1)S(1)}, bf16[32,2,1,4,128]{4,0,3,2,1:T(8,128)(2,1)S(1)}, u32[]{:S(2)}, u32[]{:S(2)}) collective-permute-start(bf16[32,2,1,4,128]{4,0,3,2,1:T(8,128)(2,1)S(1)} %get-tuple-element.32), channel_id=1, source_target_pairs={{1,0},{2,1},{3,2},{4,3},{5,4},{6,5},{7,6},{8,7},{9,8},{10,9},{11,1... | collective-permute-start | bytes 196616 | tf_op jit(solution)/shard_map/ppermute | solution.py:17
  42.7 1.3 %collective-permute-done.5 = bf16[32,2,1,4,128]{4,0,3,2,1:T(8,128)(2,1)S(1)} collective-permute-done((bf16[32,2,1,4,128]{4,0,3,2,1:T(8,128)(2,1)S(1)}, bf16[32,2,1,4,128]{4,0,3,2,1:T(8,128)(2,1)S(1)}, u32[]{:S(2)}, u32[]{:S(2)}) %collective-permute-start.5) | collective-permute-done | bytes 65568 | tf_op jit(solution)/shard_map/ppermute | solution.py:17
  47.4 1.4 %copy-done.3 = bf16[4,8,432,128]{3,2,1,0:T(8,128)(2,1)S(1)} copy-done((bf16[4,8,432,128]{3,2,1,0:T(8,128)(2,1)S(1)}, bf16[4,8,432,128]{3,2,1,0:T(8,128)(2,1)}, u32[]{:S(2)}) %copy-start.3) | copy-done | bytes 3538968
  48.7 2.0 %fusion.4 = f32[16,4,432,1,1]{0,2,4,3,1:T(8,128)S(1)} fusion(bf16[16,4,4,8,128]{4,0,3,2,1:T(8,128)(2,1)S(1)} %get-tuple-element.16, bf16[4,8,432,128]{3,2,1,0:T(8,128)(2,1)S(1)} %copy-done.3), kind=kOutput, calls=%fused_computation.4 | convolution fusion | flops 226492416 | bytes 4173824 | tf_op jit(solution)/shard_map/orxym,xykm->ork/dot_general | solution.py:154
  50.7 0.8 multiply_reduce_fusion
  51.7 5.7 %collective-permute-start.6 = (f32[49,432]{1,0:T(8,128)S(1)}, f32[49,432]{1,0:T(8,128)S(1)}, u32[]{:S(2)}, u32[]{:S(2)}) collective-permute-start(f32[49,432]{1,0:T(8,128)S(1)} %fusion.23), channel_id=1, source_target_pairs={{0,1},{1,0},{2,3},{3,2},{4,5},{5,4},{6,7},{7,6},{8,9},{9,8},{10,11... | collective-permute-start | bytes 254024 | tf_op jit(solution)/shard_map/ppermute | solution.py:79
  57.3 1.0 collective-permute-done.6
  58.4 5.4 %collective-permute-done.7 = f32[49,432]{1,0:T(8,128)S(1)} collective-permute-done((f32[49,432]{1,0:T(8,128)S(1)}, f32[49,432]{1,0:T(8,128)S(1)}, u32[]{:S(2)}, u32[]{:S(2)}) %collective-permute-start.7) | collective-permute-done | bytes 84704 | tf_op jit(solution)/shard_map/ppermute | solution.py:79
  64.0 6.3 %collective-permute-done.8 = f32[49,432]{1,0:T(8,128)S(1)} collective-permute-done((f32[49,432]{1,0:T(8,128)S(1)}, f32[49,432]{1,0:T(8,128)S(1)}, u32[]{:S(2)}, u32[]{:S(2)}) %collective-permute-start.8) | collective-permute-done | bytes 84704 | tf_op jit(solution)/shard_map/ppermute | solution.py:79
  70.4 6.3 %collective-permute-done.9 = f32[49,432]{1,0:T(8,128)S(1)} collective-permute-done((f32[49,432]{1,0:T(8,128)S(1)}, f32[49,432]{1,0:T(8,128)S(1)}, u32[]{:S(2)}, u32[]{:S(2)}) %collective-permute-start.9) | collective-permute-done | bytes 84704 | tf_op jit(solution)/shard_map/ppermute | solution.py:79
  76.7 2.0 %collective-permute-start.10 = (f32[49,432]{1,0:T(8,128)S(1)}, f32[49,432]{1,0:T(8,128)S(1)}, u32[]{:S(2)}, u32[]{:S(2)}) collective-permute-start(f32[49,432]{1,0:T(8,128)S(1)} %add.93), channel_id=1, source_target_pairs={{0,16},{16,0},{32,48},{48,32},{64,80},{80,64},{96,112},{112,96},{1... | collective-permute-start | bytes 254024 | tf_op jit(solution)/shard_map/ppermute | solution.py:79
  78.7 2.9 %collective-permute-done.10 = f32[49,432]{1,0:T(8,128)S(1)} collective-permute-done((f32[49,432]{1,0:T(8,128)S(1)}, f32[49,432]{1,0:T(8,128)S(1)}, u32[]{:S(2)}, u32[]{:S(2)}) %collective-permute-start.10) | collective-permute-done | bytes 84704 | tf_op jit(solution)/shard_map/ppermute | solution.py:79
  81.6 4.4 %collective-permute-start.11 = (f32[49,432]{1,0:T(8,128)S(1)}, f32[49,432]{1,0:T(8,128)S(1)}, u32[]{:S(2)}, u32[]{:S(2)}) collective-permute-start(f32[49,432]{1,0:T(8,128)S(1)} %add.94), channel_id=1, source_target_pairs={{0,32},{16,48},{32,0},{48,16},{64,96},{80,112},{96,64},{112,80},{1... | collective-permute-start | bytes 254024 | tf_op jit(solution)/shard_map/ppermute | solution.py:79
  85.9 4.0 %collective-permute-done.11 = f32[49,432]{1,0:T(8,128)S(1)} collective-permute-done((f32[49,432]{1,0:T(8,128)S(1)}, f32[49,432]{1,0:T(8,128)S(1)}, u32[]{:S(2)}, u32[]{:S(2)}) %collective-permute-start.11) | collective-permute-done | bytes 84704 | tf_op jit(solution)/shard_map/ppermute | solution.py:79
  90.0 9.0 %collective-permute-start.12 = (f32[49,432]{1,0:T(8,128)S(1)}, f32[49,432]{1,0:T(8,128)S(1)}, u32[]{:S(2)}, u32[]{:S(2)}) collective-permute-start(f32[49,432]{1,0:T(8,128)S(1)} %add.95), channel_id=1, source_target_pairs={{0,64},{16,80},{32,96},{48,112},{64,0},{80,16},{96,32},{112,48},{1... | collective-permute-start | bytes 254024 | tf_op jit(solution)/shard_map/ppermute | solution.py:79
  99.0 2.8 %collective-permute-done.12 = f32[49,432]{1,0:T(8,128)S(1)} collective-permute-done((f32[49,432]{1,0:T(8,128)S(1)}, f32[49,432]{1,0:T(8,128)S(1)}, u32[]{:S(2)}, u32[]{:S(2)}) %collective-permute-start.12) | collective-permute-done | bytes 84704 | tf_op jit(solution)/shard_map/ppermute | solution.py:79
  103.1 3.6 %collective-permute-done.13 = f32[49,432]{1,0:T(8,128)S(1)} collective-permute-done((f32[49,432]{1,0:T(8,128)S(1)}, f32[49,432]{1,0:T(8,128)S(1)}, u32[]{:S(2)}, u32[]{:S(2)}) %collective-permute-start.13) | collective-permute-done | bytes 84704 | tf_op jit(solution)/shard_map/ppermute | solution.py:79
  107.8 0.8 copy.102
  (203 shorter events, 13.3 us)
Async XLA Ops:
  1.4 11.7 %collective-permute-start = (bf16[4,1,8,512]{3,2,1,0:T(8,128)(2,1)S(1)}, bf16[4,1,8,512]{3,2,1,0:T(8,128)(2,1)S(1)}, u32[]{:S(2)}, u32[]{:S(2)}) collective-permute-start(bf16[4,1,8,512]{3,2,1,0:T(8,128)(2,1)S(1)} %get-tuple-element.35), channel_id=1, source_target_pairs={{0,1},{1,2},{2,3},{3,4},{4,5},{5,6},{6,7},{7,8},{8,9},{9,10},{10,1... | collective-permute-start | bytes 98312 | tf_op jit(solution)/shard_map/ppermute | solution.py:15
  3.3 10.3 %collective-permute-start.1 = (bf16[4,1,8,512]{3,2,1,0:T(8,128)(2,1)S(1)}, bf16[4,1,8,512]{3,2,1,0:T(8,128)(2,1)S(1)}, u32[]{:S(2)}, u32[]{:S(2)}) collective-permute-start(bf16[4,1,8,512]{3,2,1,0:T(8,128)(2,1)S(1)} %get-tuple-element.36), channel_id=1, source_target_pairs={{1,0},{2,1},{3,2},{4,3},{5,4},{6,5},{7,6},{8,7},{9,8},{10,9},{11,1... | collective-permute-start | bytes 98312 | tf_op jit(solution)/shard_map/ppermute | solution.py:17
  16.0 0.8 copy-start.4
  16.8 1.8 %copy-start.2 = (bf16[4,8,432,128]{3,2,1,0:T(8,128)(2,1)}, bf16[4,8,432,128]{3,2,1,0:T(8,128)(2,1)S(1)}, u32[]{:S(2)}) copy-start(bf16[4,8,432,128]{3,2,1,0:T(8,128)(2,1)S(1)} %constant_dynamic-update-slice_fusion) | copy-start | bytes 10616836
  16.8 7.4 %copy-start = (bf16[32,16,3,3,3]{0,1,4,3,2:T(8,128)(2,1)S(1)}, bf16[32,16,3,3,3]{0,1,4,3,2:T(8,128)(2,1)}, u32[]{:S(2)}) copy-start(bf16[32,16,3,3,3]{0,1,4,3,2:T(8,128)(2,1)} %param.12) | copy-start | bytes 82948
  18.7 5.8 %collective-permute-start.2 = (bf16[16,2,1,4,128]{4,0,3,2,1:T(8,128)(2,1)S(1)}, bf16[16,2,1,4,128]{4,0,3,2,1:T(8,128)(2,1)S(1)}, u32[]{:S(2)}, u32[]{:S(2)}) collective-permute-start(bf16[16,2,1,4,128]{4,0,3,2,1:T(8,128)(2,1)S(1)} %get-tuple-element.41), channel_id=1, source_target_pairs={{0,1},{1,2},{2,3},{3,4},{4,5},{5,6},{6,7},{7,8},{8,9},{9,10},{10,1... | collective-permute-start | bytes 98312 | tf_op jit(solution)/shard_map/ppermute | solution.py:15
  21.9 7.7 %collective-permute-start.3 = (bf16[16,2,1,4,128]{4,0,3,2,1:T(8,128)(2,1)S(1)}, bf16[16,2,1,4,128]{4,0,3,2,1:T(8,128)(2,1)S(1)}, u32[]{:S(2)}, u32[]{:S(2)}) collective-permute-start(bf16[16,2,1,4,128]{4,0,3,2,1:T(8,128)(2,1)S(1)} %get-tuple-element.42), channel_id=1, source_target_pairs={{1,0},{2,1},{3,2},{4,3},{5,4},{6,5},{7,6},{8,7},{9,8},{10,9},{11,1... | collective-permute-start | bytes 98312 | tf_op jit(solution)/shard_map/ppermute | solution.py:17
  30.4 1.0 copy-start.5
  32.0 10.7 %collective-permute-start.4 = (bf16[32,2,1,4,128]{4,0,3,2,1:T(8,128)(2,1)S(1)}, bf16[32,2,1,4,128]{4,0,3,2,1:T(8,128)(2,1)S(1)}, u32[]{:S(2)}, u32[]{:S(2)}) collective-permute-start(bf16[32,2,1,4,128]{4,0,3,2,1:T(8,128)(2,1)S(1)} %get-tuple-element.31), channel_id=1, source_target_pairs={{0,1},{1,2},{2,3},{3,4},{4,5},{5,6},{6,7},{7,8},{8,9},{9,10},{10,1... | collective-permute-start | bytes 196616 | tf_op jit(solution)/shard_map/ppermute | solution.py:15
  40.1 3.8 %collective-permute-start.5 = (bf16[32,2,1,4,128]{4,0,3,2,1:T(8,128)(2,1)S(1)}, bf16[32,2,1,4,128]{4,0,3,2,1:T(8,128)(2,1)S(1)}, u32[]{:S(2)}, u32[]{:S(2)}) collective-permute-start(bf16[32,2,1,4,128]{4,0,3,2,1:T(8,128)(2,1)S(1)} %get-tuple-element.32), channel_id=1, source_target_pairs={{1,0},{2,1},{3,2},{4,3},{5,4},{6,5},{7,6},{8,7},{9,8},{10,9},{11,1... | collective-permute-start | bytes 196616 | tf_op jit(solution)/shard_map/ppermute | solution.py:17
  46.7 2.0 %copy-start.3 = (bf16[4,8,432,128]{3,2,1,0:T(8,128)(2,1)S(1)}, bf16[4,8,432,128]{3,2,1,0:T(8,128)(2,1)}, u32[]{:S(2)}) copy-start(bf16[4,8,432,128]{3,2,1,0:T(8,128)(2,1)} %copy-done.2) | copy-start | bytes 10616836
  48.7 2.0 %copy-start.1 = (f32[4,3,4,3]{3,2,1,0:T(4,128)S(1)}, f32[4,3,4,3]{3,2,1,0:T(4,128)}, u32[]{:S(2)}) copy-start(f32[4,3,4,3]{3,2,1,0:T(4,128)} %constant.48) | copy-start | bytes 1732
  51.7 6.6 %collective-permute-start.6 = (f32[49,432]{1,0:T(8,128)S(1)}, f32[49,432]{1,0:T(8,128)S(1)}, u32[]{:S(2)}, u32[]{:S(2)}) collective-permute-start(f32[49,432]{1,0:T(8,128)S(1)} %fusion.23), channel_id=1, source_target_pairs={{0,1},{1,0},{2,3},{3,2},{4,5},{5,4},{6,7},{7,6},{8,9},{9,8},{10,11... | collective-permute-start | bytes 254024 | tf_op jit(solution)/shard_map/ppermute | solution.py:79
  58.3 5.5 %collective-permute-start.7 = (f32[49,432]{1,0:T(8,128)S(1)}, f32[49,432]{1,0:T(8,128)S(1)}, u32[]{:S(2)}, u32[]{:S(2)}) collective-permute-start(f32[49,432]{1,0:T(8,128)S(1)} %fusion.32), channel_id=1, source_target_pairs={{0,2},{1,3},{2,0},{3,1},{4,6},{5,7},{6,4},{7,5},{8,10},{9,11},{10,... | collective-permute-start | bytes 254024 | tf_op jit(solution)/shard_map/ppermute | solution.py:79
  63.9 6.4 %collective-permute-start.8 = (f32[49,432]{1,0:T(8,128)S(1)}, f32[49,432]{1,0:T(8,128)S(1)}, u32[]{:S(2)}, u32[]{:S(2)}) collective-permute-start(f32[49,432]{1,0:T(8,128)S(1)} %add.91), channel_id=1, source_target_pairs={{0,4},{1,5},{2,6},{3,7},{4,0},{5,1},{6,2},{7,3},{8,12},{9,13},{10,... | collective-permute-start | bytes 254024 | tf_op jit(solution)/shard_map/ppermute | solution.py:79
  70.3 6.4 %collective-permute-start.9 = (f32[49,432]{1,0:T(8,128)S(1)}, f32[49,432]{1,0:T(8,128)S(1)}, u32[]{:S(2)}, u32[]{:S(2)}) collective-permute-start(f32[49,432]{1,0:T(8,128)S(1)} %add.92), channel_id=1, source_target_pairs={{0,8},{1,9},{2,10},{3,11},{4,12},{5,13},{6,14},{7,15},{8,0},{9,1},... | collective-permute-start | bytes 254024 | tf_op jit(solution)/shard_map/ppermute | solution.py:79
  76.7 4.9 %collective-permute-start.10 = (f32[49,432]{1,0:T(8,128)S(1)}, f32[49,432]{1,0:T(8,128)S(1)}, u32[]{:S(2)}, u32[]{:S(2)}) collective-permute-start(f32[49,432]{1,0:T(8,128)S(1)} %add.93), channel_id=1, source_target_pairs={{0,16},{16,0},{32,48},{48,32},{64,80},{80,64},{96,112},{112,96},{1... | collective-permute-start | bytes 254024 | tf_op jit(solution)/shard_map/ppermute | solution.py:79
  81.6 8.4 %collective-permute-start.11 = (f32[49,432]{1,0:T(8,128)S(1)}, f32[49,432]{1,0:T(8,128)S(1)}, u32[]{:S(2)}, u32[]{:S(2)}) collective-permute-start(f32[49,432]{1,0:T(8,128)S(1)} %add.94), channel_id=1, source_target_pairs={{0,32},{16,48},{32,0},{48,16},{64,96},{80,112},{96,64},{112,80},{1... | collective-permute-start | bytes 254024 | tf_op jit(solution)/shard_map/ppermute | solution.py:79
  90.0 11.8 %collective-permute-start.12 = (f32[49,432]{1,0:T(8,128)S(1)}, f32[49,432]{1,0:T(8,128)S(1)}, u32[]{:S(2)}, u32[]{:S(2)}) collective-permute-start(f32[49,432]{1,0:T(8,128)S(1)} %add.95), channel_id=1, source_target_pairs={{0,64},{16,80},{32,96},{48,112},{64,0},{80,16},{96,32},{112,48},{1... | collective-permute-start | bytes 254024 | tf_op jit(solution)/shard_map/ppermute | solution.py:79
  101.8 4.9 %collective-permute-start.13 = (f32[49,432]{1,0:T(8,128)S(1)}, f32[49,432]{1,0:T(8,128)S(1)}, u32[]{:S(2)}, u32[]{:S(2)}) collective-permute-start(f32[49,432]{1,0:T(8,128)S(1)} %add.96), channel_id=1, source_target_pairs={{0,128},{16,144},{32,160},{48,176},{64,192},{80,208},{96,224},{112... | collective-permute-start | bytes 254024 | tf_op jit(solution)/shard_map/ppermute | solution.py:79

commit v4 on v3

--- a/solution.py
+++ b/solution.py
@@ -157,20 +157,23 @@
     )
     grad_b1 = jnp.sum(grad_first.astype(jnp.float32), axis=(1, 2, 3, 4))
     chan1 = w_second.shape[1]
-    lanes = grad_w2.shape[1]
-    biases = jnp.concatenate([grad_b1, grad_b2])
-    rows = jnp.concatenate(
+    rows_w2, lanes_w2 = grad_w2.shape
+    side = grad_w1.reshape(rows_w2, -1)
+    lanes_w1 = side.shape[1]
+    packed = jnp.concatenate(
         [
             grad_w2,
-            jnp.pad(grad_w1, ((0, 0), (0, lanes - grad_w1.shape[1]))),
-            jnp.pad(biases, (0, lanes - biases.shape[0]))[None],
-        ]
+            side,
+            grad_b2[:, None],
+            jnp.pad(grad_b1, (0, rows_w2 - grad_b1.shape[0]))[:, None],
+        ],
+        axis=1,
     )
-    totals = butterfly_sum(rows, ("space", "dp"))
-    out_w2 = tap_minor(totals[: grad_w2.shape[0]], chan1)
-    out_w1 = tap_minor(totals[grad_w2.shape[0] : -1, : grad_w1.shape[1]], chan0)
-    out_b1 = totals[-1, : grad_b1.shape[0]]
-    out_b2 = totals[-1, grad_b1.shape[0] : biases.shape[0]]
+    totals = butterfly_sum(packed, ("space", "dp"))
+    out_w2 = tap_minor(totals[:, :lanes_w2], chan1)
+    out_w1 = tap_minor(totals[:, lanes_w2 : lanes_w2 + lanes_w1].reshape(grad_w1.shape), chan0)
+    out_b2 = totals[:, lanes_w2 + lanes_w1]
+    out_b1 = totals[: grad_b1.shape[0], lanes_w2 + lanes_w1 + 1]
     return (output[None], out_w1, out_b1, out_w2, out_b2)
 
 

time: 110 us -> 104 us (0.945)
  waiting for transfers between devices: 38.5 us -> 32.9 us
  starting transfers between devices: 43.2 us -> 41.5 us
  local copies, waits for them, and re-layouts: 16.1 us -> 17.3 us
    ppermute x8, waiting for transfers between devices: 32.1 us -> 26.6 us  [butterfly_sum(): lax.ppermute(rows, axis, [(i, i ^ step) for i in range(count)])]
    ppermute x8, starting transfers between devices: 22 us -> 20.3 us  [butterfly_sum(): lax.ppermute(rows, axis, [(i, i ^ step) for i in range(count)])]
    slice x4, local copies, waits for them, and re-layouts: 0.93 us -> 2.28 us  [the longest x1 0.82 us: shards(): out_w2 = tap_minor(totals[:, :lanes_w2], chan1)]
    unnamed x140 -> x141, local copies, waits for them, and re-layouts: 9.24 us -> 10.1 us
  transfers between devices with their start and end apart: 14 -> 14, of which waited for: 10 -> 10; matrix products, arithmetic and copies ran while one was open for 7% -> 8% of each run, Pallas kernels for 0% -> 0%
where the time goes in v4:
time: 104 us; the launch traced here: 103 us
  starting transfers between devices  41.5 us (40%)
  waiting for transfers between devices  32.9 us (32%)
  local copies, waits for them, and re-layouts  17.3 us (17%)
  other arithmetic  5.15 us (5%)
  matrix products  4.65 us (4%)
  between operations  1.67 us (2%)
    ppermute x8, waiting for transfers between devices, butterfly_sum(): lax.ppermute(rows, axis, [(i, i ^ step) for i in range(count)])  26.6 us
    ppermute x8, starting transfers between devices, butterfly_sum(): lax.ppermute(rows, axis, [(i, i ^ step) for i in range(count)])  20.3 us
    ppermute x3, starting transfers between devices, with_halo(): lax.ppermute(tail, axis, [(i, (i + 1) % count) for i in range(ends)])  13.3 us
    unnamed x141, local copies, waits for them, and re-layouts  10.1 us
    ppermute x3, starting transfers between devices, with_halo(): lax.ppermute(head, axis, [((i + 1) % count, i) for i in range(ends)])  7.93 us
    ppermute x3, waiting for transfers between devices, with_halo(): lax.ppermute(head, axis, [((i + 1) % count, i) for i in range(ends)])  6.3 us
  transfers between devices with their start and end apart: 14, of which 10 were waited for; matrix products, arithmetic and copies ran while one was open for 8% of the time, Pallas kernels for 0%

profile of v4, /device:TPU:24, one launch (start us, length us, event | category | flops | bytes accessed | tf_op | source)
XLA Modules:
  0.0 103.2 jit_solution(8235155164691428696)
XLA Ops:
  0.6 0.8 fusion.32
  1.4 1.9 %collective-permute-start = (bf16[4,1,8,512]{3,2,1,0:T(8,128)(2,1)S(1)}, bf16[4,1,8,512]{3,2,1,0:T(8,128)(2,1)S(1)}, u32[]{:S(2)}, u32[]{:S(2)}) collective-permute-start(bf16[4,1,8,512]{3,2,1,0:T(8,128)(2,1)S(1)} %get-tuple-element.45), channel_id=1, source_target_pairs={{0,1},{1,2},{2,3},{3,4},{4,5},{5,6},{6,7},{7,8},{8,9},{9,10},{10,1... | collective-permute-start | bytes 98312 | tf_op jit(solution)/shard_map/ppermute | solution.py:15
  3.3 3.6 %collective-permute-start.1 = (bf16[4,1,8,512]{3,2,1,0:T(8,128)(2,1)S(1)}, bf16[4,1,8,512]{3,2,1,0:T(8,128)(2,1)S(1)}, u32[]{:S(2)}, u32[]{:S(2)}) collective-permute-start(bf16[4,1,8,512]{3,2,1,0:T(8,128)(2,1)S(1)} %get-tuple-element.46), channel_id=1, source_target_pairs={{1,0},{2,1},{3,2},{4,3},{5,4},{6,5},{7,6},{8,7},{9,8},{10,9},{11,1... | collective-permute-start | bytes 98312 | tf_op jit(solution)/shard_map/ppermute | solution.py:17
  7.0 0.8 convert_bitcast_fusion
  8.5 1.9 %multiply_reduce_fusion.1 = bf16[16,4,3,3,3,4,4]{0,6,5,4,3,2,1:T(4,128)(2,1)S(1)} fusion(f32[4,3,4,3]{3,2,1,0:T(4,128)} %constant.46, f32[16,3,3,4,3]{0,3,4,2,1:T(4,128)S(1)} %convert_bitcast_fusion), kind=kLoop, calls=%fused_computation.9 | loop fusion | flops 138240 | bytes 62784 | tf_op jit(solution)/shard_map/reduce_sum | solution.py:116
  10.4 1.8 %copy.90 = bf16[1,4,4,8,512]{3,4,2,1,0:T(8,128)(2,1)S(1)} copy(bf16[1,4,4,8,512]{4,3,2,1,0:T(8,128)(2,1)} %param.8) | data formatting | bytes 262144 | tf_op args[0]
  12.2 0.9 copy.93
  16.8 0.9 fusion.20
  17.7 0.8 copy-done.2
  18.7 3.2 %collective-permute-start.2 = (bf16[16,2,1,4,128]{4,0,3,2,1:T(8,128)(2,1)S(1)}, bf16[16,2,1,4,128]{4,0,3,2,1:T(8,128)(2,1)S(1)}, u32[]{:S(2)}, u32[]{:S(2)}) collective-permute-start(bf16[16,2,1,4,128]{4,0,3,2,1:T(8,128)(2,1)S(1)} %get-tuple-element.51), channel_id=1, source_target_pairs={{0,1},{1,2},{2,3},{3,4},{4,5},{5,6},{6,7},{7,8},{8,9},{9,10},{10,1... | collective-permute-start | bytes 98312 | tf_op jit(solution)/shard_map/ppermute | solution.py:15
  21.9 2.4 %collective-permute-start.3 = (bf16[16,2,1,4,128]{4,0,3,2,1:T(8,128)(2,1)S(1)}, bf16[16,2,1,4,128]{4,0,3,2,1:T(8,128)(2,1)S(1)}, u32[]{:S(2)}, u32[]{:S(2)}) collective-permute-start(bf16[16,2,1,4,128]{4,0,3,2,1:T(8,128)(2,1)S(1)} %get-tuple-element.52), channel_id=1, source_target_pairs={{1,0},{2,1},{3,2},{4,3},{5,4},{6,5},{7,6},{8,7},{9,8},{10,9},{11,1... | collective-permute-start | bytes 98312 | tf_op jit(solution)/shard_map/ppermute | solution.py:17
  24.5 5.1 %collective-permute-done.3 = bf16[16,2,1,4,128]{4,0,3,2,1:T(8,128)(2,1)S(1)} collective-permute-done((bf16[16,2,1,4,128]{4,0,3,2,1:T(8,128)(2,1)S(1)}, bf16[16,2,1,4,128]{4,0,3,2,1:T(8,128)(2,1)S(1)}, u32[]{:S(2)}, u32[]{:S(2)}) %collective-permute-start.3) | collective-permute-done | bytes 32800 | tf_op jit(solution)/shard_map/ppermute | solution.py:17
  32.0 8.2 %collective-permute-start.4 = (bf16[32,2,1,4,128]{4,0,3,2,1:T(8,128)(2,1)S(1)}, bf16[32,2,1,4,128]{4,0,3,2,1:T(8,128)(2,1)S(1)}, u32[]{:S(2)}, u32[]{:S(2)}) collective-permute-start(bf16[32,2,1,4,128]{4,0,3,2,1:T(8,128)(2,1)S(1)} %get-tuple-element.41), channel_id=1, source_target_pairs={{0,1},{1,2},{2,3},{3,4},{4,5},{5,6},{6,7},{7,8},{8,9},{9,10},{10,1... | collective-permute-start | bytes 196616 | tf_op jit(solution)/shard_map/ppermute | solution.py:15
  40.1 1.9 %collective-permute-start.5 = (bf16[32,2,1,4,128]{4,0,3,2,1:T(8,128)(2,1)S(1)}, bf16[32,2,1,4,128]{4,0,3,2,1:T(8,128)(2,1)S(1)}, u32[]{:S(2)}, u32[]{:S(2)}) collective-permute-start(bf16[32,2,1,4,128]{4,0,3,2,1:T(8,128)(2,1)S(1)} %get-tuple-element.42), channel_id=1, source_target_pairs={{1,0},{2,1},{3,2},{4,3},{5,4},{6,5},{7,6},{8,7},{9,8},{10,9},{11,1... | collective-permute-start | bytes 196616 | tf_op jit(solution)/shard_map/ppermute | solution.py:17
  42.8 1.2 %collective-permute-done.5 = bf16[32,2,1,4,128]{4,0,3,2,1:T(8,128)(2,1)S(1)} collective-permute-done((bf16[32,2,1,4,128]{4,0,3,2,1:T(8,128)(2,1)S(1)}, bf16[32,2,1,4,128]{4,0,3,2,1:T(8,128)(2,1)S(1)}, u32[]{:S(2)}, u32[]{:S(2)}) %collective-permute-start.5) | collective-permute-done | bytes 65568 | tf_op jit(solution)/shard_map/ppermute | solution.py:17
  47.4 1.4 %copy-done.3 = bf16[4,8,432,128]{3,2,1,0:T(8,128)(2,1)S(1)} copy-done((bf16[4,8,432,128]{3,2,1,0:T(8,128)(2,1)S(1)}, bf16[4,8,432,128]{3,2,1,0:T(8,128)(2,1)}, u32[]{:S(2)}) %copy-start.3) | copy-done | bytes 3538968
  48.7 2.0 %fusion.4 = f32[16,4,432,1,1]{0,2,4,3,1:T(8,128)S(1)} fusion(bf16[16,4,4,8,128]{4,0,3,2,1:T(8,128)(2,1)S(1)} %get-tuple-element.28, bf16[4,8,432,128]{3,2,1,0:T(8,128)(2,1)S(1)} %copy-done.3), kind=kOutput, calls=%fused_computation.4 | convolution fusion | flops 226492416 | bytes 4173824 | tf_op jit(solution)/shard_map/orxym,xykm->ork/dot_general | solution.py:154
  50.7 0.8 multiply_reduce_fusion
  52.1 5.6 %collective-permute-start.6 = (f32[32,488]{1,0:T(8,128)S(1)}, f32[32,488]{1,0:T(8,128)S(1)}, u32[]{:S(2)}, u32[]{:S(2)}) collective-permute-start(f32[32,488]{1,0:T(8,128)S(1)} %pad_maximum_fusion.5), channel_id=1, source_target_pairs={{0,1},{1,0},{2,3},{3,2},{4,5},{5,4},{6,7},{7,6},{8,9},{9,8},{10,11... | collective-permute-start | bytes 187400 | tf_op jit(solution)/shard_map/ppermute | solution.py:79
  57.7 0.9 collective-permute-done.6
  58.7 4.3 %collective-permute-done.7 = f32[32,488]{1,0:T(8,128)S(1)} collective-permute-done((f32[32,488]{1,0:T(8,128)S(1)}, f32[32,488]{1,0:T(8,128)S(1)}, u32[]{:S(2)}, u32[]{:S(2)}) %collective-permute-start.7) | collective-permute-done | bytes 62496 | tf_op jit(solution)/shard_map/ppermute | solution.py:79
  63.2 5.8 %collective-permute-done.8 = f32[32,488]{1,0:T(8,128)S(1)} collective-permute-done((f32[32,488]{1,0:T(8,128)S(1)}, f32[32,488]{1,0:T(8,128)S(1)}, u32[]{:S(2)}, u32[]{:S(2)}) %collective-permute-start.8) | collective-permute-done | bytes 62496 | tf_op jit(solution)/shard_map/ppermute | solution.py:79
  69.1 5.8 %collective-permute-done.9 = f32[32,488]{1,0:T(8,128)S(1)} collective-permute-done((f32[32,488]{1,0:T(8,128)S(1)}, f32[32,488]{1,0:T(8,128)S(1)}, u32[]{:S(2)}, u32[]{:S(2)}) %collective-permute-start.9) | collective-permute-done | bytes 62496 | tf_op jit(solution)/shard_map/ppermute | solution.py:79
  74.8 2.0 %collective-permute-start.10 = (f32[32,488]{1,0:T(8,128)S(1)}, f32[32,488]{1,0:T(8,128)S(1)}, u32[]{:S(2)}, u32[]{:S(2)}) collective-permute-start(f32[32,488]{1,0:T(8,128)S(1)} %add.91), channel_id=1, source_target_pairs={{0,16},{16,0},{32,48},{48,32},{64,80},{80,64},{96,112},{112,96},{1... | collective-permute-start | bytes 187400 | tf_op jit(solution)/shard_map/ppermute | solution.py:79
  76.8 2.4 %collective-permute-done.10 = f32[32,488]{1,0:T(8,128)S(1)} collective-permute-done((f32[32,488]{1,0:T(8,128)S(1)}, f32[32,488]{1,0:T(8,128)S(1)}, u32[]{:S(2)}, u32[]{:S(2)}) %collective-permute-start.10) | collective-permute-done | bytes 62496 | tf_op jit(solution)/shard_map/ppermute | solution.py:79
  79.2 3.7 %collective-permute-start.11 = (f32[32,488]{1,0:T(8,128)S(1)}, f32[32,488]{1,0:T(8,128)S(1)}, u32[]{:S(2)}, u32[]{:S(2)}) collective-permute-start(f32[32,488]{1,0:T(8,128)S(1)} %add.92), channel_id=1, source_target_pairs={{0,32},{16,48},{32,0},{48,16},{64,96},{80,112},{96,64},{112,80},{1... | collective-permute-start | bytes 187400 | tf_op jit(solution)/shard_map/ppermute | solution.py:79
  82.9 2.2 %collective-permute-done.11 = f32[32,488]{1,0:T(8,128)S(1)} collective-permute-done((f32[32,488]{1,0:T(8,128)S(1)}, f32[32,488]{1,0:T(8,128)S(1)}, u32[]{:S(2)}, u32[]{:S(2)}) %collective-permute-start.11) | collective-permute-done | bytes 62496 | tf_op jit(solution)/shard_map/ppermute | solution.py:79
  85.2 8.1 %collective-permute-start.12 = (f32[32,488]{1,0:T(8,128)S(1)}, f32[32,488]{1,0:T(8,128)S(1)}, u32[]{:S(2)}, u32[]{:S(2)}) collective-permute-start(f32[32,488]{1,0:T(8,128)S(1)} %add.93), channel_id=1, source_target_pairs={{0,64},{16,80},{32,96},{48,112},{64,0},{80,16},{96,32},{112,48},{1... | collective-permute-start | bytes 187400 | tf_op jit(solution)/shard_map/ppermute | solution.py:79
  93.3 2.2 %collective-permute-done.12 = f32[32,488]{1,0:T(8,128)S(1)} collective-permute-done((f32[32,488]{1,0:T(8,128)S(1)}, f32[32,488]{1,0:T(8,128)S(1)}, u32[]{:S(2)}, u32[]{:S(2)}) %collective-permute-start.12) | collective-permute-done | bytes 62496 | tf_op jit(solution)/shard_map/ppermute | solution.py:79
  96.8 3.0 %collective-permute-done.13 = f32[32,488]{1,0:T(8,128)S(1)} collective-permute-done((f32[32,488]{1,0:T(8,128)S(1)}, f32[32,488]{1,0:T(8,128)S(1)}, u32[]{:S(2)}, u32[]{:S(2)}) %collective-permute-start.13) | collective-permute-done | bytes 62496 | tf_op jit(solution)/shard_map/ppermute | solution.py:79
  101.5 0.9 copy.110
  102.4 0.8 copy.108
  (204 shorter events, 14.3 us)
Async XLA Ops:
  1.4 11.7 %collective-permute-start = (bf16[4,1,8,512]{3,2,1,0:T(8,128)(2,1)S(1)}, bf16[4,1,8,512]{3,2,1,0:T(8,128)(2,1)S(1)}, u32[]{:S(2)}, u32[]{:S(2)}) collective-permute-start(bf16[4,1,8,512]{3,2,1,0:T(8,128)(2,1)S(1)} %get-tuple-element.45), channel_id=1, source_target_pairs={{0,1},{1,2},{2,3},{3,4},{4,5},{5,6},{6,7},{7,8},{8,9},{9,10},{10,1... | collective-permute-start | bytes 98312 | tf_op jit(solution)/shard_map/ppermute | solution.py:15
  3.3 10.3 %collective-permute-start.1 = (bf16[4,1,8,512]{3,2,1,0:T(8,128)(2,1)S(1)}, bf16[4,1,8,512]{3,2,1,0:T(8,128)(2,1)S(1)}, u32[]{:S(2)}, u32[]{:S(2)}) collective-permute-start(bf16[4,1,8,512]{3,2,1,0:T(8,128)(2,1)S(1)} %get-tuple-element.46), channel_id=1, source_target_pairs={{1,0},{2,1},{3,2},{4,3},{5,4},{6,5},{7,6},{8,7},{9,8},{10,9},{11,1... | collective-permute-start | bytes 98312 | tf_op jit(solution)/shard_map/ppermute | solution.py:17
  16.0 0.8 copy-start.4
  16.8 1.8 %copy-start.2 = (bf16[4,8,432,128]{3,2,1,0:T(8,128)(2,1)}, bf16[4,8,432,128]{3,2,1,0:T(8,128)(2,1)S(1)}, u32[]{:S(2)}) copy-start(bf16[4,8,432,128]{3,2,1,0:T(8,128)(2,1)S(1)} %constant_dynamic-update-slice_fusion) | copy-start | bytes 10616836
  16.8 7.4 %copy-start = (bf16[32,16,3,3,3]{0,1,4,3,2:T(8,128)(2,1)S(1)}, bf16[32,16,3,3,3]{0,1,4,3,2:T(8,128)(2,1)}, u32[]{:S(2)}) copy-start(bf16[32,16,3,3,3]{0,1,4,3,2:T(8,128)(2,1)} %param.12) | copy-start | bytes 82948
  18.7 5.8 %collective-permute-start.2 = (bf16[16,2,1,4,128]{4,0,3,2,1:T(8,128)(2,1)S(1)}, bf16[16,2,1,4,128]{4,0,3,2,1:T(8,128)(2,1)S(1)}, u32[]{:S(2)}, u32[]{:S(2)}) collective-permute-start(bf16[16,2,1,4,128]{4,0,3,2,1:T(8,128)(2,1)S(1)} %get-tuple-element.51), channel_id=1, source_target_pairs={{0,1},{1,2},{2,3},{3,4},{4,5},{5,6},{6,7},{7,8},{8,9},{9,10},{10,1... | collective-permute-start | bytes 98312 | tf_op jit(solution)/shard_map/ppermute | solution.py:15
  21.9 7.7 %collective-permute-start.3 = (bf16[16,2,1,4,128]{4,0,3,2,1:T(8,128)(2,1)S(1)}, bf16[16,2,1,4,128]{4,0,3,2,1:T(8,128)(2,1)S(1)}, u32[]{:S(2)}, u32[]{:S(2)}) collective-permute-start(bf16[16,2,1,4,128]{4,0,3,2,1:T(8,128)(2,1)S(1)} %get-tuple-element.52), channel_id=1, source_target_pairs={{1,0},{2,1},{3,2},{4,3},{5,4},{6,5},{7,6},{8,7},{9,8},{10,9},{11,1... | collective-permute-start | bytes 98312 | tf_op jit(solution)/shard_map/ppermute | solution.py:17
  30.4 1.0 copy-start.5
  32.0 10.8 %collective-permute-start.4 = (bf16[32,2,1,4,128]{4,0,3,2,1:T(8,128)(2,1)S(1)}, bf16[32,2,1,4,128]{4,0,3,2,1:T(8,128)(2,1)S(1)}, u32[]{:S(2)}, u32[]{:S(2)}) collective-permute-start(bf16[32,2,1,4,128]{4,0,3,2,1:T(8,128)(2,1)S(1)} %get-tuple-element.41), channel_id=1, source_target_pairs={{0,1},{1,2},{2,3},{3,4},{4,5},{5,6},{6,7},{7,8},{8,9},{9,10},{10,1... | collective-permute-start | bytes 196616 | tf_op jit(solution)/shard_map/ppermute | solution.py:15
  40.1 3.8 %collective-permute-start.5 = (bf16[32,2,1,4,128]{4,0,3,2,1:T(8,128)(2,1)S(1)}, bf16[32,2,1,4,128]{4,0,3,2,1:T(8,128)(2,1)S(1)}, u32[]{:S(2)}, u32[]{:S(2)}) collective-permute-start(bf16[32,2,1,4,128]{4,0,3,2,1:T(8,128)(2,1)S(1)} %get-tuple-element.42), channel_id=1, source_target_pairs={{1,0},{2,1},{3,2},{4,3},{5,4},{6,5},{7,6},{8,7},{9,8},{10,9},{11,1... | collective-permute-start | bytes 196616 | tf_op jit(solution)/shard_map/ppermute | solution.py:17
  46.7 2.0 %copy-start.3 = (bf16[4,8,432,128]{3,2,1,0:T(8,128)(2,1)S(1)}, bf16[4,8,432,128]{3,2,1,0:T(8,128)(2,1)}, u32[]{:S(2)}) copy-start(bf16[4,8,432,128]{3,2,1,0:T(8,128)(2,1)} %copy-done.2) | copy-start | bytes 10616836
  48.7 2.0 %copy-start.1 = (f32[4,3,4,3]{3,2,1,0:T(4,128)S(1)}, f32[4,3,4,3]{3,2,1,0:T(4,128)}, u32[]{:S(2)}) copy-start(f32[4,3,4,3]{3,2,1,0:T(4,128)} %constant.46) | copy-start | bytes 1732
  52.1 6.5 %collective-permute-start.6 = (f32[32,488]{1,0:T(8,128)S(1)}, f32[32,488]{1,0:T(8,128)S(1)}, u32[]{:S(2)}, u32[]{:S(2)}) collective-permute-start(f32[32,488]{1,0:T(8,128)S(1)} %pad_maximum_fusion.5), channel_id=1, source_target_pairs={{0,1},{1,0},{2,3},{3,2},{4,5},{5,4},{6,7},{7,6},{8,9},{9,8},{10,11... | collective-permute-start | bytes 187400 | tf_op jit(solution)/shard_map/ppermute | solution.py:79
  58.7 4.4 %collective-permute-start.7 = (f32[32,488]{1,0:T(8,128)S(1)}, f32[32,488]{1,0:T(8,128)S(1)}, u32[]{:S(2)}, u32[]{:S(2)}) collective-permute-start(f32[32,488]{1,0:T(8,128)S(1)} %fusion.38), channel_id=1, source_target_pairs={{0,2},{1,3},{2,0},{3,1},{4,6},{5,7},{6,4},{7,5},{8,10},{9,11},{10,... | collective-permute-start | bytes 187400 | tf_op jit(solution)/shard_map/ppermute | solution.py:79
  63.1 5.9 %collective-permute-start.8 = (f32[32,488]{1,0:T(8,128)S(1)}, f32[32,488]{1,0:T(8,128)S(1)}, u32[]{:S(2)}, u32[]{:S(2)}) collective-permute-start(f32[32,488]{1,0:T(8,128)S(1)} %add.89), channel_id=1, source_target_pairs={{0,4},{1,5},{2,6},{3,7},{4,0},{5,1},{6,2},{7,3},{8,12},{9,13},{10,... | collective-permute-start | bytes 187400 | tf_op jit(solution)/shard_map/ppermute | solution.py:79
  69.0 5.9 %collective-permute-start.9 = (f32[32,488]{1,0:T(8,128)S(1)}, f32[32,488]{1,0:T(8,128)S(1)}, u32[]{:S(2)}, u32[]{:S(2)}) collective-permute-start(f32[32,488]{1,0:T(8,128)S(1)} %add.90), channel_id=1, source_target_pairs={{0,8},{1,9},{2,10},{3,11},{4,12},{5,13},{6,14},{7,15},{8,0},{9,1},... | collective-permute-start | bytes 187400 | tf_op jit(solution)/shard_map/ppermute | solution.py:79
  74.8 4.4 %collective-permute-start.10 = (f32[32,488]{1,0:T(8,128)S(1)}, f32[32,488]{1,0:T(8,128)S(1)}, u32[]{:S(2)}, u32[]{:S(2)}) collective-permute-start(f32[32,488]{1,0:T(8,128)S(1)} %add.91), channel_id=1, source_target_pairs={{0,16},{16,0},{32,48},{48,32},{64,80},{80,64},{96,112},{112,96},{1... | collective-permute-start | bytes 187400 | tf_op jit(solution)/shard_map/ppermute | solution.py:79
  79.2 6.0 %collective-permute-start.11 = (f32[32,488]{1,0:T(8,128)S(1)}, f32[32,488]{1,0:T(8,128)S(1)}, u32[]{:S(2)}, u32[]{:S(2)}) collective-permute-start(f32[32,488]{1,0:T(8,128)S(1)} %add.92), channel_id=1, source_target_pairs={{0,32},{16,48},{32,0},{48,16},{64,96},{80,112},{96,64},{112,80},{1... | collective-permute-start | bytes 187400 | tf_op jit(solution)/shard_map/ppermute | solution.py:79
  85.2 10.3 %collective-permute-start.12 = (f32[32,488]{1,0:T(8,128)S(1)}, f32[32,488]{1,0:T(8,128)S(1)}, u32[]{:S(2)}, u32[]{:S(2)}) collective-permute-start(f32[32,488]{1,0:T(8,128)S(1)} %add.93), channel_id=1, source_target_pairs={{0,64},{16,80},{32,96},{48,112},{64,0},{80,16},{96,32},{112,48},{1... | collective-permute-start | bytes 187400 | tf_op jit(solution)/shard_map/ppermute | solution.py:79
  95.5 4.4 %collective-permute-start.13 = (f32[32,488]{1,0:T(8,128)S(1)}, f32[32,488]{1,0:T(8,128)S(1)}, u32[]{:S(2)}, u32[]{:S(2)}) collective-permute-start(f32[32,488]{1,0:T(8,128)S(1)} %add.94), channel_id=1, source_target_pairs={{0,128},{16,144},{32,160},{48,176},{64,192},{80,208},{96,224},{112... | collective-permute-start | bytes 187400 | tf_op jit(solution)/shard_map/ppermute | solution.py:79

commit v5 on v4

--- a/solution.py
+++ b/solution.py
@@ -5,11 +5,11 @@
 from jax.sharding import PartitionSpec as P
 
 
-def with_halo(cells, axis, dim):
+def with_halo(cells, axis, dim, width=1):
     count = lax.axis_size(axis)
     ends = count - 1
-    head = lax.slice_in_dim(cells, 0, 1, axis=dim)
-    tail = lax.slice_in_dim(cells, cells.shape[dim] - 1, cells.shape[dim], axis=dim)
+    head = lax.slice_in_dim(cells, 0, width, axis=dim)
+    tail = lax.slice_in_dim(cells, cells.shape[dim] - width, cells.shape[dim], axis=dim)
     return jnp.concatenate(
         [
             lax.ppermute(tail, axis, [(i, (i + 1) % count) for i in range(ends)]),
@@ -127,17 +127,24 @@
     sample = volume[0]
     cot = cotangent[0]
     chan0, _, height, width = sample.shape
-    halo = with_halo(sample, "space", 1)
+    depth = sample.shape[1]
+    halo = with_halo(sample, "space", 1, 3)
     merged = jnp.transpose(halo.reshape(chan0, halo.shape[1], height, width // 4, 4), (1, 2, 4, 0, 3))
-    patches_first = merged_patches(merged.reshape(halo.shape[1], height, 4 * chan0, width // 4))
-    pre_first = (
+    patches_wide = merged_patches(merged.reshape(halo.shape[1], height, 4 * chan0, width // 4))
+    pre_wide = (
         jnp.einsum(
-            "ork,xykm->orxym", merged_kernel(w_first, 4), patches_first, preferred_element_type=jnp.float32
+            "ork,xykm->orxym", merged_kernel(w_first, 4), patches_wide, preferred_element_type=jnp.float32
         )
         + b_first[:, None, None, None, None]
     )
-    pooled = pool(jax.nn.silu(pre_first)).astype(jnp.bfloat16)
-    pooled_halo = jnp.transpose(with_halo(pooled, "space", 2), (1, 2, 3, 0, 4))
+    pooled_wide = pool(jax.nn.silu(pre_wide)).astype(jnp.bfloat16)
+    place = lax.axis_index("space")
+    rows = jnp.arange(pooled_wide.shape[2])
+    inside = ((rows > 0) | (place > 0)) & ((rows < pooled_wide.shape[2] - 1) | (place < lax.axis_size("space") - 1))
+    pooled_wide = jnp.where(inside[None, None, :, None, None], pooled_wide, jnp.zeros_like(pooled_wide))
+    pooled_halo = jnp.transpose(pooled_wide, (1, 2, 3, 0, 4))
+    pre_first = pre_wide[:, :, 2 : 2 + depth]
+    patches_first = patches_wide[2 : 2 + depth]
     patches_second = phase_patches(pooled_halo)
     pre_second = conv_taps(tap_major(w_second), patches_second) + b_second[:, None, None, None, None]
     output = pool(jax.nn.silu(pre_second))[:, 0].astype(jnp.bfloat16)

time: 104 us -> 98.5 us (0.947)
  starting transfers between devices: 41.5 us -> 33.9 us
  matrix products: 4.65 us -> 9.16 us
  local copies, waits for them, and re-layouts: 17.3 us -> 20.4 us
  waiting for transfers between devices: 32.9 us -> 29.9 us
  other arithmetic: 5.15 us -> 2.99 us
    ppermute x3 -> x2, starting transfers between devices: 13.3 us -> 6.87 us  [with_halo(): lax.ppermute(tail, axis, [(i, (i + 1) % count) for i in range(ends)])]
    ppermute x3 -> x2, waiting for transfers between devices: 6.3 us -> 3.22 us  [with_halo(): lax.ppermute(head, axis, [((i + 1) % count, i) for i in range(ends)])]
    dot_general x1, matrix products: 0.89 us -> 3.41 us  [shards(): jnp.einsum('ork,xykm->orxym', merged_kernel(w_first, 4), patches_wide, pr...]
    ppermute x3 -> x2, starting transfers between devices: 7.93 us -> 5.74 us  [with_halo(): lax.ppermute(head, axis, [((i + 1) % count, i) for i in range(ends)])]
    dot_general x1, matrix products: 1.98 us -> 3.98 us  [shards(): jnp.einsum('orxym,xykm->ork', grad_first, patches_first, preferred_elemen...]
    unnamed x141 -> x145, local copies, waits for them, and re-layouts: 10.1 us -> 10.5 us
  transfers between devices with their start and end apart: 14 -> 12, of which waited for: 10 -> 9; matrix products, arithmetic and copies ran while one was open for 8% -> 7% of each run, Pallas kernels for 0% -> 0%
where the time goes in v5:
time: 98.5 us; the launch traced here: 98.1 us
  starting transfers between devices  33.9 us (34%)
  waiting for transfers between devices  29.9 us (30%)
  local copies, waits for them, and re-layouts  20.4 us (21%)
  matrix products  9.16 us (9%)
  other arithmetic  2.99 us (3%)
  between operations  1.78 us (2%)
    ppermute x8, waiting for transfers between devices, butterfly_sum(): lax.ppermute(rows, axis, [(i, i ^ step) for i in range(count)])  26.6 us
    ppermute x8, starting transfers between devices, butterfly_sum(): lax.ppermute(rows, axis, [(i, i ^ step) for i in range(count)])  21.3 us
    unnamed x145, local copies, waits for them, and re-layouts  10.5 us
    ppermute x2, starting transfers between devices, with_halo(): lax.ppermute(tail, axis, [(i, (i + 1) % count) for i in range(ends)])  6.87 us
    ppermute x2, starting transfers between devices, with_halo(): lax.ppermute(head, axis, [((i + 1) % count, i) for i in range(ends)])  5.74 us
    dot_general x1, matrix products, shards(): jnp.einsum('orxym,xykm->ork', grad_first, patches_first, preferred_elemen...  3.98 us
    dot_general x1, matrix products, shards(): jnp.einsum('ork,xykm->orxym', merged_kernel(w_first, 4), patches_wide, pr...  3.41 us
    ppermute x2, waiting for transfers between devices, with_halo(): lax.ppermute(head, axis, [((i + 1) % count, i) for i in range(ends)])  3.22 us
  transfers between devices with their start and end apart: 12, of which 9 were waited for; matrix products, arithmetic and copies ran while one was open for 7% of the time, Pallas kernels for 0%

profile of v5, /device:TPU:24, one launch (start us, length us, event | category | flops | bytes accessed | tf_op | source)
XLA Modules:
  0.0 98.1 jit_solution(7855095294599342273)
XLA Ops:
  0.6 1.0 %fusion.32 = (bf16[4,3,8,512]{3,2,1,0:T(8,128)(2,1)S(1)}, bf16[4,3,8,512]{3,2,1,0:T(8,128)(2,1)S(1)}) fusion(bf16[4,4,8,512]{3,2,1,0:T(8,128)(2,1)} %bitcast.133), kind=kLoop, calls=%fused_computation.198 | loop fusion | bytes 393216 | tf_op jit(solution)/shard_map/slice | solution.py:12
  1.6 1.9 %collective-permute-start = (bf16[4,3,8,512]{3,2,1,0:T(8,128)(2,1)S(1)}, bf16[4,3,8,512]{3,2,1,0:T(8,128)(2,1)S(1)}, u32[]{:S(2)}, u32[]{:S(2)}) collective-permute-start(bf16[4,3,8,512]{3,2,1,0:T(8,128)(2,1)S(1)} %get-tuple-element.45), channel_id=1, source_target_pairs={{0,1},{1,2},{2,3},{3,4},{4,5},{5,6},{6,7},{7,8},{8,9},{9,10},{10,1... | collective-permute-start | bytes 294920 | tf_op jit(solution)/shard_map/ppermute | solution.py:15
  3.6 3.6 %collective-permute-start.1 = (bf16[4,3,8,512]{3,2,1,0:T(8,128)(2,1)S(1)}, bf16[4,3,8,512]{3,2,1,0:T(8,128)(2,1)S(1)}, u32[]{:S(2)}, u32[]{:S(2)}) collective-permute-start(bf16[4,3,8,512]{3,2,1,0:T(8,128)(2,1)S(1)} %get-tuple-element.46), channel_id=1, source_target_pairs={{1,0},{2,1},{3,2},{4,3},{5,4},{6,5},{7,6},{8,7},{9,8},{10,9},{11,1... | collective-permute-start | bytes 294920 | tf_op jit(solution)/shard_map/ppermute | solution.py:17
  7.2 1.8 %copy.88 = bf16[1,4,4,8,512]{3,4,2,1,0:T(8,128)(2,1)S(1)} copy(bf16[1,4,4,8,512]{4,3,2,1,0:T(8,128)(2,1)} %param.8) | data formatting | bytes 262144 | tf_op args[0]
  9.1 0.9 copy.91
  10.3 1.0 %multiply_reduce_fusion.1 = bf16[16,4,3,3,3,4,4]{0,6,5,4,3,2,1:T(4,128)(2,1)S(1)} fusion(f32[4,3,4,3]{3,2,1,0:T(4,128)S(1)} %copy-done.2, f32[16,3,3,4,3]{0,3,4,2,1:T(4,128)S(1)} %convert_bitcast_fusion), kind=kLoop, calls=%fused_computation.9 | loop fusion | flops 138240 | bytes 62784 | tf_op jit(solution)/shard_map/reduce_sum | solution.py:116
  11.3 0.8 copy.87
  12.1 0.7 copy.90
  12.8 0.8 copy.89
  18.7 3.4 %divide_multiply_fusion = (f32[16,4,8,8,128]{4,0,3,2,1:T(8,128)S(1)}, f32[16,4,8,8,128]{4,0,3,2,1:T(8,128)}) fusion(f32[16]{0:T(128)S(1)} %copy-done.6, bf16[16,4,432,1,1]{0,2,4,3,1:T(8,128)(2,1)S(1)} %bitcast.135, bf16[8,8,432,128]{3,2,1,0:T(8,128)(2,1)S(1)} %constant_dynamic-update-slice_fusion), kind=kOutput, calls=%fused_computation.10 | convolution fusion | flops 455606272 | bytes 11327552 | tf_op jit(solution)/shard_map/ork,xykm->orxym/dot_general | solution.py:135
  24.9 5.0 %collective-permute-start.2 = (bf16[32,2,1,4,128]{4,0,3,2,1:T(8,128)(2,1)S(1)}, bf16[32,2,1,4,128]{4,0,3,2,1:T(8,128)(2,1)S(1)}, u32[]{:S(2)}, u32[]{:S(2)}) collective-permute-start(bf16[32,2,1,4,128]{4,0,3,2,1:T(8,128)(2,1)S(1)} %get-tuple-element.41), channel_id=1, source_target_pairs={{0,1},{1,2},{2,3},{3,4},{4,5},{5,6},{6,7},{7,8},{8,9},{9,10},{10,1... | collective-permute-start | bytes 196616 | tf_op jit(solution)/shard_map/ppermute | solution.py:15
  29.9 2.1 %collective-permute-start.3 = (bf16[32,2,1,4,128]{4,0,3,2,1:T(8,128)(2,1)S(1)}, bf16[32,2,1,4,128]{4,0,3,2,1:T(8,128)(2,1)S(1)}, u32[]{:S(2)}, u32[]{:S(2)}) collective-permute-start(bf16[32,2,1,4,128]{4,0,3,2,1:T(8,128)(2,1)S(1)} %get-tuple-element.42), channel_id=1, source_target_pairs={{1,0},{2,1},{3,2},{4,3},{5,4},{6,5},{7,6},{8,7},{9,8},{10,9},{11,1... | collective-permute-start | bytes 196616 | tf_op jit(solution)/shard_map/ppermute | solution.py:17
  32.7 3.2 %collective-permute-done.3 = bf16[32,2,1,4,128]{4,0,3,2,1:T(8,128)(2,1)S(1)} collective-permute-done((bf16[32,2,1,4,128]{4,0,3,2,1:T(8,128)(2,1)S(1)}, bf16[32,2,1,4,128]{4,0,3,2,1:T(8,128)(2,1)S(1)}, u32[]{:S(2)}, u32[]{:S(2)}) %collective-permute-start.3) | collective-permute-done | bytes 65568 | tf_op jit(solution)/shard_map/ppermute | solution.py:17
  38.7 1.4 %copy-done = f32[16,4,8,8,128]{4,0,3,2,1:T(8,128)S(1)} copy-done((f32[16,4,8,8,128]{4,0,3,2,1:T(8,128)S(1)}, f32[16,4,8,8,128]{4,0,3,2,1:T(8,128)}, u32[]{:S(2)}) %copy-start) | copy-done | bytes 2097176
  40.7 4.0 %fusion.2 = f32[16,4,432,1,1]{0,2,4,3,1:T(8,128)S(1)} fusion(bf16[16,4,4,8,128]{4,0,3,2,1:T(8,128)(2,1)S(1)} %get-tuple-element.28, bf16[8,8,432,128]{3,2,1,0:T(8,128)(2,1)} %copy-done.5), kind=kOutput, calls=%fused_computation.3 | convolution fusion | flops 226492416 | bytes 4173824 | tf_op jit(solution)/shard_map/orxym,xykm->ork/dot_general | solution.py:161
  44.7 0.8 multiply_reduce_fusion
  46.0 6.6 %collective-permute-start.4 = (f32[32,488]{1,0:T(8,128)S(1)}, f32[32,488]{1,0:T(8,128)S(1)}, u32[]{:S(2)}, u32[]{:S(2)}) collective-permute-start(f32[32,488]{1,0:T(8,128)S(1)} %pad_maximum_fusion.5), channel_id=1, source_target_pairs={{0,1},{1,0},{2,3},{3,2},{4,5},{5,4},{6,7},{7,6},{8,9},{9,8},{10,11... | collective-permute-start | bytes 187400 | tf_op jit(solution)/shard_map/ppermute | solution.py:79
  52.6 0.9 collective-permute-done.4
  53.7 4.3 %collective-permute-done.5 = f32[32,488]{1,0:T(8,128)S(1)} collective-permute-done((f32[32,488]{1,0:T(8,128)S(1)}, f32[32,488]{1,0:T(8,128)S(1)}, u32[]{:S(2)}, u32[]{:S(2)}) %collective-permute-start.5) | collective-permute-done | bytes 62496 | tf_op jit(solution)/shard_map/ppermute | solution.py:79
  58.1 5.8 %collective-permute-done.6 = f32[32,488]{1,0:T(8,128)S(1)} collective-permute-done((f32[32,488]{1,0:T(8,128)S(1)}, f32[32,488]{1,0:T(8,128)S(1)}, u32[]{:S(2)}, u32[]{:S(2)}) %collective-permute-start.6) | collective-permute-done | bytes 62496 | tf_op jit(solution)/shard_map/ppermute | solution.py:79
  64.0 5.8 %collective-permute-done.7 = f32[32,488]{1,0:T(8,128)S(1)} collective-permute-done((f32[32,488]{1,0:T(8,128)S(1)}, f32[32,488]{1,0:T(8,128)S(1)}, u32[]{:S(2)}, u32[]{:S(2)}) %collective-permute-start.7) | collective-permute-done | bytes 62496 | tf_op jit(solution)/shard_map/ppermute | solution.py:79
  69.8 2.0 %collective-permute-start.8 = (f32[32,488]{1,0:T(8,128)S(1)}, f32[32,488]{1,0:T(8,128)S(1)}, u32[]{:S(2)}, u32[]{:S(2)}) collective-permute-start(f32[32,488]{1,0:T(8,128)S(1)} %add.94), channel_id=1, source_target_pairs={{0,16},{16,0},{32,48},{48,32},{64,80},{80,64},{96,112},{112,96},{1... | collective-permute-start | bytes 187400 | tf_op jit(solution)/shard_map/ppermute | solution.py:79
  71.8 2.3 %collective-permute-done.8 = f32[32,488]{1,0:T(8,128)S(1)} collective-permute-done((f32[32,488]{1,0:T(8,128)S(1)}, f32[32,488]{1,0:T(8,128)S(1)}, u32[]{:S(2)}, u32[]{:S(2)}) %collective-permute-start.8) | collective-permute-done | bytes 62496 | tf_op jit(solution)/shard_map/ppermute | solution.py:79
  74.1 3.7 %collective-permute-start.9 = (f32[32,488]{1,0:T(8,128)S(1)}, f32[32,488]{1,0:T(8,128)S(1)}, u32[]{:S(2)}, u32[]{:S(2)}) collective-permute-start(f32[32,488]{1,0:T(8,128)S(1)} %add.95), channel_id=1, source_target_pairs={{0,32},{16,48},{32,0},{48,16},{64,96},{80,112},{96,64},{112,80},{1... | collective-permute-start | bytes 187400 | tf_op jit(solution)/shard_map/ppermute | solution.py:79
  77.9 2.2 %collective-permute-done.9 = f32[32,488]{1,0:T(8,128)S(1)} collective-permute-done((f32[32,488]{1,0:T(8,128)S(1)}, f32[32,488]{1,0:T(8,128)S(1)}, u32[]{:S(2)}, u32[]{:S(2)}) %collective-permute-start.9) | collective-permute-done | bytes 62496 | tf_op jit(solution)/shard_map/ppermute | solution.py:79
  80.1 8.1 %collective-permute-start.10 = (f32[32,488]{1,0:T(8,128)S(1)}, f32[32,488]{1,0:T(8,128)S(1)}, u32[]{:S(2)}, u32[]{:S(2)}) collective-permute-start(f32[32,488]{1,0:T(8,128)S(1)} %add.96), channel_id=1, source_target_pairs={{0,64},{16,80},{32,96},{48,112},{64,0},{80,16},{96,32},{112,48},{1... | collective-permute-start | bytes 187400 | tf_op jit(solution)/shard_map/ppermute | solution.py:79
  88.2 2.2 %collective-permute-done.10 = f32[32,488]{1,0:T(8,128)S(1)} collective-permute-done((f32[32,488]{1,0:T(8,128)S(1)}, f32[32,488]{1,0:T(8,128)S(1)}, u32[]{:S(2)}, u32[]{:S(2)}) %collective-permute-start.10) | collective-permute-done | bytes 62496 | tf_op jit(solution)/shard_map/ppermute | solution.py:79
  91.7 3.1 %collective-permute-done.11 = f32[32,488]{1,0:T(8,128)S(1)} collective-permute-done((f32[32,488]{1,0:T(8,128)S(1)}, f32[32,488]{1,0:T(8,128)S(1)}, u32[]{:S(2)}, u32[]{:S(2)}) %collective-permute-start.11) | collective-permute-done | bytes 62496 | tf_op jit(solution)/shard_map/ppermute | solution.py:79
  94.9 0.7 slice_reduce_fusion
  95.6 0.7 slice_reduce_fusion.1
  96.5 0.9 copy.108
  97.3 0.8 copy.106
  (203 shorter events, 13.9 us)
Async XLA Ops:
  1.6 9.7 %collective-permute-start = (bf16[4,3,8,512]{3,2,1,0:T(8,128)(2,1)S(1)}, bf16[4,3,8,512]{3,2,1,0:T(8,128)(2,1)S(1)}, u32[]{:S(2)}, u32[]{:S(2)}) collective-permute-start(bf16[4,3,8,512]{3,2,1,0:T(8,128)(2,1)S(1)} %get-tuple-element.45), channel_id=1, source_target_pairs={{0,1},{1,2},{2,3},{3,4},{4,5},{5,6},{6,7},{7,8},{8,9},{9,10},{10,1... | collective-permute-start | bytes 294920 | tf_op jit(solution)/shard_map/ppermute | solution.py:15
  3.6 6.4 %copy-start.3 = (bf16[16,4,3,3,3]{0,1,4,3,2:T(4,128)(2,1)S(1)}, bf16[16,4,3,3,3]{0,1,4,3,2:T(4,128)(2,1)}, u32[]{:S(2)}) copy-start(bf16[16,4,3,3,3]{0,1,4,3,2:T(4,128)(2,1)} %param.10) | copy-start | bytes 10372
  3.6 6.5 %copy-start.4 = (bf16[1,32,1,2,128]{4,3,2,1,0:T(2,128)(2,1)S(1)}, bf16[1,32,1,2,128]{4,3,2,1,0:T(2,128)(2,1)}, u32[]{:S(2)}) copy-start(bf16[1,32,1,2,128]{4,3,2,1,0:T(2,128)(2,1)} %param.9) | copy-start | bytes 49156
  3.6 9.3 %collective-permute-start.1 = (bf16[4,3,8,512]{3,2,1,0:T(8,128)(2,1)S(1)}, bf16[4,3,8,512]{3,2,1,0:T(8,128)(2,1)S(1)}, u32[]{:S(2)}, u32[]{:S(2)}) collective-permute-start(bf16[4,3,8,512]{3,2,1,0:T(8,128)(2,1)S(1)} %get-tuple-element.46), channel_id=1, source_target_pairs={{1,0},{2,1},{3,2},{4,3},{5,4},{6,5},{7,6},{8,7},{9,8},{10,9},{11,1... | collective-permute-start | bytes 294920 | tf_op jit(solution)/shard_map/ppermute | solution.py:17
  9.1 1.0 %copy-start.1 = (bf16[32,16,3,3,3]{0,1,4,3,2:T(8,128)(2,1)S(1)}, bf16[32,16,3,3,3]{0,1,4,3,2:T(8,128)(2,1)}, u32[]{:S(2)}) copy-start(bf16[32,16,3,3,3]{0,1,4,3,2:T(8,128)(2,1)} %param.12) | copy-start | bytes 82948
  9.1 1.2 %copy-start.2 = (f32[4,3,4,3]{3,2,1,0:T(4,128)S(1)}, f32[4,3,4,3]{3,2,1,0:T(4,128)}, u32[]{:S(2)}) copy-start(f32[4,3,4,3]{3,2,1,0:T(4,128)} %constant.57) | copy-start | bytes 1732
  17.9 0.7 copy-start.6
  18.6 3.5 %copy-start.5 = (bf16[8,8,432,128]{3,2,1,0:T(8,128)(2,1)}, bf16[8,8,432,128]{3,2,1,0:T(8,128)(2,1)S(1)}, u32[]{:S(2)}) copy-start(bf16[8,8,432,128]{3,2,1,0:T(8,128)(2,1)S(1)} %constant_dynamic-update-slice_fusion) | copy-start | bytes 21233668
  23.3 1.0 %copy-start.7 = (f32[32]{0:T(128)S(1)}, f32[32]{0:T(128)}, u32[]{:S(2)}) copy-start(f32[32]{0:T(128)} %param.13) | copy-start | bytes 388
  24.9 7.8 %collective-permute-start.2 = (bf16[32,2,1,4,128]{4,0,3,2,1:T(8,128)(2,1)S(1)}, bf16[32,2,1,4,128]{4,0,3,2,1:T(8,128)(2,1)S(1)}, u32[]{:S(2)}, u32[]{:S(2)}) collective-permute-start(bf16[32,2,1,4,128]{4,0,3,2,1:T(8,128)(2,1)S(1)} %get-tuple-element.41), channel_id=1, source_target_pairs={{0,1},{1,2},{2,3},{3,4},{4,5},{5,6},{6,7},{7,8},{8,9},{9,10},{10,1... | collective-permute-start | bytes 196616 | tf_op jit(solution)/shard_map/ppermute | solution.py:15
  29.9 6.0 %collective-permute-start.3 = (bf16[32,2,1,4,128]{4,0,3,2,1:T(8,128)(2,1)S(1)}, bf16[32,2,1,4,128]{4,0,3,2,1:T(8,128)(2,1)S(1)}, u32[]{:S(2)}, u32[]{:S(2)}) collective-permute-start(bf16[32,2,1,4,128]{4,0,3,2,1:T(8,128)(2,1)S(1)} %get-tuple-element.42), channel_id=1, source_target_pairs={{1,0},{2,1},{3,2},{4,3},{5,4},{6,5},{7,6},{8,7},{9,8},{10,9},{11,1... | collective-permute-start | bytes 196616 | tf_op jit(solution)/shard_map/ppermute | solution.py:17
  38.6 1.6 %copy-start = (f32[16,4,8,8,128]{4,0,3,2,1:T(8,128)S(1)}, f32[16,4,8,8,128]{4,0,3,2,1:T(8,128)}, u32[]{:S(2)}) copy-start(f32[16,4,8,8,128]{4,0,3,2,1:T(8,128)} %get-tuple-element.52) | copy-start | bytes 6291460
  46.0 7.5 %collective-permute-start.4 = (f32[32,488]{1,0:T(8,128)S(1)}, f32[32,488]{1,0:T(8,128)S(1)}, u32[]{:S(2)}, u32[]{:S(2)}) collective-permute-start(f32[32,488]{1,0:T(8,128)S(1)} %pad_maximum_fusion.5), channel_id=1, source_target_pairs={{0,1},{1,0},{2,3},{3,2},{4,5},{5,4},{6,7},{7,6},{8,9},{9,8},{10,11... | collective-permute-start | bytes 187400 | tf_op jit(solution)/shard_map/ppermute | solution.py:79
  53.6 4.4 %collective-permute-start.5 = (f32[32,488]{1,0:T(8,128)S(1)}, f32[32,488]{1,0:T(8,128)S(1)}, u32[]{:S(2)}, u32[]{:S(2)}) collective-permute-start(f32[32,488]{1,0:T(8,128)S(1)} %fusion.37), channel_id=1, source_target_pairs={{0,2},{1,3},{2,0},{3,1},{4,6},{5,7},{6,4},{7,5},{8,10},{9,11},{10,... | collective-permute-start | bytes 187400 | tf_op jit(solution)/shard_map/ppermute | solution.py:79
  58.0 5.9 %collective-permute-start.6 = (f32[32,488]{1,0:T(8,128)S(1)}, f32[32,488]{1,0:T(8,128)S(1)}, u32[]{:S(2)}, u32[]{:S(2)}) collective-permute-start(f32[32,488]{1,0:T(8,128)S(1)} %add.92), channel_id=1, source_target_pairs={{0,4},{1,5},{2,6},{3,7},{4,0},{5,1},{6,2},{7,3},{8,12},{9,13},{10,... | collective-permute-start | bytes 187400 | tf_op jit(solution)/shard_map/ppermute | solution.py:79
  63.9 5.9 %collective-permute-start.7 = (f32[32,488]{1,0:T(8,128)S(1)}, f32[32,488]{1,0:T(8,128)S(1)}, u32[]{:S(2)}, u32[]{:S(2)}) collective-permute-start(f32[32,488]{1,0:T(8,128)S(1)} %add.93), channel_id=1, source_target_pairs={{0,8},{1,9},{2,10},{3,11},{4,12},{5,13},{6,14},{7,15},{8,0},{9,1},... | collective-permute-start | bytes 187400 | tf_op jit(solution)/shard_map/ppermute | solution.py:79
  69.8 4.4 %collective-permute-start.8 = (f32[32,488]{1,0:T(8,128)S(1)}, f32[32,488]{1,0:T(8,128)S(1)}, u32[]{:S(2)}, u32[]{:S(2)}) collective-permute-start(f32[32,488]{1,0:T(8,128)S(1)} %add.94), channel_id=1, source_target_pairs={{0,16},{16,0},{32,48},{48,32},{64,80},{80,64},{96,112},{112,96},{1... | collective-permute-start | bytes 187400 | tf_op jit(solution)/shard_map/ppermute | solution.py:79
  74.1 6.0 %collective-permute-start.9 = (f32[32,488]{1,0:T(8,128)S(1)}, f32[32,488]{1,0:T(8,128)S(1)}, u32[]{:S(2)}, u32[]{:S(2)}) collective-permute-start(f32[32,488]{1,0:T(8,128)S(1)} %add.95), channel_id=1, source_target_pairs={{0,32},{16,48},{32,0},{48,16},{64,96},{80,112},{96,64},{112,80},{1... | collective-permute-start | bytes 187400 | tf_op jit(solution)/shard_map/ppermute | solution.py:79
  80.1 10.3 %collective-permute-start.10 = (f32[32,488]{1,0:T(8,128)S(1)}, f32[32,488]{1,0:T(8,128)S(1)}, u32[]{:S(2)}, u32[]{:S(2)}) collective-permute-start(f32[32,488]{1,0:T(8,128)S(1)} %add.96), channel_id=1, source_target_pairs={{0,64},{16,80},{32,96},{48,112},{64,0},{80,16},{96,32},{112,48},{1... | collective-permute-start | bytes 187400 | tf_op jit(solution)/shard_map/ppermute | solution.py:79
  90.4 4.4 %collective-permute-start.11 = (f32[32,488]{1,0:T(8,128)S(1)}, f32[32,488]{1,0:T(8,128)S(1)}, u32[]{:S(2)}, u32[]{:S(2)}) collective-permute-start(f32[32,488]{1,0:T(8,128)S(1)} %add.97), channel_id=1, source_target_pairs={{0,128},{16,144},{32,160},{48,176},{64,192},{80,208},{96,224},{112... | collective-permute-start | bytes 187400 | tf_op jit(solution)/shard_map/ppermute | solution.py:79

commit v6 on v5

--- a/solution.py
+++ b/solution.py
@@ -158,7 +158,14 @@
     back = conv_taps(flipped, phase_patches(grad_halo))
     grad_first = (upsample(back, 4) * 0.125 * silu_slope(pre_first)).astype(jnp.bfloat16)
     grad_w1 = merged_grad(
-        jnp.einsum("orxym,xykm->ork", grad_first, patches_first, preferred_element_type=jnp.float32),
+        lax.optimization_barrier(
+            jnp.einsum(
+                "qxym,xykm->qk",
+                grad_first.reshape((-1,) + grad_first.shape[2:]),
+                patches_first,
+                preferred_element_type=jnp.float32,
+            )
+        ).reshape(grad_first.shape[0], grad_first.shape[1], -1),
         chan0,
         4,
     )

time: 98.5 us -> 109 us (1.11)
  local copies, waits for them, and re-layouts: 20.4 us -> 27.5 us
  other arithmetic: 2.99 us -> 5.56 us
    mul x0 -> x2, local copies, waits for them, and re-layouts: none -> 6.35 us  [merged_grad(): full[..., None] * sel[None, :, None, None, :, :, None, :]]
    reduce_sum x1, other arithmetic: 0.76 us -> 1.97 us  [merged_grad(): (full[..., None] * sel[None, :, None, None, :, :, None, :]).sum(axis=(1,...]
    unnamed x145 -> x149, local copies, waits for them, and re-layouts: 10.5 us -> 10.5 us
where the time goes in v6:
time: 109 us; the launch traced here: 108 us
  starting transfers between devices  33.9 us (31%)
  waiting for transfers between devices  29.2 us (27%)
  local copies, waits for them, and re-layouts  27.5 us (25%)
  matrix products  10.2 us (9%)
  other arithmetic  5.56 us (5%)
  between operations  1.77 us (2%)
    ppermute x8, waiting for transfers between devices, butterfly_sum(): lax.ppermute(rows, axis, [(i, i ^ step) for i in range(count)])  26.6 us
    ppermute x8, starting transfers between devices, butterfly_sum(): lax.ppermute(rows, axis, [(i, i ^ step) for i in range(count)])  21.3 us
    unnamed x149, local copies, waits for them, and re-layouts  10.5 us
    ppermute x2, starting transfers between devices, with_halo(): lax.ppermute(tail, axis, [(i, (i + 1) % count) for i in range(ends)])  6.87 us
    mul x2, local copies, waits for them, and re-layouts, merged_grad(): full[..., None] * sel[None, :, None, None, :, :, None, :]  6.35 us
    ppermute x2, starting transfers between devices, with_halo(): lax.ppermute(head, axis, [((i + 1) % count, i) for i in range(ends)])  5.74 us
    dot_general x1, matrix products, shards(): jnp.einsum('qxym,xykm->qk', grad_first.reshape((-1,) + grad_first.shape[2...  3.84 us
    dot_general x1, matrix products, shards(): jnp.einsum('ork,xykm->orxym', merged_kernel(w_first, 4), patches_wide, pr...  3.44 us
  transfers between devices with their start and end apart: 12, of which 9 were waited for; matrix products, arithmetic and copies ran while one was open for 7% of the time, Pallas kernels for 0%

profile of v6, /device:TPU:24, one launch (start us, length us, event | category | flops | bytes accessed | tf_op | source)
XLA Modules:
  0.0 108.2 jit_solution(9002757627752345917)
XLA Ops:
  0.6 1.0 fusion.37
  1.6 1.9 %collective-permute-start = (bf16[4,3,8,512]{3,2,1,0:T(8,128)(2,1)S(1)}, bf16[4,3,8,512]{3,2,1,0:T(8,128)(2,1)S(1)}, u32[]{:S(2)}, u32[]{:S(2)}) collective-permute-start(bf16[4,3,8,512]{3,2,1,0:T(8,128)(2,1)S(1)} %get-tuple-element.45), channel_id=1, source_target_pairs={{0,1},{1,2},{2,3},{3,4},{4,5},{5,6},{6,7},{7,8},{8,9},{9,10},{10,1... | collective-permute-start | bytes 294920 | tf_op jit(solution)/shard_map/ppermute | solution.py:15
  3.6 3.6 %collective-permute-start.1 = (bf16[4,3,8,512]{3,2,1,0:T(8,128)(2,1)S(1)}, bf16[4,3,8,512]{3,2,1,0:T(8,128)(2,1)S(1)}, u32[]{:S(2)}, u32[]{:S(2)}) collective-permute-start(bf16[4,3,8,512]{3,2,1,0:T(8,128)(2,1)S(1)} %get-tuple-element.46), channel_id=1, source_target_pairs={{1,0},{2,1},{3,2},{4,3},{5,4},{6,5},{7,6},{8,7},{9,8},{10,9},{11,1... | collective-permute-start | bytes 294920 | tf_op jit(solution)/shard_map/ppermute | solution.py:17
  7.2 1.8 %copy.91 = bf16[1,4,4,8,512]{3,4,2,1,0:T(8,128)(2,1)S(1)} copy(bf16[1,4,4,8,512]{4,3,2,1,0:T(8,128)(2,1)} %param.8) | data formatting | bytes 262144 | tf_op args[0]
  9.1 0.9 copy.94
  10.3 1.0 multiply_reduce_fusion.1
  18.7 3.4 %divide_multiply_fusion = (f32[16,4,8,8,128]{4,0,3,2,1:T(8,128)S(1)}, f32[16,4,8,8,128]{4,0,3,2,1:T(8,128)}) fusion(f32[16]{0:T(128)S(1)} %copy-done.8, bf16[16,4,432,1,1]{0,2,4,3,1:T(8,128)(2,1)S(1)} %bitcast.127, bf16[8,8,432,128]{3,2,1,0:T(8,128)(2,1)S(1)} %constant_dynamic-update-slice_fusion), kind=kOutput, calls=%fused_computation.10 | convolution fusion | flops 455606272 | bytes 11327552 | tf_op jit(solution)/shard_map/ork,xykm->orxym/dot_general | solution.py:135
  24.3 1.1 %convert_reduce_fusion.1 = (f32[32]{0:T(128)S(1)}, bf16[32,2,2,4,128]{4,0,3,2,1:T(8,128)(2,1)S(1)}, f32[32,4,128]{2,0,1:T(8,128)}) fusion(f32[32,4,128]{2,0,1:T(8,128)S(1)} %bitcast.131, f32[32]{0:T(128)S(1)} %copy-done.9, bf16[32,432,1,1,1]{0,1,4,3,2:T(8,128)(2,1)S(1)} %bitcast.130, bf16[1,2,4,432,128]{4,3,2,1,0:T(8,128)(2,1)S(1)} %bitcast.134, ...), kind=kOutput, calls=%fused_computation.170 | convolution fusion | flops 58408928 | bytes 2059520 | tf_op jit(solution)/shard_map/ok,rxykm->orxym/dot_general | solution.py:52
  25.4 4.9 %collective-permute-start.2 = (bf16[32,2,1,4,128]{4,0,3,2,1:T(8,128)(2,1)S(1)}, bf16[32,2,1,4,128]{4,0,3,2,1:T(8,128)(2,1)S(1)}, u32[]{:S(2)}, u32[]{:S(2)}) collective-permute-start(bf16[32,2,1,4,128]{4,0,3,2,1:T(8,128)(2,1)S(1)} %get-tuple-element.41), channel_id=1, source_target_pairs={{0,1},{1,2},{2,3},{3,4},{4,5},{5,6},{6,7},{7,8},{8,9},{9,10},{10,1... | collective-permute-start | bytes 196616 | tf_op jit(solution)/shard_map/ppermute | solution.py:15
  30.4 2.1 %collective-permute-start.3 = (bf16[32,2,1,4,128]{4,0,3,2,1:T(8,128)(2,1)S(1)}, bf16[32,2,1,4,128]{4,0,3,2,1:T(8,128)(2,1)S(1)}, u32[]{:S(2)}, u32[]{:S(2)}) collective-permute-start(bf16[32,2,1,4,128]{4,0,3,2,1:T(8,128)(2,1)S(1)} %get-tuple-element.42), channel_id=1, source_target_pairs={{1,0},{2,1},{3,2},{4,3},{5,4},{6,5},{7,6},{8,7},{9,8},{10,9},{11,1... | collective-permute-start | bytes 196616 | tf_op jit(solution)/shard_map/ppermute | solution.py:17
  32.5 1.2 %fusion.22 = f32[32,432]{1,0:T(8,128)} fusion(bf16[32,2,2,4,128]{4,0,3,2,1:T(8,128)(2,1)S(1)} %get-tuple-element.26, bf16[1,2,4,432,128]{4,3,2,1,0:T(8,128)(2,1)S(1)} %bitcast.135, bf16[1,2,4,432,128]{4,3,2,1,0:T(8,128)(2,1)S(1)} %bitcast.137), kind=kOutput, calls=%fused_computation.19 | convolution fusion | flops 57507840 | bytes 1955840 | tf_op jit(solution)/shard_map/orxym,rxykm->ok/dot_general | solution.py:56
  33.8 2.6 %collective-permute-done.3 = bf16[32,2,1,4,128]{4,0,3,2,1:T(8,128)(2,1)S(1)} collective-permute-done((bf16[32,2,1,4,128]{4,0,3,2,1:T(8,128)(2,1)S(1)}, bf16[32,2,1,4,128]{4,0,3,2,1:T(8,128)(2,1)S(1)}, u32[]{:S(2)}, u32[]{:S(2)}) %collective-permute-start.3) | collective-permute-done | bytes 65568 | tf_op jit(solution)/shard_map/ppermute | solution.py:17
  39.2 1.4 %copy-done = f32[16,4,8,8,128]{4,0,3,2,1:T(8,128)S(1)} copy-done((f32[16,4,8,8,128]{4,0,3,2,1:T(8,128)S(1)}, f32[16,4,8,8,128]{4,0,3,2,1:T(8,128)}, u32[]{:S(2)}) %copy-start) | copy-done | bytes 2097176
  40.7 1.0 convert_reduce_fusion
  41.9 3.8 %fusion.13 = f32[64,432]{1,0:T(8,128)} fusion(bf16[8,8,432,128]{3,2,1,0:T(8,128)(2,1)} %copy-done.7, bf16[64,4,8,128]{3,2,1,0:T(8,128)(2,1)S(1)} %bitcast.125), kind=kOutput, calls=%fused_computation.16 | convolution fusion | flops 226492416 | bytes 4173824 | tf_op jit(solution)/shard_map/qxym,xykm->qk/dot_general | solution.py:162
  45.7 2.6 %reshape.105 = f32[16,4,3,3,3,4,4]{6,5,4,3,2,1,0:T(4,128)S(1)} reshape(f32[64,432]{1,0:T(8,128)} %fusion.13) | data formatting | bytes 221184 | tf_op jit(solution)/shard_map/mul | solution.py:122
  48.3 3.7 %copy.107 = f32[16,4,3,3,3,4,4]{0,6,5,4,3,2,1:T(4,128)} copy(f32[16,4,3,3,3,4,4]{6,5,4,3,2,1,0:T(4,128)S(1)} %reshape.105) | data formatting | bytes 221184 | tf_op jit(solution)/shard_map/mul | solution.py:122
  52.0 2.0 %multiply_reduce_fusion = f32[16,3,3,4,3]{0,3,4,2,1:T(4,128)S(1)} fusion(f32[16,4,3,3,3,4,4]{0,6,5,4,3,2,1:T(4,128)} %copy.107, f32[4,3,4,3]{3,2,1,0:T(4,128)} %constant.57), kind=kLoop, calls=%fused_computation.8 | loop fusion | flops 164160 | bytes 118080 | tf_op jit(solution)/shard_map/reduce_sum | solution.py:122
  55.2 0.9 pad_maximum_fusion.5
  56.1 6.6 %collective-permute-start.4 = (f32[32,488]{1,0:T(8,128)S(1)}, f32[32,488]{1,0:T(8,128)S(1)}, u32[]{:S(2)}, u32[]{:S(2)}) collective-permute-start(f32[32,488]{1,0:T(8,128)S(1)} %pad_maximum_fusion.5), channel_id=1, source_target_pairs={{0,1},{1,0},{2,3},{3,2},{4,5},{5,4},{6,7},{7,6},{8,9},{9,8},{10,11... | collective-permute-start | bytes 187400 | tf_op jit(solution)/shard_map/ppermute | solution.py:79
  62.7 0.9 collective-permute-done.4
  63.8 4.3 %collective-permute-done.5 = f32[32,488]{1,0:T(8,128)S(1)} collective-permute-done((f32[32,488]{1,0:T(8,128)S(1)}, f32[32,488]{1,0:T(8,128)S(1)}, u32[]{:S(2)}, u32[]{:S(2)}) %collective-permute-start.5) | collective-permute-done | bytes 62496 | tf_op jit(solution)/shard_map/ppermute | solution.py:79
  68.2 5.8 %collective-permute-done.6 = f32[32,488]{1,0:T(8,128)S(1)} collective-permute-done((f32[32,488]{1,0:T(8,128)S(1)}, f32[32,488]{1,0:T(8,128)S(1)}, u32[]{:S(2)}, u32[]{:S(2)}) %collective-permute-start.6) | collective-permute-done | bytes 62496 | tf_op jit(solution)/shard_map/ppermute | solution.py:79
  74.1 5.8 %collective-permute-done.7 = f32[32,488]{1,0:T(8,128)S(1)} collective-permute-done((f32[32,488]{1,0:T(8,128)S(1)}, f32[32,488]{1,0:T(8,128)S(1)}, u32[]{:S(2)}, u32[]{:S(2)}) %collective-permute-start.7) | collective-permute-done | bytes 62496 | tf_op jit(solution)/shard_map/ppermute | solution.py:79
  79.8 2.0 %collective-permute-start.8 = (f32[32,488]{1,0:T(8,128)S(1)}, f32[32,488]{1,0:T(8,128)S(1)}, u32[]{:S(2)}, u32[]{:S(2)}) collective-permute-start(f32[32,488]{1,0:T(8,128)S(1)} %add.94), channel_id=1, source_target_pairs={{0,16},{16,0},{32,48},{48,32},{64,80},{80,64},{96,112},{112,96},{1... | collective-permute-start | bytes 187400 | tf_op jit(solution)/shard_map/ppermute | solution.py:79
  81.9 2.3 %collective-permute-done.8 = f32[32,488]{1,0:T(8,128)S(1)} collective-permute-done((f32[32,488]{1,0:T(8,128)S(1)}, f32[32,488]{1,0:T(8,128)S(1)}, u32[]{:S(2)}, u32[]{:S(2)}) %collective-permute-start.8) | collective-permute-done | bytes 62496 | tf_op jit(solution)/shard_map/ppermute | solution.py:79
  84.2 3.7 %collective-permute-start.9 = (f32[32,488]{1,0:T(8,128)S(1)}, f32[32,488]{1,0:T(8,128)S(1)}, u32[]{:S(2)}, u32[]{:S(2)}) collective-permute-start(f32[32,488]{1,0:T(8,128)S(1)} %add.95), channel_id=1, source_target_pairs={{0,32},{16,48},{32,0},{48,16},{64,96},{80,112},{96,64},{112,80},{1... | collective-permute-start | bytes 187400 | tf_op jit(solution)/shard_map/ppermute | solution.py:79
  87.9 2.2 %collective-permute-done.9 = f32[32,488]{1,0:T(8,128)S(1)} collective-permute-done((f32[32,488]{1,0:T(8,128)S(1)}, f32[32,488]{1,0:T(8,128)S(1)}, u32[]{:S(2)}, u32[]{:S(2)}) %collective-permute-start.9) | collective-permute-done | bytes 62496 | tf_op jit(solution)/shard_map/ppermute | solution.py:79
  90.2 8.1 %collective-permute-start.10 = (f32[32,488]{1,0:T(8,128)S(1)}, f32[32,488]{1,0:T(8,128)S(1)}, u32[]{:S(2)}, u32[]{:S(2)}) collective-permute-start(f32[32,488]{1,0:T(8,128)S(1)} %add.96), channel_id=1, source_target_pairs={{0,64},{16,80},{32,96},{48,112},{64,0},{80,16},{96,32},{112,48},{1... | collective-permute-start | bytes 187400 | tf_op jit(solution)/shard_map/ppermute | solution.py:79
  98.3 2.2 %collective-permute-done.10 = f32[32,488]{1,0:T(8,128)S(1)} collective-permute-done((f32[32,488]{1,0:T(8,128)S(1)}, f32[32,488]{1,0:T(8,128)S(1)}, u32[]{:S(2)}, u32[]{:S(2)}) %collective-permute-start.10) | collective-permute-done | bytes 62496 | tf_op jit(solution)/shard_map/ppermute | solution.py:79
  101.8 3.0 %collective-permute-done.11 = f32[32,488]{1,0:T(8,128)S(1)} collective-permute-done((f32[32,488]{1,0:T(8,128)S(1)}, f32[32,488]{1,0:T(8,128)S(1)}, u32[]{:S(2)}, u32[]{:S(2)}) %collective-permute-start.11) | collective-permute-done | bytes 62496 | tf_op jit(solution)/shard_map/ppermute | solution.py:79
  106.5 0.9 copy.113
  (210 shorter events, 17.3 us)
Async XLA Ops:
  1.6 9.7 %collective-permute-start = (bf16[4,3,8,512]{3,2,1,0:T(8,128)(2,1)S(1)}, bf16[4,3,8,512]{3,2,1,0:T(8,128)(2,1)S(1)}, u32[]{:S(2)}, u32[]{:S(2)}) collective-permute-start(bf16[4,3,8,512]{3,2,1,0:T(8,128)(2,1)S(1)} %get-tuple-element.45), channel_id=1, source_target_pairs={{0,1},{1,2},{2,3},{3,4},{4,5},{5,6},{6,7},{7,8},{8,9},{9,10},{10,1... | collective-permute-start | bytes 294920 | tf_op jit(solution)/shard_map/ppermute | solution.py:15
  3.6 6.4 %copy-start.5 = (bf16[16,4,3,3,3]{0,1,4,3,2:T(4,128)(2,1)S(1)}, bf16[16,4,3,3,3]{0,1,4,3,2:T(4,128)(2,1)}, u32[]{:S(2)}) copy-start(bf16[16,4,3,3,3]{0,1,4,3,2:T(4,128)(2,1)} %param.10) | copy-start | bytes 10372
  3.6 6.5 %copy-start.6 = (bf16[1,32,1,2,128]{4,3,2,1,0:T(2,128)(2,1)S(1)}, bf16[1,32,1,2,128]{4,3,2,1,0:T(2,128)(2,1)}, u32[]{:S(2)}) copy-start(bf16[1,32,1,2,128]{4,3,2,1,0:T(2,128)(2,1)} %param.9) | copy-start | bytes 49156
  3.6 9.3 %collective-permute-start.1 = (bf16[4,3,8,512]{3,2,1,0:T(8,128)(2,1)S(1)}, bf16[4,3,8,512]{3,2,1,0:T(8,128)(2,1)S(1)}, u32[]{:S(2)}, u32[]{:S(2)}) collective-permute-start(bf16[4,3,8,512]{3,2,1,0:T(8,128)(2,1)S(1)} %get-tuple-element.46), channel_id=1, source_target_pairs={{1,0},{2,1},{3,2},{4,3},{5,4},{6,5},{7,6},{8,7},{9,8},{10,9},{11,1... | collective-permute-start | bytes 294920 | tf_op jit(solution)/shard_map/ppermute | solution.py:17
  9.1 1.0 copy-start.2
  9.1 1.2 %copy-start.3 = (f32[4,3,4,3]{3,2,1,0:T(4,128)S(1)}, f32[4,3,4,3]{3,2,1,0:T(4,128)}, u32[]{:S(2)}) copy-start(f32[4,3,4,3]{3,2,1,0:T(4,128)} %constant.57) | copy-start | bytes 1732
  17.9 0.7 copy-start.8
  18.6 3.5 %copy-start.7 = (bf16[8,8,432,128]{3,2,1,0:T(8,128)(2,1)}, bf16[8,8,432,128]{3,2,1,0:T(8,128)(2,1)S(1)}, u32[]{:S(2)}) copy-start(bf16[8,8,432,128]{3,2,1,0:T(8,128)(2,1)S(1)} %constant_dynamic-update-slice_fusion) | copy-start | bytes 21233668
  23.3 1.0 copy-start.9
  25.4 8.4 %collective-permute-start.2 = (bf16[32,2,1,4,128]{4,0,3,2,1:T(8,128)(2,1)S(1)}, bf16[32,2,1,4,128]{4,0,3,2,1:T(8,128)(2,1)S(1)}, u32[]{:S(2)}, u32[]{:S(2)}) collective-permute-start(bf16[32,2,1,4,128]{4,0,3,2,1:T(8,128)(2,1)S(1)} %get-tuple-element.41), channel_id=1, source_target_pairs={{0,1},{1,2},{2,3},{3,4},{4,5},{5,6},{6,7},{7,8},{8,9},{9,10},{10,1... | collective-permute-start | bytes 196616 | tf_op jit(solution)/shard_map/ppermute | solution.py:15
  30.4 6.0 %collective-permute-start.3 = (bf16[32,2,1,4,128]{4,0,3,2,1:T(8,128)(2,1)S(1)}, bf16[32,2,1,4,128]{4,0,3,2,1:T(8,128)(2,1)S(1)}, u32[]{:S(2)}, u32[]{:S(2)}) collective-permute-start(bf16[32,2,1,4,128]{4,0,3,2,1:T(8,128)(2,1)S(1)} %get-tuple-element.42), channel_id=1, source_target_pairs={{1,0},{2,1},{3,2},{4,3},{5,4},{6,5},{7,6},{8,7},{9,8},{10,9},{11,1... | collective-permute-start | bytes 196616 | tf_op jit(solution)/shard_map/ppermute | solution.py:17
  39.1 1.6 %copy-start = (f32[16,4,8,8,128]{4,0,3,2,1:T(8,128)S(1)}, f32[16,4,8,8,128]{4,0,3,2,1:T(8,128)}, u32[]{:S(2)}) copy-start(f32[16,4,8,8,128]{4,0,3,2,1:T(8,128)} %get-tuple-element.52) | copy-start | bytes 6291460
  52.0 11.6 %copy-start.1 = (f32[32,432]{1,0:T(8,128)S(1)}, f32[32,432]{1,0:T(8,128)}, u32[]{:S(2)}) copy-start(f32[32,432]{1,0:T(8,128)} %fusion.22) | copy-start | bytes 165892
  52.0 46.2 %copy-start.4 = (f32[32,4,128]{2,0,1:T(8,128)S(1)}, f32[32,4,128]{2,0,1:T(8,128)}, u32[]{:S(2)}) copy-start(f32[32,4,128]{2,0,1:T(8,128)} %get-tuple-element.36) | copy-start | bytes 196612
  56.1 7.5 %collective-permute-start.4 = (f32[32,488]{1,0:T(8,128)S(1)}, f32[32,488]{1,0:T(8,128)S(1)}, u32[]{:S(2)}, u32[]{:S(2)}) collective-permute-start(f32[32,488]{1,0:T(8,128)S(1)} %pad_maximum_fusion.5), channel_id=1, source_target_pairs={{0,1},{1,0},{2,3},{3,2},{4,5},{5,4},{6,7},{7,6},{8,9},{9,8},{10,11... | collective-permute-start | bytes 187400 | tf_op jit(solution)/shard_map/ppermute | solution.py:79
  63.7 4.4 %collective-permute-start.5 = (f32[32,488]{1,0:T(8,128)S(1)}, f32[32,488]{1,0:T(8,128)S(1)}, u32[]{:S(2)}, u32[]{:S(2)}) collective-permute-start(f32[32,488]{1,0:T(8,128)S(1)} %fusion.41), channel_id=1, source_target_pairs={{0,2},{1,3},{2,0},{3,1},{4,6},{5,7},{6,4},{7,5},{8,10},{9,11},{10,... | collective-permute-start | bytes 187400 | tf_op jit(solution)/shard_map/ppermute | solution.py:79
  68.1 5.9 %collective-permute-start.6 = (f32[32,488]{1,0:T(8,128)S(1)}, f32[32,488]{1,0:T(8,128)S(1)}, u32[]{:S(2)}, u32[]{:S(2)}) collective-permute-start(f32[32,488]{1,0:T(8,128)S(1)} %add.92), channel_id=1, source_target_pairs={{0,4},{1,5},{2,6},{3,7},{4,0},{5,1},{6,2},{7,3},{8,12},{9,13},{10,... | collective-permute-start | bytes 187400 | tf_op jit(solution)/shard_map/ppermute | solution.py:79
  74.0 5.9 %collective-permute-start.7 = (f32[32,488]{1,0:T(8,128)S(1)}, f32[32,488]{1,0:T(8,128)S(1)}, u32[]{:S(2)}, u32[]{:S(2)}) collective-permute-start(f32[32,488]{1,0:T(8,128)S(1)} %add.93), channel_id=1, source_target_pairs={{0,8},{1,9},{2,10},{3,11},{4,12},{5,13},{6,14},{7,15},{8,0},{9,1},... | collective-permute-start | bytes 187400 | tf_op jit(solution)/shard_map/ppermute | solution.py:79
  79.8 4.4 %collective-permute-start.8 = (f32[32,488]{1,0:T(8,128)S(1)}, f32[32,488]{1,0:T(8,128)S(1)}, u32[]{:S(2)}, u32[]{:S(2)}) collective-permute-start(f32[32,488]{1,0:T(8,128)S(1)} %add.94), channel_id=1, source_target_pairs={{0,16},{16,0},{32,48},{48,32},{64,80},{80,64},{96,112},{112,96},{1... | collective-permute-start | bytes 187400 | tf_op jit(solution)/shard_map/ppermute | solution.py:79
  84.2 6.0 %collective-permute-start.9 = (f32[32,488]{1,0:T(8,128)S(1)}, f32[32,488]{1,0:T(8,128)S(1)}, u32[]{:S(2)}, u32[]{:S(2)}) collective-permute-start(f32[32,488]{1,0:T(8,128)S(1)} %add.95), channel_id=1, source_target_pairs={{0,32},{16,48},{32,0},{48,16},{64,96},{80,112},{96,64},{112,80},{1... | collective-permute-start | bytes 187400 | tf_op jit(solution)/shard_map/ppermute | solution.py:79
  90.2 10.3 %collective-permute-start.10 = (f32[32,488]{1,0:T(8,128)S(1)}, f32[32,488]{1,0:T(8,128)S(1)}, u32[]{:S(2)}, u32[]{:S(2)}) collective-permute-start(f32[32,488]{1,0:T(8,128)S(1)} %add.96), channel_id=1, source_target_pairs={{0,64},{16,80},{32,96},{48,112},{64,0},{80,16},{96,32},{112,48},{1... | collective-permute-start | bytes 187400 | tf_op jit(solution)/shard_map/ppermute | solution.py:79
  100.5 4.4 %collective-permute-start.11 = (f32[32,488]{1,0:T(8,128)S(1)}, f32[32,488]{1,0:T(8,128)S(1)}, u32[]{:S(2)}, u32[]{:S(2)}) collective-permute-start(f32[32,488]{1,0:T(8,128)S(1)} %add.97), channel_id=1, source_target_pairs={{0,128},{16,144},{32,160},{48,176},{64,192},{80,208},{96,224},{112... | collective-permute-start | bytes 187400 | tf_op jit(solution)/shard_map/ppermute | solution.py:79

commit v7 on v5

--- a/solution.py
+++ b/solution.py
@@ -66,8 +66,16 @@
     return jnp.repeat(jnp.repeat(jnp.repeat(field, 2, axis=1), 2, axis=2), 2, axis=3)
 
 
+def sigmoid(value):
+    return 0.5 + 0.5 * jnp.tanh(0.5 * value)
+
+
+def silu(value):
+    return value * sigmoid(value)
+
+
 def silu_slope(value):
-    sig = jax.nn.sigmoid(value)
+    sig = sigmoid(value)
     return sig * (1.0 + value * (1.0 - sig))
 
 
@@ -137,7 +145,7 @@
         )
         + b_first[:, None, None, None, None]
     )
-    pooled_wide = pool(jax.nn.silu(pre_wide)).astype(jnp.bfloat16)
+    pooled_wide = pool(silu(pre_wide)).astype(jnp.bfloat16)
     place = lax.axis_index("space")
     rows = jnp.arange(pooled_wide.shape[2])
     inside = ((rows > 0) | (place > 0)) & ((rows < pooled_wide.shape[2] - 1) | (place < lax.axis_size("space") - 1))
@@ -147,7 +155,7 @@
     patches_first = patches_wide[2 : 2 + depth]
     patches_second = phase_patches(pooled_halo)
     pre_second = conv_taps(tap_major(w_second), patches_second) + b_second[:, None, None, None, None]
-    output = pool(jax.nn.silu(pre_second))[:, 0].astype(jnp.bfloat16)
+    output = pool(silu(pre_second))[:, 0].astype(jnp.bfloat16)
     grad_second = (
         upsample(cot.astype(jnp.float32)[:, None], 2) * 0.125 * silu_slope(pre_second)
     ).astype(jnp.bfloat16)

time: 98.5 us -> 98.5 us (level)
  no operation moved by 1% of the time
where the time goes in v7:
time: 98.5 us; the launch traced here: 98.1 us
  starting transfers between devices  33.9 us (34%)
  waiting for transfers between devices  29.9 us (30%)
  local copies, waits for them, and re-layouts  20.5 us (21%)
  matrix products  9.1 us (9%)
  other arithmetic  2.94 us (3%)
  between operations  1.78 us (2%)
    ppermute x8, waiting for transfers between devices, butterfly_sum(): lax.ppermute(rows, axis, [(i, i ^ step) for i in range(count)])  26.6 us
    ppermute x8, starting transfers between devices, butterfly_sum(): lax.ppermute(rows, axis, [(i, i ^ step) for i in range(count)])  21.3 us
    unnamed x145, local copies, waits for them, and re-layouts  10.6 us
    ppermute x2, starting transfers between devices, with_halo(): lax.ppermute(tail, axis, [(i, (i + 1) % count) for i in range(ends)])  6.87 us
    ppermute x2, starting transfers between devices, with_halo(): lax.ppermute(head, axis, [((i + 1) % count, i) for i in range(ends)])  5.74 us
    dot_general x1, matrix products, shards(): jnp.einsum('orxym,xykm->ork', grad_first, patches_first, preferred_elemen...  3.98 us
    dot_general x1, matrix products, shards(): jnp.einsum('ork,xykm->orxym', merged_kernel(w_first, 4), patches_wide, pr...  3.35 us
    ppermute x2, waiting for transfers between devices, with_halo(): lax.ppermute(head, axis, [((i + 1) % count, i) for i in range(ends)])  3.22 us
  transfers between devices with their start and end apart: 12, of which 9 were waited for; matrix products, arithmetic and copies ran while one was open for 7% of the time, Pallas kernels for 0%

profile of v7, /device:TPU:24, one launch (start us, length us, event | category | flops | bytes accessed | tf_op | source)
XLA Modules:
  0.0 98.1 jit_solution(15228317935187507263)
XLA Ops:
  0.6 1.0 %fusion.32 = (bf16[4,3,8,512]{3,2,1,0:T(8,128)(2,1)S(1)}, bf16[4,3,8,512]{3,2,1,0:T(8,128)(2,1)S(1)}) fusion(bf16[4,4,8,512]{3,2,1,0:T(8,128)(2,1)} %bitcast.133), kind=kLoop, calls=%fused_computation.198 | loop fusion | bytes 393216 | tf_op jit(solution)/shard_map/slice | solution.py:12
  1.6 1.9 %collective-permute-start = (bf16[4,3,8,512]{3,2,1,0:T(8,128)(2,1)S(1)}, bf16[4,3,8,512]{3,2,1,0:T(8,128)(2,1)S(1)}, u32[]{:S(2)}, u32[]{:S(2)}) collective-permute-start(bf16[4,3,8,512]{3,2,1,0:T(8,128)(2,1)S(1)} %get-tuple-element.45), channel_id=1, source_target_pairs={{0,1},{1,2},{2,3},{3,4},{4,5},{5,6},{6,7},{7,8},{8,9},{9,10},{10,1... | collective-permute-start | bytes 294920 | tf_op jit(solution)/shard_map/ppermute | solution.py:15
  3.6 3.6 %collective-permute-start.1 = (bf16[4,3,8,512]{3,2,1,0:T(8,128)(2,1)S(1)}, bf16[4,3,8,512]{3,2,1,0:T(8,128)(2,1)S(1)}, u32[]{:S(2)}, u32[]{:S(2)}) collective-permute-start(bf16[4,3,8,512]{3,2,1,0:T(8,128)(2,1)S(1)} %get-tuple-element.46), channel_id=1, source_target_pairs={{1,0},{2,1},{3,2},{4,3},{5,4},{6,5},{7,6},{8,7},{9,8},{10,9},{11,1... | collective-permute-start | bytes 294920 | tf_op jit(solution)/shard_map/ppermute | solution.py:17
  7.2 1.8 %copy.88 = bf16[1,4,4,8,512]{3,4,2,1,0:T(8,128)(2,1)S(1)} copy(bf16[1,4,4,8,512]{4,3,2,1,0:T(8,128)(2,1)} %param.8) | data formatting | bytes 262144 | tf_op args[0]
  9.1 0.9 copy.91
  10.3 1.0 %multiply_reduce_fusion.1 = bf16[16,4,3,3,3,4,4]{0,6,5,4,3,2,1:T(4,128)(2,1)S(1)} fusion(f32[4,3,4,3]{3,2,1,0:T(4,128)S(1)} %copy-done.2, f32[16,3,3,4,3]{0,3,4,2,1:T(4,128)S(1)} %convert_bitcast_fusion), kind=kLoop, calls=%fused_computation.9 | loop fusion | flops 138240 | bytes 62784 | tf_op jit(solution)/shard_map/reduce_sum | solution.py:124
  11.3 0.8 copy.87
  12.1 0.7 copy.90
  12.8 0.8 copy.89
  18.7 3.4 %add_multiply_fusion = (f32[16,4,8,8,128]{4,0,3,2,1:T(8,128)S(1)}, f32[16,4,8,8,128]{4,0,3,2,1:T(8,128)}) fusion(f32[16]{0:T(128)S(1)} %copy-done.6, bf16[16,4,432,1,1]{0,2,4,3,1:T(8,128)(2,1)S(1)} %bitcast.135, bf16[8,8,432,128]{3,2,1,0:T(8,128)(2,1)S(1)} %constant_dynamic-update-slice_fusion), kind=kOutput, calls=%fused_computation.10 | convolution fusion | flops 455606272 | bytes 11327552 | tf_op jit(solution)/shard_map/ork,xykm->orxym/dot_general | solution.py:143
  24.9 5.0 %collective-permute-start.2 = (bf16[32,2,1,4,128]{4,0,3,2,1:T(8,128)(2,1)S(1)}, bf16[32,2,1,4,128]{4,0,3,2,1:T(8,128)(2,1)S(1)}, u32[]{:S(2)}, u32[]{:S(2)}) collective-permute-start(bf16[32,2,1,4,128]{4,0,3,2,1:T(8,128)(2,1)S(1)} %get-tuple-element.41), channel_id=1, source_target_pairs={{0,1},{1,2},{2,3},{3,4},{4,5},{5,6},{6,7},{7,8},{8,9},{9,10},{10,1... | collective-permute-start | bytes 196616 | tf_op jit(solution)/shard_map/ppermute | solution.py:15
  29.9 2.1 %collective-permute-start.3 = (bf16[32,2,1,4,128]{4,0,3,2,1:T(8,128)(2,1)S(1)}, bf16[32,2,1,4,128]{4,0,3,2,1:T(8,128)(2,1)S(1)}, u32[]{:S(2)}, u32[]{:S(2)}) collective-permute-start(bf16[32,2,1,4,128]{4,0,3,2,1:T(8,128)(2,1)S(1)} %get-tuple-element.42), channel_id=1, source_target_pairs={{1,0},{2,1},{3,2},{4,3},{5,4},{6,5},{7,6},{8,7},{9,8},{10,9},{11,1... | collective-permute-start | bytes 196616 | tf_op jit(solution)/shard_map/ppermute | solution.py:17
  32.6 3.2 %collective-permute-done.3 = bf16[32,2,1,4,128]{4,0,3,2,1:T(8,128)(2,1)S(1)} collective-permute-done((bf16[32,2,1,4,128]{4,0,3,2,1:T(8,128)(2,1)S(1)}, bf16[32,2,1,4,128]{4,0,3,2,1:T(8,128)(2,1)S(1)}, u32[]{:S(2)}, u32[]{:S(2)}) %collective-permute-start.3) | collective-permute-done | bytes 65568 | tf_op jit(solution)/shard_map/ppermute | solution.py:17
  38.7 1.4 %copy-done = f32[16,4,8,8,128]{4,0,3,2,1:T(8,128)S(1)} copy-done((f32[16,4,8,8,128]{4,0,3,2,1:T(8,128)S(1)}, f32[16,4,8,8,128]{4,0,3,2,1:T(8,128)}, u32[]{:S(2)}) %copy-start) | copy-done | bytes 2097176
  40.6 4.0 %fusion.2 = f32[16,4,432,1,1]{0,2,4,3,1:T(8,128)S(1)} fusion(bf16[16,4,4,8,128]{4,0,3,2,1:T(8,128)(2,1)S(1)} %get-tuple-element.28, bf16[8,8,432,128]{3,2,1,0:T(8,128)(2,1)} %copy-done.5), kind=kOutput, calls=%fused_computation.3 | convolution fusion | flops 226492416 | bytes 4173824 | tf_op jit(solution)/shard_map/orxym,xykm->ork/dot_general | solution.py:169
  44.6 0.8 multiply_reduce_fusion
  46.0 6.6 %collective-permute-start.4 = (f32[32,488]{1,0:T(8,128)S(1)}, f32[32,488]{1,0:T(8,128)S(1)}, u32[]{:S(2)}, u32[]{:S(2)}) collective-permute-start(f32[32,488]{1,0:T(8,128)S(1)} %pad_maximum_fusion.5), channel_id=1, source_target_pairs={{0,1},{1,0},{2,3},{3,2},{4,5},{5,4},{6,7},{7,6},{8,9},{9,8},{10,11... | collective-permute-start | bytes 187400 | tf_op jit(solution)/shard_map/ppermute | solution.py:87
  52.6 0.9 collective-permute-done.4
  53.6 4.3 %collective-permute-done.5 = f32[32,488]{1,0:T(8,128)S(1)} collective-permute-done((f32[32,488]{1,0:T(8,128)S(1)}, f32[32,488]{1,0:T(8,128)S(1)}, u32[]{:S(2)}, u32[]{:S(2)}) %collective-permute-start.5) | collective-permute-done | bytes 62496 | tf_op jit(solution)/shard_map/ppermute | solution.py:87
  58.1 5.8 %collective-permute-done.6 = f32[32,488]{1,0:T(8,128)S(1)} collective-permute-done((f32[32,488]{1,0:T(8,128)S(1)}, f32[32,488]{1,0:T(8,128)S(1)}, u32[]{:S(2)}, u32[]{:S(2)}) %collective-permute-start.6) | collective-permute-done | bytes 62496 | tf_op jit(solution)/shard_map/ppermute | solution.py:87
  63.9 5.8 %collective-permute-done.7 = f32[32,488]{1,0:T(8,128)S(1)} collective-permute-done((f32[32,488]{1,0:T(8,128)S(1)}, f32[32,488]{1,0:T(8,128)S(1)}, u32[]{:S(2)}, u32[]{:S(2)}) %collective-permute-start.7) | collective-permute-done | bytes 62496 | tf_op jit(solution)/shard_map/ppermute | solution.py:87
  69.7 2.0 %collective-permute-start.8 = (f32[32,488]{1,0:T(8,128)S(1)}, f32[32,488]{1,0:T(8,128)S(1)}, u32[]{:S(2)}, u32[]{:S(2)}) collective-permute-start(f32[32,488]{1,0:T(8,128)S(1)} %add.92), channel_id=1, source_target_pairs={{0,16},{16,0},{32,48},{48,32},{64,80},{80,64},{96,112},{112,96},{1... | collective-permute-start | bytes 187400 | tf_op jit(solution)/shard_map/ppermute | solution.py:87
  71.7 2.3 %collective-permute-done.8 = f32[32,488]{1,0:T(8,128)S(1)} collective-permute-done((f32[32,488]{1,0:T(8,128)S(1)}, f32[32,488]{1,0:T(8,128)S(1)}, u32[]{:S(2)}, u32[]{:S(2)}) %collective-permute-start.8) | collective-permute-done | bytes 62496 | tf_op jit(solution)/shard_map/ppermute | solution.py:87
  74.1 3.7 %collective-permute-start.9 = (f32[32,488]{1,0:T(8,128)S(1)}, f32[32,488]{1,0:T(8,128)S(1)}, u32[]{:S(2)}, u32[]{:S(2)}) collective-permute-start(f32[32,488]{1,0:T(8,128)S(1)} %add.93), channel_id=1, source_target_pairs={{0,32},{16,48},{32,0},{48,16},{64,96},{80,112},{96,64},{112,80},{1... | collective-permute-start | bytes 187400 | tf_op jit(solution)/shard_map/ppermute | solution.py:87
  77.8 2.2 %collective-permute-done.9 = f32[32,488]{1,0:T(8,128)S(1)} collective-permute-done((f32[32,488]{1,0:T(8,128)S(1)}, f32[32,488]{1,0:T(8,128)S(1)}, u32[]{:S(2)}, u32[]{:S(2)}) %collective-permute-start.9) | collective-permute-done | bytes 62496 | tf_op jit(solution)/shard_map/ppermute | solution.py:87
  80.1 8.1 %collective-permute-start.10 = (f32[32,488]{1,0:T(8,128)S(1)}, f32[32,488]{1,0:T(8,128)S(1)}, u32[]{:S(2)}, u32[]{:S(2)}) collective-permute-start(f32[32,488]{1,0:T(8,128)S(1)} %add.94), channel_id=1, source_target_pairs={{0,64},{16,80},{32,96},{48,112},{64,0},{80,16},{96,32},{112,48},{1... | collective-permute-start | bytes 187400 | tf_op jit(solution)/shard_map/ppermute | solution.py:87
  88.1 2.2 %collective-permute-done.10 = f32[32,488]{1,0:T(8,128)S(1)} collective-permute-done((f32[32,488]{1,0:T(8,128)S(1)}, f32[32,488]{1,0:T(8,128)S(1)}, u32[]{:S(2)}, u32[]{:S(2)}) %collective-permute-start.10) | collective-permute-done | bytes 62496 | tf_op jit(solution)/shard_map/ppermute | solution.py:87
  91.7 3.1 %collective-permute-done.11 = f32[32,488]{1,0:T(8,128)S(1)} collective-permute-done((f32[32,488]{1,0:T(8,128)S(1)}, f32[32,488]{1,0:T(8,128)S(1)}, u32[]{:S(2)}, u32[]{:S(2)}) %collective-permute-start.11) | collective-permute-done | bytes 62496 | tf_op jit(solution)/shard_map/ppermute | solution.py:87
  94.8 0.7 slice_reduce_fusion
  95.5 0.7 slice_reduce_fusion.1
  96.4 0.9 copy.108
  97.3 0.8 copy.106
  (203 shorter events, 13.9 us)
Async XLA Ops:
  1.6 9.7 %collective-permute-start = (bf16[4,3,8,512]{3,2,1,0:T(8,128)(2,1)S(1)}, bf16[4,3,8,512]{3,2,1,0:T(8,128)(2,1)S(1)}, u32[]{:S(2)}, u32[]{:S(2)}) collective-permute-start(bf16[4,3,8,512]{3,2,1,0:T(8,128)(2,1)S(1)} %get-tuple-element.45), channel_id=1, source_target_pairs={{0,1},{1,2},{2,3},{3,4},{4,5},{5,6},{6,7},{7,8},{8,9},{9,10},{10,1... | collective-permute-start | bytes 294920 | tf_op jit(solution)/shard_map/ppermute | solution.py:15
  3.6 6.4 %copy-start.3 = (bf16[16,4,3,3,3]{0,1,4,3,2:T(4,128)(2,1)S(1)}, bf16[16,4,3,3,3]{0,1,4,3,2:T(4,128)(2,1)}, u32[]{:S(2)}) copy-start(bf16[16,4,3,3,3]{0,1,4,3,2:T(4,128)(2,1)} %param.10) | copy-start | bytes 10372
  3.6 6.5 %copy-start.4 = (bf16[1,32,1,2,128]{4,3,2,1,0:T(2,128)(2,1)S(1)}, bf16[1,32,1,2,128]{4,3,2,1,0:T(2,128)(2,1)}, u32[]{:S(2)}) copy-start(bf16[1,32,1,2,128]{4,3,2,1,0:T(2,128)(2,1)} %param.9) | copy-start | bytes 49156
  3.6 9.3 %collective-permute-start.1 = (bf16[4,3,8,512]{3,2,1,0:T(8,128)(2,1)S(1)}, bf16[4,3,8,512]{3,2,1,0:T(8,128)(2,1)S(1)}, u32[]{:S(2)}, u32[]{:S(2)}) collective-permute-start(bf16[4,3,8,512]{3,2,1,0:T(8,128)(2,1)S(1)} %get-tuple-element.46), channel_id=1, source_target_pairs={{1,0},{2,1},{3,2},{4,3},{5,4},{6,5},{7,6},{8,7},{9,8},{10,9},{11,1... | collective-permute-start | bytes 294920 | tf_op jit(solution)/shard_map/ppermute | solution.py:17
  9.1 1.0 %copy-start.1 = (bf16[32,16,3,3,3]{0,1,4,3,2:T(8,128)(2,1)S(1)}, bf16[32,16,3,3,3]{0,1,4,3,2:T(8,128)(2,1)}, u32[]{:S(2)}) copy-start(bf16[32,16,3,3,3]{0,1,4,3,2:T(8,128)(2,1)} %param.12) | copy-start | bytes 82948
  9.1 1.2 %copy-start.2 = (f32[4,3,4,3]{3,2,1,0:T(4,128)S(1)}, f32[4,3,4,3]{3,2,1,0:T(4,128)}, u32[]{:S(2)}) copy-start(f32[4,3,4,3]{3,2,1,0:T(4,128)} %constant.57) | copy-start | bytes 1732
  17.9 0.7 copy-start.6
  18.6 3.5 %copy-start.5 = (bf16[8,8,432,128]{3,2,1,0:T(8,128)(2,1)}, bf16[8,8,432,128]{3,2,1,0:T(8,128)(2,1)S(1)}, u32[]{:S(2)}) copy-start(bf16[8,8,432,128]{3,2,1,0:T(8,128)(2,1)S(1)} %constant_dynamic-update-slice_fusion) | copy-start | bytes 21233668
  23.3 1.0 %copy-start.7 = (f32[32]{0:T(128)S(1)}, f32[32]{0:T(128)}, u32[]{:S(2)}) copy-start(f32[32]{0:T(128)} %param.13) | copy-start | bytes 388
  24.9 7.8 %collective-permute-start.2 = (bf16[32,2,1,4,128]{4,0,3,2,1:T(8,128)(2,1)S(1)}, bf16[32,2,1,4,128]{4,0,3,2,1:T(8,128)(2,1)S(1)}, u32[]{:S(2)}, u32[]{:S(2)}) collective-permute-start(bf16[32,2,1,4,128]{4,0,3,2,1:T(8,128)(2,1)S(1)} %get-tuple-element.41), channel_id=1, source_target_pairs={{0,1},{1,2},{2,3},{3,4},{4,5},{5,6},{6,7},{7,8},{8,9},{9,10},{10,1... | collective-permute-start | bytes 196616 | tf_op jit(solution)/shard_map/ppermute | solution.py:15
  29.9 6.0 %collective-permute-start.3 = (bf16[32,2,1,4,128]{4,0,3,2,1:T(8,128)(2,1)S(1)}, bf16[32,2,1,4,128]{4,0,3,2,1:T(8,128)(2,1)S(1)}, u32[]{:S(2)}, u32[]{:S(2)}) collective-permute-start(bf16[32,2,1,4,128]{4,0,3,2,1:T(8,128)(2,1)S(1)} %get-tuple-element.42), channel_id=1, source_target_pairs={{1,0},{2,1},{3,2},{4,3},{5,4},{6,5},{7,6},{8,7},{9,8},{10,9},{11,1... | collective-permute-start | bytes 196616 | tf_op jit(solution)/shard_map/ppermute | solution.py:17
  38.5 1.6 %copy-start = (f32[16,4,8,8,128]{4,0,3,2,1:T(8,128)S(1)}, f32[16,4,8,8,128]{4,0,3,2,1:T(8,128)}, u32[]{:S(2)}) copy-start(f32[16,4,8,8,128]{4,0,3,2,1:T(8,128)} %get-tuple-element.52) | copy-start | bytes 6291460
  46.0 7.5 %collective-permute-start.4 = (f32[32,488]{1,0:T(8,128)S(1)}, f32[32,488]{1,0:T(8,128)S(1)}, u32[]{:S(2)}, u32[]{:S(2)}) collective-permute-start(f32[32,488]{1,0:T(8,128)S(1)} %pad_maximum_fusion.5), channel_id=1, source_target_pairs={{0,1},{1,0},{2,3},{3,2},{4,5},{5,4},{6,7},{7,6},{8,9},{9,8},{10,11... | collective-permute-start | bytes 187400 | tf_op jit(solution)/shard_map/ppermute | solution.py:87
  53.6 4.4 %collective-permute-start.5 = (f32[32,488]{1,0:T(8,128)S(1)}, f32[32,488]{1,0:T(8,128)S(1)}, u32[]{:S(2)}, u32[]{:S(2)}) collective-permute-start(f32[32,488]{1,0:T(8,128)S(1)} %fusion.37), channel_id=1, source_target_pairs={{0,2},{1,3},{2,0},{3,1},{4,6},{5,7},{6,4},{7,5},{8,10},{9,11},{10,... | collective-permute-start | bytes 187400 | tf_op jit(solution)/shard_map/ppermute | solution.py:87
  58.0 5.9 %collective-permute-start.6 = (f32[32,488]{1,0:T(8,128)S(1)}, f32[32,488]{1,0:T(8,128)S(1)}, u32[]{:S(2)}, u32[]{:S(2)}) collective-permute-start(f32[32,488]{1,0:T(8,128)S(1)} %add.90), channel_id=1, source_target_pairs={{0,4},{1,5},{2,6},{3,7},{4,0},{5,1},{6,2},{7,3},{8,12},{9,13},{10,... | collective-permute-start | bytes 187400 | tf_op jit(solution)/shard_map/ppermute | solution.py:87
  63.8 5.9 %collective-permute-start.7 = (f32[32,488]{1,0:T(8,128)S(1)}, f32[32,488]{1,0:T(8,128)S(1)}, u32[]{:S(2)}, u32[]{:S(2)}) collective-permute-start(f32[32,488]{1,0:T(8,128)S(1)} %add.91), channel_id=1, source_target_pairs={{0,8},{1,9},{2,10},{3,11},{4,12},{5,13},{6,14},{7,15},{8,0},{9,1},... | collective-permute-start | bytes 187400 | tf_op jit(solution)/shard_map/ppermute | solution.py:87
  69.7 4.4 %collective-permute-start.8 = (f32[32,488]{1,0:T(8,128)S(1)}, f32[32,488]{1,0:T(8,128)S(1)}, u32[]{:S(2)}, u32[]{:S(2)}) collective-permute-start(f32[32,488]{1,0:T(8,128)S(1)} %add.92), channel_id=1, source_target_pairs={{0,16},{16,0},{32,48},{48,32},{64,80},{80,64},{96,112},{112,96},{1... | collective-permute-start | bytes 187400 | tf_op jit(solution)/shard_map/ppermute | solution.py:87
  74.1 6.0 %collective-permute-start.9 = (f32[32,488]{1,0:T(8,128)S(1)}, f32[32,488]{1,0:T(8,128)S(1)}, u32[]{:S(2)}, u32[]{:S(2)}) collective-permute-start(f32[32,488]{1,0:T(8,128)S(1)} %add.93), channel_id=1, source_target_pairs={{0,32},{16,48},{32,0},{48,16},{64,96},{80,112},{96,64},{112,80},{1... | collective-permute-start | bytes 187400 | tf_op jit(solution)/shard_map/ppermute | solution.py:87
  80.1 10.3 %collective-permute-start.10 = (f32[32,488]{1,0:T(8,128)S(1)}, f32[32,488]{1,0:T(8,128)S(1)}, u32[]{:S(2)}, u32[]{:S(2)}) collective-permute-start(f32[32,488]{1,0:T(8,128)S(1)} %add.94), channel_id=1, source_target_pairs={{0,64},{16,80},{32,96},{48,112},{64,0},{80,16},{96,32},{112,48},{1... | collective-permute-start | bytes 187400 | tf_op jit(solution)/shard_map/ppermute | solution.py:87
  90.4 4.4 %collective-permute-start.11 = (f32[32,488]{1,0:T(8,128)S(1)}, f32[32,488]{1,0:T(8,128)S(1)}, u32[]{:S(2)}, u32[]{:S(2)}) collective-permute-start(f32[32,488]{1,0:T(8,128)S(1)} %add.95), channel_id=1, source_target_pairs={{0,128},{16,144},{32,160},{48,176},{64,192},{80,208},{96,224},{112... | collective-permute-start | bytes 187400 | tf_op jit(solution)/shard_map/ppermute | solution.py:87

commit v8 on v5

--- a/solution.py
+++ b/solution.py
@@ -176,7 +176,7 @@
         ],
         axis=1,
     )
-    totals = butterfly_sum(packed, ("space", "dp"))
+    totals = butterfly_sum(packed, ("dp", "space"))
     out_w2 = tap_minor(totals[:, :lanes_w2], chan1)
     out_w1 = tap_minor(totals[:, lanes_w2 : lanes_w2 + lanes_w1].reshape(grad_w1.shape), chan0)
     out_b2 = totals[:, lanes_w2 + lanes_w1]

time: 98.5 us -> 95.9 us (0.974); the launches traced: 98.1 us -> 94 us
  starting transfers between devices: 33.9 us -> 29.8 us
    ppermute x8, starting transfers between devices: 21.3 us -> 17.2 us  [butterfly_sum(): lax.ppermute(rows, axis, [(i, i ^ step) for i in range(count)])]
where the time goes in v8:
time: 95.9 us; the launch traced here: 94 us
  starting transfers between devices  29.8 us (31%)
  waiting for transfers between devices  29.8 us (31%)
  local copies, waits for them, and re-layouts  20.4 us (21%)
  matrix products  9.16 us (10%)
  other arithmetic  2.99 us (3%)
  between operations  1.78 us (2%)
    ppermute x8, waiting for transfers between devices, butterfly_sum(): lax.ppermute(rows, axis, [(i, i ^ step) for i in range(count)])  26.6 us
    ppermute x8, starting transfers between devices, butterfly_sum(): lax.ppermute(rows, axis, [(i, i ^ step) for i in range(count)])  17.2 us
    unnamed x145, local copies, waits for them, and re-layouts  10.5 us
    ppermute x2, starting transfers between devices, with_halo(): lax.ppermute(tail, axis, [(i, (i + 1) % count) for i in range(ends)])  6.87 us
    ppermute x2, starting transfers between devices, with_halo(): lax.ppermute(head, axis, [((i + 1) % count, i) for i in range(ends)])  5.74 us
    dot_general x1, matrix products, shards(): jnp.einsum('orxym,xykm->ork', grad_first, patches_first, preferred_elemen...  3.98 us
    dot_general x1, matrix products, shards(): jnp.einsum('ork,xykm->orxym', merged_kernel(w_first, 4), patches_wide, pr...  3.41 us
    ppermute x2, waiting for transfers between devices, with_halo(): lax.ppermute(head, axis, [((i + 1) % count, i) for i in range(ends)])  3.22 us
  transfers between devices with their start and end apart: 12, of which 9 were waited for; matrix products, arithmetic and copies ran while one was open for 7% of the time, Pallas kernels for 0%

profile of v8, /device:TPU:24, one launch (start us, length us, event | category | flops | bytes accessed | tf_op | source)
XLA Modules:
  0.0 94.0 jit_solution(1268792316086968418)
XLA Ops:
  0.6 1.0 %fusion.32 = (bf16[4,3,8,512]{3,2,1,0:T(8,128)(2,1)S(1)}, bf16[4,3,8,512]{3,2,1,0:T(8,128)(2,1)S(1)}) fusion(bf16[4,4,8,512]{3,2,1,0:T(8,128)(2,1)} %bitcast.133), kind=kLoop, calls=%fused_computation.198 | loop fusion | bytes 393216 | tf_op jit(solution)/shard_map/slice | solution.py:12
  1.6 1.9 %collective-permute-start = (bf16[4,3,8,512]{3,2,1,0:T(8,128)(2,1)S(1)}, bf16[4,3,8,512]{3,2,1,0:T(8,128)(2,1)S(1)}, u32[]{:S(2)}, u32[]{:S(2)}) collective-permute-start(bf16[4,3,8,512]{3,2,1,0:T(8,128)(2,1)S(1)} %get-tuple-element.45), channel_id=1, source_target_pairs={{0,1},{1,2},{2,3},{3,4},{4,5},{5,6},{6,7},{7,8},{8,9},{9,10},{10,1... | collective-permute-start | bytes 294920 | tf_op jit(solution)/shard_map/ppermute | solution.py:15
  3.6 3.6 %collective-permute-start.1 = (bf16[4,3,8,512]{3,2,1,0:T(8,128)(2,1)S(1)}, bf16[4,3,8,512]{3,2,1,0:T(8,128)(2,1)S(1)}, u32[]{:S(2)}, u32[]{:S(2)}) collective-permute-start(bf16[4,3,8,512]{3,2,1,0:T(8,128)(2,1)S(1)} %get-tuple-element.46), channel_id=1, source_target_pairs={{1,0},{2,1},{3,2},{4,3},{5,4},{6,5},{7,6},{8,7},{9,8},{10,9},{11,1... | collective-permute-start | bytes 294920 | tf_op jit(solution)/shard_map/ppermute | solution.py:17
  7.2 1.8 %copy.88 = bf16[1,4,4,8,512]{3,4,2,1,0:T(8,128)(2,1)S(1)} copy(bf16[1,4,4,8,512]{4,3,2,1,0:T(8,128)(2,1)} %param.8) | data formatting | bytes 262144 | tf_op args[0]
  9.1 0.9 copy.91
  10.3 1.0 %multiply_reduce_fusion.1 = bf16[16,4,3,3,3,4,4]{0,6,5,4,3,2,1:T(4,128)(2,1)S(1)} fusion(f32[4,3,4,3]{3,2,1,0:T(4,128)S(1)} %copy-done.2, f32[16,3,3,4,3]{0,3,4,2,1:T(4,128)S(1)} %convert_bitcast_fusion), kind=kLoop, calls=%fused_computation.9 | loop fusion | flops 138240 | bytes 62784 | tf_op jit(solution)/shard_map/reduce_sum | solution.py:116
  11.3 0.8 copy.87
  12.8 0.8 copy.89
  18.7 3.4 %divide_multiply_fusion = (f32[16,4,8,8,128]{4,0,3,2,1:T(8,128)S(1)}, f32[16,4,8,8,128]{4,0,3,2,1:T(8,128)}) fusion(f32[16]{0:T(128)S(1)} %copy-done.6, bf16[16,4,432,1,1]{0,2,4,3,1:T(8,128)(2,1)S(1)} %bitcast.135, bf16[8,8,432,128]{3,2,1,0:T(8,128)(2,1)S(1)} %constant_dynamic-update-slice_fusion), kind=kOutput, calls=%fused_computation.10 | convolution fusion | flops 455606272 | bytes 11327552 | tf_op jit(solution)/shard_map/ork,xykm->orxym/dot_general | solution.py:135
  24.9 5.0 %collective-permute-start.2 = (bf16[32,2,1,4,128]{4,0,3,2,1:T(8,128)(2,1)S(1)}, bf16[32,2,1,4,128]{4,0,3,2,1:T(8,128)(2,1)S(1)}, u32[]{:S(2)}, u32[]{:S(2)}) collective-permute-start(bf16[32,2,1,4,128]{4,0,3,2,1:T(8,128)(2,1)S(1)} %get-tuple-element.41), channel_id=1, source_target_pairs={{0,1},{1,2},{2,3},{3,4},{4,5},{5,6},{6,7},{7,8},{8,9},{9,10},{10,1... | collective-permute-start | bytes 196616 | tf_op jit(solution)/shard_map/ppermute | solution.py:15
  29.9 2.1 %collective-permute-start.3 = (bf16[32,2,1,4,128]{4,0,3,2,1:T(8,128)(2,1)S(1)}, bf16[32,2,1,4,128]{4,0,3,2,1:T(8,128)(2,1)S(1)}, u32[]{:S(2)}, u32[]{:S(2)}) collective-permute-start(bf16[32,2,1,4,128]{4,0,3,2,1:T(8,128)(2,1)S(1)} %get-tuple-element.42), channel_id=1, source_target_pairs={{1,0},{2,1},{3,2},{4,3},{5,4},{6,5},{7,6},{8,7},{9,8},{10,9},{11,1... | collective-permute-start | bytes 196616 | tf_op jit(solution)/shard_map/ppermute | solution.py:17
  32.7 3.2 %collective-permute-done.3 = bf16[32,2,1,4,128]{4,0,3,2,1:T(8,128)(2,1)S(1)} collective-permute-done((bf16[32,2,1,4,128]{4,0,3,2,1:T(8,128)(2,1)S(1)}, bf16[32,2,1,4,128]{4,0,3,2,1:T(8,128)(2,1)S(1)}, u32[]{:S(2)}, u32[]{:S(2)}) %collective-permute-start.3) | collective-permute-done | bytes 65568 | tf_op jit(solution)/shard_map/ppermute | solution.py:17
  38.7 1.4 %copy-done = f32[16,4,8,8,128]{4,0,3,2,1:T(8,128)S(1)} copy-done((f32[16,4,8,8,128]{4,0,3,2,1:T(8,128)S(1)}, f32[16,4,8,8,128]{4,0,3,2,1:T(8,128)}, u32[]{:S(2)}) %copy-start) | copy-done | bytes 2097176
  40.7 4.0 %fusion.2 = f32[16,4,432,1,1]{0,2,4,3,1:T(8,128)S(1)} fusion(bf16[16,4,4,8,128]{4,0,3,2,1:T(8,128)(2,1)S(1)} %get-tuple-element.28, bf16[8,8,432,128]{3,2,1,0:T(8,128)(2,1)} %copy-done.5), kind=kOutput, calls=%fused_computation.3 | convolution fusion | flops 226492416 | bytes 4173824 | tf_op jit(solution)/shard_map/orxym,xykm->ork/dot_general | solution.py:161
  44.7 0.8 multiply_reduce_fusion
  46.0 1.9 %collective-permute-start.4 = (f32[32,488]{1,0:T(8,128)S(1)}, f32[32,488]{1,0:T(8,128)S(1)}, u32[]{:S(2)}, u32[]{:S(2)}) collective-permute-start(f32[32,488]{1,0:T(8,128)S(1)} %pad_maximum_fusion.5), channel_id=1, source_target_pairs={{0,16},{16,0},{32,48},{48,32},{64,80},{80,64},{96,112},{112,96},{1... | collective-permute-start | bytes 187400 | tf_op jit(solution)/shard_map/ppermute | solution.py:79
  48.0 2.3 %collective-permute-done.4 = f32[32,488]{1,0:T(8,128)S(1)} collective-permute-done((f32[32,488]{1,0:T(8,128)S(1)}, f32[32,488]{1,0:T(8,128)S(1)}, u32[]{:S(2)}, u32[]{:S(2)}) %collective-permute-start.4) | collective-permute-done | bytes 62496 | tf_op jit(solution)/shard_map/ppermute | solution.py:79
  50.4 3.3 %collective-permute-start.5 = (f32[32,488]{1,0:T(8,128)S(1)}, f32[32,488]{1,0:T(8,128)S(1)}, u32[]{:S(2)}, u32[]{:S(2)}) collective-permute-start(f32[32,488]{1,0:T(8,128)S(1)} %fusion.37), channel_id=1, source_target_pairs={{0,32},{16,48},{32,0},{48,16},{64,96},{80,112},{96,64},{112,80},{1... | collective-permute-start | bytes 187400 | tf_op jit(solution)/shard_map/ppermute | solution.py:79
  53.7 2.3 %collective-permute-done.5 = f32[32,488]{1,0:T(8,128)S(1)} collective-permute-done((f32[32,488]{1,0:T(8,128)S(1)}, f32[32,488]{1,0:T(8,128)S(1)}, u32[]{:S(2)}, u32[]{:S(2)}) %collective-permute-start.5) | collective-permute-done | bytes 62496 | tf_op jit(solution)/shard_map/ppermute | solution.py:79
  56.1 7.6 %collective-permute-start.6 = (f32[32,488]{1,0:T(8,128)S(1)}, f32[32,488]{1,0:T(8,128)S(1)}, u32[]{:S(2)}, u32[]{:S(2)}) collective-permute-start(f32[32,488]{1,0:T(8,128)S(1)} %add.92), channel_id=1, source_target_pairs={{0,64},{16,80},{32,96},{48,112},{64,0},{80,16},{96,32},{112,48},{1... | collective-permute-start | bytes 187400 | tf_op jit(solution)/shard_map/ppermute | solution.py:79
  63.6 3.0 %collective-permute-done.6 = f32[32,488]{1,0:T(8,128)S(1)} collective-permute-done((f32[32,488]{1,0:T(8,128)S(1)}, f32[32,488]{1,0:T(8,128)S(1)}, u32[]{:S(2)}, u32[]{:S(2)}) %collective-permute-start.6) | collective-permute-done | bytes 62496 | tf_op jit(solution)/shard_map/ppermute | solution.py:79
  67.3 3.7 %collective-permute-done.7 = f32[32,488]{1,0:T(8,128)S(1)} collective-permute-done((f32[32,488]{1,0:T(8,128)S(1)}, f32[32,488]{1,0:T(8,128)S(1)}, u32[]{:S(2)}, u32[]{:S(2)}) %collective-permute-start.7) | collective-permute-done | bytes 62496 | tf_op jit(solution)/shard_map/ppermute | solution.py:79
  71.0 2.6 %collective-permute-start.8 = (f32[32,488]{1,0:T(8,128)S(1)}, f32[32,488]{1,0:T(8,128)S(1)}, u32[]{:S(2)}, u32[]{:S(2)}) collective-permute-start(f32[32,488]{1,0:T(8,128)S(1)} %add.94), channel_id=1, source_target_pairs={{0,1},{1,0},{2,3},{3,2},{4,5},{5,4},{6,7},{7,6},{8,9},{9,8},{10,11... | collective-permute-start | bytes 187400 | tf_op jit(solution)/shard_map/ppermute | solution.py:79
  73.6 0.9 collective-permute-done.8
  74.6 4.3 %collective-permute-done.9 = f32[32,488]{1,0:T(8,128)S(1)} collective-permute-done((f32[32,488]{1,0:T(8,128)S(1)}, f32[32,488]{1,0:T(8,128)S(1)}, u32[]{:S(2)}, u32[]{:S(2)}) %collective-permute-start.9) | collective-permute-done | bytes 62496 | tf_op jit(solution)/shard_map/ppermute | solution.py:79
  79.1 5.7 %collective-permute-done.10 = f32[32,488]{1,0:T(8,128)S(1)} collective-permute-done((f32[32,488]{1,0:T(8,128)S(1)}, f32[32,488]{1,0:T(8,128)S(1)}, u32[]{:S(2)}, u32[]{:S(2)}) %collective-permute-start.10) | collective-permute-done | bytes 62496 | tf_op jit(solution)/shard_map/ppermute | solution.py:79
  84.8 0.9 collective-permute-start.11
  86.4 4.3 %collective-permute-done.11 = f32[32,488]{1,0:T(8,128)S(1)} collective-permute-done((f32[32,488]{1,0:T(8,128)S(1)}, f32[32,488]{1,0:T(8,128)S(1)}, u32[]{:S(2)}, u32[]{:S(2)}) %collective-permute-start.11) | collective-permute-done | bytes 62496 | tf_op jit(solution)/shard_map/ppermute | solution.py:79
  90.8 0.7 slice_reduce_fusion
  91.5 0.7 slice_reduce_fusion.1
  92.3 0.9 copy.108
  93.2 0.8 copy.106
  (203 shorter events, 14.5 us)
Async XLA Ops:
  1.6 9.7 %collective-permute-start = (bf16[4,3,8,512]{3,2,1,0:T(8,128)(2,1)S(1)}, bf16[4,3,8,512]{3,2,1,0:T(8,128)(2,1)S(1)}, u32[]{:S(2)}, u32[]{:S(2)}) collective-permute-start(bf16[4,3,8,512]{3,2,1,0:T(8,128)(2,1)S(1)} %get-tuple-element.45), channel_id=1, source_target_pairs={{0,1},{1,2},{2,3},{3,4},{4,5},{5,6},{6,7},{7,8},{8,9},{9,10},{10,1... | collective-permute-start | bytes 294920 | tf_op jit(solution)/shard_map/ppermute | solution.py:15
  3.6 6.4 %copy-start.3 = (bf16[16,4,3,3,3]{0,1,4,3,2:T(4,128)(2,1)S(1)}, bf16[16,4,3,3,3]{0,1,4,3,2:T(4,128)(2,1)}, u32[]{:S(2)}) copy-start(bf16[16,4,3,3,3]{0,1,4,3,2:T(4,128)(2,1)} %param.10) | copy-start | bytes 10372
  3.6 6.5 %copy-start.4 = (bf16[1,32,1,2,128]{4,3,2,1,0:T(2,128)(2,1)S(1)}, bf16[1,32,1,2,128]{4,3,2,1,0:T(2,128)(2,1)}, u32[]{:S(2)}) copy-start(bf16[1,32,1,2,128]{4,3,2,1,0:T(2,128)(2,1)} %param.9) | copy-start | bytes 49156
  3.6 9.3 %collective-permute-start.1 = (bf16[4,3,8,512]{3,2,1,0:T(8,128)(2,1)S(1)}, bf16[4,3,8,512]{3,2,1,0:T(8,128)(2,1)S(1)}, u32[]{:S(2)}, u32[]{:S(2)}) collective-permute-start(bf16[4,3,8,512]{3,2,1,0:T(8,128)(2,1)S(1)} %get-tuple-element.46), channel_id=1, source_target_pairs={{1,0},{2,1},{3,2},{4,3},{5,4},{6,5},{7,6},{8,7},{9,8},{10,9},{11,1... | collective-permute-start | bytes 294920 | tf_op jit(solution)/shard_map/ppermute | solution.py:17
  9.1 1.0 %copy-start.1 = (bf16[32,16,3,3,3]{0,1,4,3,2:T(8,128)(2,1)S(1)}, bf16[32,16,3,3,3]{0,1,4,3,2:T(8,128)(2,1)}, u32[]{:S(2)}) copy-start(bf16[32,16,3,3,3]{0,1,4,3,2:T(8,128)(2,1)} %param.12) | copy-start | bytes 82948
  9.1 1.2 %copy-start.2 = (f32[4,3,4,3]{3,2,1,0:T(4,128)S(1)}, f32[4,3,4,3]{3,2,1,0:T(4,128)}, u32[]{:S(2)}) copy-start(f32[4,3,4,3]{3,2,1,0:T(4,128)} %constant.57) | copy-start | bytes 1732
  17.9 0.7 copy-start.6
  18.6 3.5 %copy-start.5 = (bf16[8,8,432,128]{3,2,1,0:T(8,128)(2,1)}, bf16[8,8,432,128]{3,2,1,0:T(8,128)(2,1)S(1)}, u32[]{:S(2)}) copy-start(bf16[8,8,432,128]{3,2,1,0:T(8,128)(2,1)S(1)} %constant_dynamic-update-slice_fusion) | copy-start | bytes 21233668
  23.3 1.0 %copy-start.7 = (f32[32]{0:T(128)S(1)}, f32[32]{0:T(128)}, u32[]{:S(2)}) copy-start(f32[32]{0:T(128)} %param.13) | copy-start | bytes 388
  24.9 7.8 %collective-permute-start.2 = (bf16[32,2,1,4,128]{4,0,3,2,1:T(8,128)(2,1)S(1)}, bf16[32,2,1,4,128]{4,0,3,2,1:T(8,128)(2,1)S(1)}, u32[]{:S(2)}, u32[]{:S(2)}) collective-permute-start(bf16[32,2,1,4,128]{4,0,3,2,1:T(8,128)(2,1)S(1)} %get-tuple-element.41), channel_id=1, source_target_pairs={{0,1},{1,2},{2,3},{3,4},{4,5},{5,6},{6,7},{7,8},{8,9},{9,10},{10,1... | collective-permute-start | bytes 196616 | tf_op jit(solution)/shard_map/ppermute | solution.py:15
  29.9 6.0 %collective-permute-start.3 = (bf16[32,2,1,4,128]{4,0,3,2,1:T(8,128)(2,1)S(1)}, bf16[32,2,1,4,128]{4,0,3,2,1:T(8,128)(2,1)S(1)}, u32[]{:S(2)}, u32[]{:S(2)}) collective-permute-start(bf16[32,2,1,4,128]{4,0,3,2,1:T(8,128)(2,1)S(1)} %get-tuple-element.42), channel_id=1, source_target_pairs={{1,0},{2,1},{3,2},{4,3},{5,4},{6,5},{7,6},{8,7},{9,8},{10,9},{11,1... | collective-permute-start | bytes 196616 | tf_op jit(solution)/shard_map/ppermute | solution.py:17
  38.6 1.6 %copy-start = (f32[16,4,8,8,128]{4,0,3,2,1:T(8,128)S(1)}, f32[16,4,8,8,128]{4,0,3,2,1:T(8,128)}, u32[]{:S(2)}) copy-start(f32[16,4,8,8,128]{4,0,3,2,1:T(8,128)} %get-tuple-element.52) | copy-start | bytes 6291460
  46.0 4.3 %collective-permute-start.4 = (f32[32,488]{1,0:T(8,128)S(1)}, f32[32,488]{1,0:T(8,128)S(1)}, u32[]{:S(2)}, u32[]{:S(2)}) collective-permute-start(f32[32,488]{1,0:T(8,128)S(1)} %pad_maximum_fusion.5), channel_id=1, source_target_pairs={{0,16},{16,0},{32,48},{48,32},{64,80},{80,64},{96,112},{112,96},{1... | collective-permute-start | bytes 187400 | tf_op jit(solution)/shard_map/ppermute | solution.py:79
  50.4 5.6 %collective-permute-start.5 = (f32[32,488]{1,0:T(8,128)S(1)}, f32[32,488]{1,0:T(8,128)S(1)}, u32[]{:S(2)}, u32[]{:S(2)}) collective-permute-start(f32[32,488]{1,0:T(8,128)S(1)} %fusion.37), channel_id=1, source_target_pairs={{0,32},{16,48},{32,0},{48,16},{64,96},{80,112},{96,64},{112,80},{1... | collective-permute-start | bytes 187400 | tf_op jit(solution)/shard_map/ppermute | solution.py:79
  56.1 10.5 %collective-permute-start.6 = (f32[32,488]{1,0:T(8,128)S(1)}, f32[32,488]{1,0:T(8,128)S(1)}, u32[]{:S(2)}, u32[]{:S(2)}) collective-permute-start(f32[32,488]{1,0:T(8,128)S(1)} %add.92), channel_id=1, source_target_pairs={{0,64},{16,80},{32,96},{48,112},{64,0},{80,16},{96,32},{112,48},{1... | collective-permute-start | bytes 187400 | tf_op jit(solution)/shard_map/ppermute | solution.py:79
  66.6 4.4 %collective-permute-start.7 = (f32[32,488]{1,0:T(8,128)S(1)}, f32[32,488]{1,0:T(8,128)S(1)}, u32[]{:S(2)}, u32[]{:S(2)}) collective-permute-start(f32[32,488]{1,0:T(8,128)S(1)} %add.93), channel_id=1, source_target_pairs={{0,128},{16,144},{32,160},{48,176},{64,192},{80,208},{96,224},{112... | collective-permute-start | bytes 187400 | tf_op jit(solution)/shard_map/ppermute | solution.py:79
  71.0 3.5 %collective-permute-start.8 = (f32[32,488]{1,0:T(8,128)S(1)}, f32[32,488]{1,0:T(8,128)S(1)}, u32[]{:S(2)}, u32[]{:S(2)}) collective-permute-start(f32[32,488]{1,0:T(8,128)S(1)} %add.94), channel_id=1, source_target_pairs={{0,1},{1,0},{2,3},{3,2},{4,5},{5,4},{6,7},{7,6},{8,9},{9,8},{10,11... | collective-permute-start | bytes 187400 | tf_op jit(solution)/shard_map/ppermute | solution.py:79
  74.5 4.4 %collective-permute-start.9 = (f32[32,488]{1,0:T(8,128)S(1)}, f32[32,488]{1,0:T(8,128)S(1)}, u32[]{:S(2)}, u32[]{:S(2)}) collective-permute-start(f32[32,488]{1,0:T(8,128)S(1)} %add.95), channel_id=1, source_target_pairs={{0,2},{1,3},{2,0},{3,1},{4,6},{5,7},{6,4},{7,5},{8,10},{9,11},{10,... | collective-permute-start | bytes 187400 | tf_op jit(solution)/shard_map/ppermute | solution.py:79
  78.9 5.9 %collective-permute-start.10 = (f32[32,488]{1,0:T(8,128)S(1)}, f32[32,488]{1,0:T(8,128)S(1)}, u32[]{:S(2)}, u32[]{:S(2)}) collective-permute-start(f32[32,488]{1,0:T(8,128)S(1)} %add.96), channel_id=1, source_target_pairs={{0,4},{1,5},{2,6},{3,7},{4,0},{5,1},{6,2},{7,3},{8,12},{9,13},{10,... | collective-permute-start | bytes 187400 | tf_op jit(solution)/shard_map/ppermute | solution.py:79
  84.8 5.9 %collective-permute-start.11 = (f32[32,488]{1,0:T(8,128)S(1)}, f32[32,488]{1,0:T(8,128)S(1)}, u32[]{:S(2)}, u32[]{:S(2)}) collective-permute-start(f32[32,488]{1,0:T(8,128)S(1)} %add.97), channel_id=1, source_target_pairs={{0,8},{1,9},{2,10},{3,11},{4,12},{5,13},{6,14},{7,15},{8,0},{9,1},... | collective-permute-start | bytes 187400 | tf_op jit(solution)/shard_map/ppermute | solution.py:79

commit v9 on v8

--- a/solution.py
+++ b/solution.py
@@ -179,8 +179,9 @@
     totals = butterfly_sum(packed, ("dp", "space"))
     out_w2 = tap_minor(totals[:, :lanes_w2], chan1)
     out_w1 = tap_minor(totals[:, lanes_w2 : lanes_w2 + lanes_w1].reshape(grad_w1.shape), chan0)
-    out_b2 = totals[:, lanes_w2 + lanes_w1]
-    out_b1 = totals[: grad_b1.shape[0], lanes_w2 + lanes_w1 + 1]
+    bias_rows = totals[:, lanes_w2 + lanes_w1 : lanes_w2 + lanes_w1 + 2].T
+    out_b2 = bias_rows[0]
+    out_b1 = bias_rows[1, : grad_b1.shape[0]]
     return (output[None], out_w1, out_b1, out_w2, out_b2)
 
 

time: 95.9 us -> 95.9 us (level)
  no operation moved by 1% of the time
where the time goes in v9:
time: 95.9 us; the launch traced here: 94 us
  starting transfers between devices  29.8 us (31%)
  waiting for transfers between devices  29.8 us (31%)
  local copies, waits for them, and re-layouts  20.5 us (21%)
  matrix products  9.16 us (10%)
  other arithmetic  2.99 us (3%)
  between operations  1.78 us (2%)
    ppermute x8, waiting for transfers between devices, butterfly_sum(): lax.ppermute(rows, axis, [(i, i ^ step) for i in range(count)])  26.6 us
    ppermute x8, starting transfers between devices, butterfly_sum(): lax.ppermute(rows, axis, [(i, i ^ step) for i in range(count)])  17.2 us
    unnamed x145, local copies, waits for them, and re-layouts  10.5 us
    ppermute x2, starting transfers between devices, with_halo(): lax.ppermute(tail, axis, [(i, (i + 1) % count) for i in range(ends)])  6.87 us
    ppermute x2, starting transfers between devices, with_halo(): lax.ppermute(head, axis, [((i + 1) % count, i) for i in range(ends)])  5.74 us
    dot_general x1, matrix products, shards(): jnp.einsum('orxym,xykm->ork', grad_first, patches_first, preferred_elemen...  3.98 us
    dot_general x1, matrix products, shards(): jnp.einsum('ork,xykm->orxym', merged_kernel(w_first, 4), patches_wide, pr...  3.41 us
    ppermute x2, waiting for transfers between devices, with_halo(): lax.ppermute(head, axis, [((i + 1) % count, i) for i in range(ends)])  3.22 us
  transfers between devices with their start and end apart: 12, of which 9 were waited for; matrix products, arithmetic and copies ran while one was open for 7% of the time, Pallas kernels for 0%

profile of v9, /device:TPU:24, one launch (start us, length us, event | category | flops | bytes accessed | tf_op | source)
XLA Modules:
  0.0 94.0 jit_solution(17451834537284543156)
XLA Ops:
  0.6 1.0 %fusion.32 = (bf16[4,3,8,512]{3,2,1,0:T(8,128)(2,1)S(1)}, bf16[4,3,8,512]{3,2,1,0:T(8,128)(2,1)S(1)}) fusion(bf16[4,4,8,512]{3,2,1,0:T(8,128)(2,1)} %bitcast.135), kind=kLoop, calls=%fused_computation.199 | loop fusion | bytes 393216 | tf_op jit(solution)/shard_map/slice | solution.py:12
  1.6 1.9 %collective-permute-start = (bf16[4,3,8,512]{3,2,1,0:T(8,128)(2,1)S(1)}, bf16[4,3,8,512]{3,2,1,0:T(8,128)(2,1)S(1)}, u32[]{:S(2)}, u32[]{:S(2)}) collective-permute-start(bf16[4,3,8,512]{3,2,1,0:T(8,128)(2,1)S(1)} %get-tuple-element.45), channel_id=1, source_target_pairs={{0,1},{1,2},{2,3},{3,4},{4,5},{5,6},{6,7},{7,8},{8,9},{9,10},{10,1... | collective-permute-start | bytes 294920 | tf_op jit(solution)/shard_map/ppermute | solution.py:15
  3.6 3.6 %collective-permute-start.1 = (bf16[4,3,8,512]{3,2,1,0:T(8,128)(2,1)S(1)}, bf16[4,3,8,512]{3,2,1,0:T(8,128)(2,1)S(1)}, u32[]{:S(2)}, u32[]{:S(2)}) collective-permute-start(bf16[4,3,8,512]{3,2,1,0:T(8,128)(2,1)S(1)} %get-tuple-element.46), channel_id=1, source_target_pairs={{1,0},{2,1},{3,2},{4,3},{5,4},{6,5},{7,6},{8,7},{9,8},{10,9},{11,1... | collective-permute-start | bytes 294920 | tf_op jit(solution)/shard_map/ppermute | solution.py:17
  7.2 1.8 %copy.88 = bf16[1,4,4,8,512]{3,4,2,1,0:T(8,128)(2,1)S(1)} copy(bf16[1,4,4,8,512]{4,3,2,1,0:T(8,128)(2,1)} %param.8) | data formatting | bytes 262144 | tf_op args[0]
  9.1 0.9 copy.91
  10.3 1.0 %multiply_reduce_fusion.1 = bf16[16,4,3,3,3,4,4]{0,6,5,4,3,2,1:T(4,128)(2,1)S(1)} fusion(f32[4,3,4,3]{3,2,1,0:T(4,128)S(1)} %copy-done.2, f32[16,3,3,4,3]{0,3,4,2,1:T(4,128)S(1)} %convert_bitcast_fusion), kind=kLoop, calls=%fused_computation.9 | loop fusion | flops 138240 | bytes 62784 | tf_op jit(solution)/shard_map/reduce_sum | solution.py:116
  11.3 0.8 copy.87
  12.8 0.8 copy.89
  18.7 3.4 %divide_multiply_fusion = (f32[16,4,8,8,128]{4,0,3,2,1:T(8,128)S(1)}, f32[16,4,8,8,128]{4,0,3,2,1:T(8,128)}) fusion(f32[16]{0:T(128)S(1)} %copy-done.6, bf16[16,4,432,1,1]{0,2,4,3,1:T(8,128)(2,1)S(1)} %bitcast.136, bf16[8,8,432,128]{3,2,1,0:T(8,128)(2,1)S(1)} %constant_dynamic-update-slice_fusion), kind=kOutput, calls=%fused_computation.10 | convolution fusion | flops 455606272 | bytes 11327552 | tf_op jit(solution)/shard_map/ork,xykm->orxym/dot_general | solution.py:135
  24.9 5.0 %collective-permute-start.2 = (bf16[32,2,1,4,128]{4,0,3,2,1:T(8,128)(2,1)S(1)}, bf16[32,2,1,4,128]{4,0,3,2,1:T(8,128)(2,1)S(1)}, u32[]{:S(2)}, u32[]{:S(2)}) collective-permute-start(bf16[32,2,1,4,128]{4,0,3,2,1:T(8,128)(2,1)S(1)} %get-tuple-element.41), channel_id=1, source_target_pairs={{0,1},{1,2},{2,3},{3,4},{4,5},{5,6},{6,7},{7,8},{8,9},{9,10},{10,1... | collective-permute-start | bytes 196616 | tf_op jit(solution)/shard_map/ppermute | solution.py:15
  29.9 2.1 %collective-permute-start.3 = (bf16[32,2,1,4,128]{4,0,3,2,1:T(8,128)(2,1)S(1)}, bf16[32,2,1,4,128]{4,0,3,2,1:T(8,128)(2,1)S(1)}, u32[]{:S(2)}, u32[]{:S(2)}) collective-permute-start(bf16[32,2,1,4,128]{4,0,3,2,1:T(8,128)(2,1)S(1)} %get-tuple-element.42), channel_id=1, source_target_pairs={{1,0},{2,1},{3,2},{4,3},{5,4},{6,5},{7,6},{8,7},{9,8},{10,9},{11,1... | collective-permute-start | bytes 196616 | tf_op jit(solution)/shard_map/ppermute | solution.py:17
  32.7 3.2 %collective-permute-done.3 = bf16[32,2,1,4,128]{4,0,3,2,1:T(8,128)(2,1)S(1)} collective-permute-done((bf16[32,2,1,4,128]{4,0,3,2,1:T(8,128)(2,1)S(1)}, bf16[32,2,1,4,128]{4,0,3,2,1:T(8,128)(2,1)S(1)}, u32[]{:S(2)}, u32[]{:S(2)}) %collective-permute-start.3) | collective-permute-done | bytes 65568 | tf_op jit(solution)/shard_map/ppermute | solution.py:17
  38.7 1.4 %copy-done = f32[16,4,8,8,128]{4,0,3,2,1:T(8,128)S(1)} copy-done((f32[16,4,8,8,128]{4,0,3,2,1:T(8,128)S(1)}, f32[16,4,8,8,128]{4,0,3,2,1:T(8,128)}, u32[]{:S(2)}) %copy-start) | copy-done | bytes 2097176
  40.7 4.0 %fusion.2 = f32[16,4,432,1,1]{0,2,4,3,1:T(8,128)S(1)} fusion(bf16[16,4,4,8,128]{4,0,3,2,1:T(8,128)(2,1)S(1)} %get-tuple-element.28, bf16[8,8,432,128]{3,2,1,0:T(8,128)(2,1)} %copy-done.5), kind=kOutput, calls=%fused_computation.3 | convolution fusion | flops 226492416 | bytes 4173824 | tf_op jit(solution)/shard_map/orxym,xykm->ork/dot_general | solution.py:161
  44.7 0.8 multiply_reduce_fusion
  46.0 1.9 %collective-permute-start.4 = (f32[32,488]{1,0:T(8,128)S(1)}, f32[32,488]{1,0:T(8,128)S(1)}, u32[]{:S(2)}, u32[]{:S(2)}) collective-permute-start(f32[32,488]{1,0:T(8,128)S(1)} %pad_maximum_fusion.5), channel_id=1, source_target_pairs={{0,16},{16,0},{32,48},{48,32},{64,80},{80,64},{96,112},{112,96},{1... | collective-permute-start | bytes 187400 | tf_op jit(solution)/shard_map/ppermute | solution.py:79
  48.0 2.3 %collective-permute-done.4 = f32[32,488]{1,0:T(8,128)S(1)} collective-permute-done((f32[32,488]{1,0:T(8,128)S(1)}, f32[32,488]{1,0:T(8,128)S(1)}, u32[]{:S(2)}, u32[]{:S(2)}) %collective-permute-start.4) | collective-permute-done | bytes 62496 | tf_op jit(solution)/shard_map/ppermute | solution.py:79
  50.4 3.3 %collective-permute-start.5 = (f32[32,488]{1,0:T(8,128)S(1)}, f32[32,488]{1,0:T(8,128)S(1)}, u32[]{:S(2)}, u32[]{:S(2)}) collective-permute-start(f32[32,488]{1,0:T(8,128)S(1)} %fusion.37), channel_id=1, source_target_pairs={{0,32},{16,48},{32,0},{48,16},{64,96},{80,112},{96,64},{112,80},{1... | collective-permute-start | bytes 187400 | tf_op jit(solution)/shard_map/ppermute | solution.py:79
  53.7 2.3 %collective-permute-done.5 = f32[32,488]{1,0:T(8,128)S(1)} collective-permute-done((f32[32,488]{1,0:T(8,128)S(1)}, f32[32,488]{1,0:T(8,128)S(1)}, u32[]{:S(2)}, u32[]{:S(2)}) %collective-permute-start.5) | collective-permute-done | bytes 62496 | tf_op jit(solution)/shard_map/ppermute | solution.py:79
  56.1 7.6 %collective-permute-start.6 = (f32[32,488]{1,0:T(8,128)S(1)}, f32[32,488]{1,0:T(8,128)S(1)}, u32[]{:S(2)}, u32[]{:S(2)}) collective-permute-start(f32[32,488]{1,0:T(8,128)S(1)} %add.92), channel_id=1, source_target_pairs={{0,64},{16,80},{32,96},{48,112},{64,0},{80,16},{96,32},{112,48},{1... | collective-permute-start | bytes 187400 | tf_op jit(solution)/shard_map/ppermute | solution.py:79
  63.6 3.0 %collective-permute-done.6 = f32[32,488]{1,0:T(8,128)S(1)} collective-permute-done((f32[32,488]{1,0:T(8,128)S(1)}, f32[32,488]{1,0:T(8,128)S(1)}, u32[]{:S(2)}, u32[]{:S(2)}) %collective-permute-start.6) | collective-permute-done | bytes 62496 | tf_op jit(solution)/shard_map/ppermute | solution.py:79
  66.6 0.7 collective-permute-start.7
  67.3 3.7 %collective-permute-done.7 = f32[32,488]{1,0:T(8,128)S(1)} collective-permute-done((f32[32,488]{1,0:T(8,128)S(1)}, f32[32,488]{1,0:T(8,128)S(1)}, u32[]{:S(2)}, u32[]{:S(2)}) %collective-permute-start.7) | collective-permute-done | bytes 62496 | tf_op jit(solution)/shard_map/ppermute | solution.py:79
  71.0 2.6 %collective-permute-start.8 = (f32[32,488]{1,0:T(8,128)S(1)}, f32[32,488]{1,0:T(8,128)S(1)}, u32[]{:S(2)}, u32[]{:S(2)}) collective-permute-start(f32[32,488]{1,0:T(8,128)S(1)} %add.94), channel_id=1, source_target_pairs={{0,1},{1,0},{2,3},{3,2},{4,5},{5,4},{6,7},{7,6},{8,9},{9,8},{10,11... | collective-permute-start | bytes 187400 | tf_op jit(solution)/shard_map/ppermute | solution.py:79
  73.6 0.9 collective-permute-done.8
  74.6 4.3 %collective-permute-done.9 = f32[32,488]{1,0:T(8,128)S(1)} collective-permute-done((f32[32,488]{1,0:T(8,128)S(1)}, f32[32,488]{1,0:T(8,128)S(1)}, u32[]{:S(2)}, u32[]{:S(2)}) %collective-permute-start.9) | collective-permute-done | bytes 62496 | tf_op jit(solution)/shard_map/ppermute | solution.py:79
  79.1 5.7 %collective-permute-done.10 = f32[32,488]{1,0:T(8,128)S(1)} collective-permute-done((f32[32,488]{1,0:T(8,128)S(1)}, f32[32,488]{1,0:T(8,128)S(1)}, u32[]{:S(2)}, u32[]{:S(2)}) %collective-permute-start.10) | collective-permute-done | bytes 62496 | tf_op jit(solution)/shard_map/ppermute | solution.py:79
  84.8 0.9 collective-permute-start.11
  86.4 4.3 %collective-permute-done.11 = f32[32,488]{1,0:T(8,128)S(1)} collective-permute-done((f32[32,488]{1,0:T(8,128)S(1)}, f32[32,488]{1,0:T(8,128)S(1)}, u32[]{:S(2)}, u32[]{:S(2)}) %collective-permute-start.11) | collective-permute-done | bytes 62496 | tf_op jit(solution)/shard_map/ppermute | solution.py:79
  91.5 0.7 slice_reduce_fusion.1
  92.3 0.9 copy.108
  93.2 0.8 copy.106
  (204 shorter events, 14.5 us)
Async XLA Ops:
  1.6 9.7 %collective-permute-start = (bf16[4,3,8,512]{3,2,1,0:T(8,128)(2,1)S(1)}, bf16[4,3,8,512]{3,2,1,0:T(8,128)(2,1)S(1)}, u32[]{:S(2)}, u32[]{:S(2)}) collective-permute-start(bf16[4,3,8,512]{3,2,1,0:T(8,128)(2,1)S(1)} %get-tuple-element.45), channel_id=1, source_target_pairs={{0,1},{1,2},{2,3},{3,4},{4,5},{5,6},{6,7},{7,8},{8,9},{9,10},{10,1... | collective-permute-start | bytes 294920 | tf_op jit(solution)/shard_map/ppermute | solution.py:15
  3.6 6.4 %copy-start.3 = (bf16[16,4,3,3,3]{0,1,4,3,2:T(4,128)(2,1)S(1)}, bf16[16,4,3,3,3]{0,1,4,3,2:T(4,128)(2,1)}, u32[]{:S(2)}) copy-start(bf16[16,4,3,3,3]{0,1,4,3,2:T(4,128)(2,1)} %param.10) | copy-start | bytes 10372
  3.6 6.5 %copy-start.4 = (bf16[1,32,1,2,128]{4,3,2,1,0:T(2,128)(2,1)S(1)}, bf16[1,32,1,2,128]{4,3,2,1,0:T(2,128)(2,1)}, u32[]{:S(2)}) copy-start(bf16[1,32,1,2,128]{4,3,2,1,0:T(2,128)(2,1)} %param.9) | copy-start | bytes 49156
  3.6 9.3 %collective-permute-start.1 = (bf16[4,3,8,512]{3,2,1,0:T(8,128)(2,1)S(1)}, bf16[4,3,8,512]{3,2,1,0:T(8,128)(2,1)S(1)}, u32[]{:S(2)}, u32[]{:S(2)}) collective-permute-start(bf16[4,3,8,512]{3,2,1,0:T(8,128)(2,1)S(1)} %get-tuple-element.46), channel_id=1, source_target_pairs={{1,0},{2,1},{3,2},{4,3},{5,4},{6,5},{7,6},{8,7},{9,8},{10,9},{11,1... | collective-permute-start | bytes 294920 | tf_op jit(solution)/shard_map/ppermute | solution.py:17
  9.1 1.0 %copy-start.1 = (bf16[32,16,3,3,3]{0,1,4,3,2:T(8,128)(2,1)S(1)}, bf16[32,16,3,3,3]{0,1,4,3,2:T(8,128)(2,1)}, u32[]{:S(2)}) copy-start(bf16[32,16,3,3,3]{0,1,4,3,2:T(8,128)(2,1)} %param.12) | copy-start | bytes 82948
  9.1 1.2 %copy-start.2 = (f32[4,3,4,3]{3,2,1,0:T(4,128)S(1)}, f32[4,3,4,3]{3,2,1,0:T(4,128)}, u32[]{:S(2)}) copy-start(f32[4,3,4,3]{3,2,1,0:T(4,128)} %constant.57) | copy-start | bytes 1732
  17.9 0.7 copy-start.6
  18.6 3.5 %copy-start.5 = (bf16[8,8,432,128]{3,2,1,0:T(8,128)(2,1)}, bf16[8,8,432,128]{3,2,1,0:T(8,128)(2,1)S(1)}, u32[]{:S(2)}) copy-start(bf16[8,8,432,128]{3,2,1,0:T(8,128)(2,1)S(1)} %constant_dynamic-update-slice_fusion) | copy-start | bytes 21233668
  23.3 1.0 %copy-start.7 = (f32[32]{0:T(128)S(1)}, f32[32]{0:T(128)}, u32[]{:S(2)}) copy-start(f32[32]{0:T(128)} %param.13) | copy-start | bytes 388
  24.9 7.8 %collective-permute-start.2 = (bf16[32,2,1,4,128]{4,0,3,2,1:T(8,128)(2,1)S(1)}, bf16[32,2,1,4,128]{4,0,3,2,1:T(8,128)(2,1)S(1)}, u32[]{:S(2)}, u32[]{:S(2)}) collective-permute-start(bf16[32,2,1,4,128]{4,0,3,2,1:T(8,128)(2,1)S(1)} %get-tuple-element.41), channel_id=1, source_target_pairs={{0,1},{1,2},{2,3},{3,4},{4,5},{5,6},{6,7},{7,8},{8,9},{9,10},{10,1... | collective-permute-start | bytes 196616 | tf_op jit(solution)/shard_map/ppermute | solution.py:15
  29.9 6.0 %collective-permute-start.3 = (bf16[32,2,1,4,128]{4,0,3,2,1:T(8,128)(2,1)S(1)}, bf16[32,2,1,4,128]{4,0,3,2,1:T(8,128)(2,1)S(1)}, u32[]{:S(2)}, u32[]{:S(2)}) collective-permute-start(bf16[32,2,1,4,128]{4,0,3,2,1:T(8,128)(2,1)S(1)} %get-tuple-element.42), channel_id=1, source_target_pairs={{1,0},{2,1},{3,2},{4,3},{5,4},{6,5},{7,6},{8,7},{9,8},{10,9},{11,1... | collective-permute-start | bytes 196616 | tf_op jit(solution)/shard_map/ppermute | solution.py:17
  38.6 1.6 %copy-start = (f32[16,4,8,8,128]{4,0,3,2,1:T(8,128)S(1)}, f32[16,4,8,8,128]{4,0,3,2,1:T(8,128)}, u32[]{:S(2)}) copy-start(f32[16,4,8,8,128]{4,0,3,2,1:T(8,128)} %get-tuple-element.52) | copy-start | bytes 6291460
  46.0 4.3 %collective-permute-start.4 = (f32[32,488]{1,0:T(8,128)S(1)}, f32[32,488]{1,0:T(8,128)S(1)}, u32[]{:S(2)}, u32[]{:S(2)}) collective-permute-start(f32[32,488]{1,0:T(8,128)S(1)} %pad_maximum_fusion.5), channel_id=1, source_target_pairs={{0,16},{16,0},{32,48},{48,32},{64,80},{80,64},{96,112},{112,96},{1... | collective-permute-start | bytes 187400 | tf_op jit(solution)/shard_map/ppermute | solution.py:79
  50.4 5.6 %collective-permute-start.5 = (f32[32,488]{1,0:T(8,128)S(1)}, f32[32,488]{1,0:T(8,128)S(1)}, u32[]{:S(2)}, u32[]{:S(2)}) collective-permute-start(f32[32,488]{1,0:T(8,128)S(1)} %fusion.37), channel_id=1, source_target_pairs={{0,32},{16,48},{32,0},{48,16},{64,96},{80,112},{96,64},{112,80},{1... | collective-permute-start | bytes 187400 | tf_op jit(solution)/shard_map/ppermute | solution.py:79
  56.1 10.5 %collective-permute-start.6 = (f32[32,488]{1,0:T(8,128)S(1)}, f32[32,488]{1,0:T(8,128)S(1)}, u32[]{:S(2)}, u32[]{:S(2)}) collective-permute-start(f32[32,488]{1,0:T(8,128)S(1)} %add.92), channel_id=1, source_target_pairs={{0,64},{16,80},{32,96},{48,112},{64,0},{80,16},{96,32},{112,48},{1... | collective-permute-start | bytes 187400 | tf_op jit(solution)/shard_map/ppermute | solution.py:79
  66.6 4.4 %collective-permute-start.7 = (f32[32,488]{1,0:T(8,128)S(1)}, f32[32,488]{1,0:T(8,128)S(1)}, u32[]{:S(2)}, u32[]{:S(2)}) collective-permute-start(f32[32,488]{1,0:T(8,128)S(1)} %add.93), channel_id=1, source_target_pairs={{0,128},{16,144},{32,160},{48,176},{64,192},{80,208},{96,224},{112... | collective-permute-start | bytes 187400 | tf_op jit(solution)/shard_map/ppermute | solution.py:79
  71.0 3.5 %collective-permute-start.8 = (f32[32,488]{1,0:T(8,128)S(1)}, f32[32,488]{1,0:T(8,128)S(1)}, u32[]{:S(2)}, u32[]{:S(2)}) collective-permute-start(f32[32,488]{1,0:T(8,128)S(1)} %add.94), channel_id=1, source_target_pairs={{0,1},{1,0},{2,3},{3,2},{4,5},{5,4},{6,7},{7,6},{8,9},{9,8},{10,11... | collective-permute-start | bytes 187400 | tf_op jit(solution)/shard_map/ppermute | solution.py:79
  74.5 4.4 %collective-permute-start.9 = (f32[32,488]{1,0:T(8,128)S(1)}, f32[32,488]{1,0:T(8,128)S(1)}, u32[]{:S(2)}, u32[]{:S(2)}) collective-permute-start(f32[32,488]{1,0:T(8,128)S(1)} %add.95), channel_id=1, source_target_pairs={{0,2},{1,3},{2,0},{3,1},{4,6},{5,7},{6,4},{7,5},{8,10},{9,11},{10,... | collective-permute-start | bytes 187400 | tf_op jit(solution)/shard_map/ppermute | solution.py:79
  78.9 5.9 %collective-permute-start.10 = (f32[32,488]{1,0:T(8,128)S(1)}, f32[32,488]{1,0:T(8,128)S(1)}, u32[]{:S(2)}, u32[]{:S(2)}) collective-permute-start(f32[32,488]{1,0:T(8,128)S(1)} %add.96), channel_id=1, source_target_pairs={{0,4},{1,5},{2,6},{3,7},{4,0},{5,1},{6,2},{7,3},{8,12},{9,13},{10,... | collective-permute-start | bytes 187400 | tf_op jit(solution)/shard_map/ppermute | solution.py:79
  84.8 5.9 %collective-permute-start.11 = (f32[32,488]{1,0:T(8,128)S(1)}, f32[32,488]{1,0:T(8,128)S(1)}, u32[]{:S(2)}, u32[]{:S(2)}) collective-permute-start(f32[32,488]{1,0:T(8,128)S(1)} %add.97), channel_id=1, source_target_pairs={{0,8},{1,9},{2,10},{3,11},{4,12},{5,13},{6,14},{7,15},{8,0},{9,1},... | collective-permute-start | bytes 187400 | tf_op jit(solution)/shard_map/ppermute | solution.py:79
